TPU v7x, 128 devices: a whole 4x4x4 slice. The times are simulated.
128 devices in a mesh: req: 16 (over z, y), tensor: 8 (over x, core).
Axes of the slice: x: 4, y: 4, z: 4, core: 2. Of those that a mesh axis runs over, the one named last changes fastest.
Arguments:
- residual_input: bfloat16 [8192, 7168], P('req', 'tensor'), may hold values from -6 to 6
- input_norm_gain: float32 [7168], replicated, may hold values from 0.25 to 1.75
- query_weight: bfloat16 [7168, 4096], P(None, 'tensor'), may hold values from -0.09375 to 0.09375
- key_value_weight: bfloat16 [7168, 2048], P(None, 'tensor'), may hold values from -0.09375 to 0.09375
- output_weight: bfloat16 [4096, 7168], P('tensor'), may hold values from -0.375 to 0.375
- adapter_down_maps: bfloat16 [64, 48, 7168], P('req', None, 'tensor'), may hold values from -0.0625 to 0.0625
- adapter_query_up: bfloat16 [64, 16, 4096], P('req', None, 'tensor'), may hold values from -0.375 to 0.375
- adapter_key_value_up: bfloat16 [64, 2, 16, 1024], P('req', None, None, 'tensor'), may hold values from -0.375 to 0.375
- adapter_output_down: bfloat16 [64, 16, 4096], P('req', None, 'tensor'), may hold values from -0.375 to 0.375
- adapter_output_up: bfloat16 [64, 16, 7168], P('req', None, 'tensor'), may hold values from -0.375 to 0.375
- request_adapter: int32 [64], P('req'), may hold values from 0 to 63
- prompt_length: int32 [64], P('req'), may hold values from 32 to 128, as said below
- cache_length: int32 [32], replicated, may hold values from 16 to 2048, as said below
- first_page_device: int32 [32], replicated, may hold values from 0 to 15
- page_slot_table: int32 [16, 32], P('req'), may hold values from 0 to 31, as said below
- cache_page_pool: bfloat16 [512, 128, 2048], P('req', None, 'tensor'), may hold values from -200 to 200
Outputs:
- block_out: bfloat16 [8192, 7168], P('req', 'tensor')
Inputs may be any that keep to these rules, and one draw needn't show every extreme that they name: `prompt_length`: some request in every draw fills all 128 rows of its block. `cache_length`: some cache in every draw has 2048 positions. `page_slot_table`: each row is a permutation of the cached requests over the pool slots of one device.
All inputs are finite; a program needn't handle non-finite values.
Results may differ from a plain program's by a relative error of at most 0.035.
Values may be sent and summed in bfloat16 or wider, within the bound.
No kernel may reach another device: no remote copies, remote signals or barrier semaphores. Data moves between devices by JAX's collectives and lax.ppermute only.
A program may use at most 128 MiB of HBM per device.

v0:
```python
import jax
import jax.numpy as jnp
from jax import lax
from jax.sharding import PartitionSpec as P

HEAD_SIZE = 128


ROPE_BASE = 5000000.0
ADAPTER_SCALE = 2.0
EPSILON = 1e-05
NEG_FILL = -1e30


def rotate(vectors, positions):
    half_dim = vectors.shape[-1] // 2
    frequency = ROPE_BASE ** (-jnp.arange(half_dim, dtype=jnp.float32) / half_dim)
    angles = positions.astype(jnp.float32)[..., None] * frequency
    cosine = jnp.cos(angles)
    sine_part = jnp.sin(angles)
    front_half = vectors[..., :half_dim]
    back_half = vectors[..., half_dim:]
    return jnp.concatenate(
        [front_half * cosine - back_half * sine_part, back_half * cosine + front_half * sine_part],
        axis=-1,
    )


def partial_softmax(query_rows, key_rows, value_rows, allowed):
    score_scale = query_rows.shape[-1] ** (-0.5)
    scores = (
        jnp.einsum("bsvgd,bkvd->bvsgk", query_rows, key_rows, preferred_element_type=jnp.float32)
        * score_scale
    )
    spread_mask = allowed[:, None, :, None, :]
    scores = jnp.where(spread_mask, scores, NEG_FILL)
    peak_scores = jnp.max(scores, axis=-1)
    weights = jnp.where(spread_mask, jnp.exp(scores - peak_scores[..., None]), 0.0)
    totals = jnp.sum(weights, axis=-1)
    summed = jnp.einsum(
        "bvsgk,bkvd->bvsgd",
        weights.astype(jnp.bfloat16),
        value_rows,
        preferred_element_type=jnp.float32,
    )
    return (peak_scores, totals, summed)


def local(
    residual_input,
    input_norm_gain,
    query_weight,
    key_value_weight,
    output_weight,
    adapter_down_maps,
    adapter_query_up,
    adapter_key_value_up,
    adapter_output_down,
    adapter_output_up,
    request_adapter,
    prompt_length,
    cache_length,
    first_page_device,
    page_slot_table,
    cache_page_pool,
):
    holders = lax.axis_size("req")
    req_index = lax.axis_index("req")
    tensor_index = lax.axis_index("tensor")
    request_number = request_adapter.shape[0]
    cached_count = request_number // 2
    row_count = residual_input.shape[0]
    request_slot_rows = row_count // request_number
    piece_width = residual_input.shape[1]
    local_kv = key_value_weight.shape[1] // (2 * HEAD_SIZE)
    group_size = query_weight.shape[1] // (HEAD_SIZE * local_kv)
    page_rows = cache_page_pool.shape[1]
    gathered = lax.all_gather(residual_input, "tensor", axis=1, tiled=True)
    widened = gathered.astype(jnp.float32)
    inverse = lax.rsqrt(jnp.mean(widened * widened, axis=1, keepdims=True) + EPSILON)
    normed = (widened * inverse * input_norm_gain).astype(jnp.bfloat16)
    empty_sel = tuple(
        (
            jnp.zeros((request_number,) + adapter_lookup.shape[1:], jnp.bfloat16)
            for adapter_lookup in (
                adapter_down_maps,
                adapter_query_up,
                adapter_key_value_up,
                adapter_output_down,
                adapter_output_up,
            )
        )
    )
    pieces = (
        lax.all_gather(adapter_down_maps, "req", axis=0, tiled=True),
        lax.all_gather(adapter_query_up, "req", axis=0, tiled=True),
        lax.all_gather(adapter_key_value_up, "req", axis=0, tiled=True),
        lax.all_gather(adapter_output_down, "req", axis=0, tiled=True),
        lax.all_gather(adapter_output_up, "req", axis=0, tiled=True),
    )
    block_count = pieces[0].shape[0]
    adapter_ids = jnp.arange(block_count, dtype=jnp.int32)
    onehot = (request_adapter[:, None] == adapter_ids[None, :]).astype(jnp.bfloat16)
    down_picked, query_picked, key_value_picked, output_down_picked, oup_sel = tuple(
        (
            jnp.dot(onehot, segment.reshape(block_count, -1), preferred_element_type=jnp.float32)
            .reshape(held_sel.shape)
            .astype(jnp.bfloat16)
            for held_sel, segment in zip(empty_sel, pieces)
        )
    )
    adapter_rank_size = query_picked.shape[1]
    own_columns = lax.dynamic_slice_in_dim(
        normed, tensor_index * piece_width, piece_width, 1
    ).reshape(request_number, request_slot_rows, piece_width)
    partial_low = jnp.einsum(
        "rsd,rkd->rsk", own_columns, down_picked, preferred_element_type=jnp.float32
    )
    reduced_input = (
        lax.psum(partial_low.reshape(-1, 128).astype(jnp.bfloat16), "tensor")
        .astype(jnp.float32)
        .reshape(request_number, request_slot_rows, 3 * adapter_rank_size)
        .astype(jnp.bfloat16)
    )
    query_rows = jnp.dot(normed, query_weight, preferred_element_type=jnp.float32).reshape(
        request_number, request_slot_rows, -1
    )
    query_rows = query_rows + ADAPTER_SCALE * jnp.einsum(
        "ibm,imf->ibf",
        reduced_input[..., :adapter_rank_size],
        query_picked,
        preferred_element_type=jnp.float32,
    )
    keyval = jnp.dot(normed, key_value_weight, preferred_element_type=jnp.float32).reshape(
        request_number, request_slot_rows, local_kv, 2 * HEAD_SIZE
    )
    key_add = jnp.einsum(
        "ibm,imf->ibf",
        reduced_input[..., adapter_rank_size : 2 * adapter_rank_size],
        key_value_picked[:, 0],
        preferred_element_type=jnp.float32,
    ).reshape(request_number, request_slot_rows, local_kv, HEAD_SIZE)
    value_add = jnp.einsum(
        "ibm,imf->ibf",
        reduced_input[..., 2 * adapter_rank_size :],
        key_value_picked[:, 1],
        preferred_element_type=jnp.float32,
    ).reshape(request_number, request_slot_rows, local_kv, HEAD_SIZE)
    my_cache = lax.dynamic_slice_in_dim(cache_length, req_index * cached_count, cached_count, 0)
    offsets = jnp.stack([jnp.zeros_like(my_cache), my_cache], axis=1).reshape(request_number)
    slot_index = jnp.arange(request_slot_rows, dtype=jnp.int32)
    positions = offsets[:, None] + slot_index[None, :]
    query_rot = rotate(
        query_rows.reshape(request_number, request_slot_rows, local_kv, group_size, HEAD_SIZE),
        positions[:, :, None, None],
    ).astype(jnp.bfloat16)
    key_rot = rotate(keyval[..., :HEAD_SIZE] + key_add, positions[:, :, None]).astype(jnp.bfloat16)
    value_new = (keyval[..., HEAD_SIZE:] + value_add).astype(jnp.bfloat16)
    causal = slot_index[None, :, None] >= slot_index[None, None, :]
    own_mask = causal & (slot_index[None, None, :] < prompt_length[:, None, None])
    own_part = partial_softmax(query_rot, key_rot, value_new, own_mask)
    asked_queries = query_rot[1::2]
    slot_order = page_slot_table[0].reshape(holders, cached_count).T.reshape(-1)
    outgoing = cache_page_pool[slot_order].reshape(
        cached_count, holders, page_rows, cache_page_pool.shape[2]
    )
    arrived = lax.all_to_all(outgoing, "req", split_axis=1, concat_axis=1, tiled=True)
    my_base = lax.dynamic_slice_in_dim(first_page_device, req_index * cached_count, cached_count, 0)
    page_of = (jnp.arange(holders, dtype=jnp.int32)[None, :] - my_base[:, None]) % holders
    key_pos = (
        page_of[:, :, None] * page_rows + jnp.arange(page_rows, dtype=jnp.int32)[None, None, :]
    ).reshape(cached_count, holders * page_rows)
    entries = arrived.reshape(cached_count, holders * page_rows, local_kv, 2 * HEAD_SIZE)
    visible = jnp.broadcast_to(
        (key_pos < my_cache[:, None])[:, None, :],
        (cached_count, request_slot_rows, holders * page_rows),
    )
    cache_part = partial_softmax(
        asked_queries, entries[..., :HEAD_SIZE], entries[..., HEAD_SIZE:], visible
    )
    filler = jnp.full_like(cache_part[0], NEG_FILL)
    spread_peak = jnp.stack([filler, cache_part[0]], axis=1).reshape(own_part[0].shape)
    spread_total = jnp.stack([jnp.zeros_like(cache_part[1]), cache_part[1]], axis=1).reshape(
        own_part[1].shape
    )
    spread_sum = jnp.stack([jnp.zeros_like(cache_part[2]), cache_part[2]], axis=1).reshape(
        own_part[2].shape
    )
    highest_all = jnp.maximum(own_part[0], spread_peak)
    own_weight = jnp.exp(own_part[0] - highest_all)
    cache_weight = jnp.exp(spread_peak - highest_all)
    denominator = own_part[1] * own_weight + spread_total * cache_weight
    numerator = own_part[2] * own_weight[..., None] + spread_sum * cache_weight[..., None]
    live_rows = slot_index[None, :] < prompt_length[:, None]
    attended = jnp.where(
        live_rows[:, None, :, None, None], numerator / denominator[..., None], 0.0
    ).astype(jnp.bfloat16)
    attended = jnp.transpose(attended, (0, 2, 1, 3, 4)).reshape(row_count, -1)
    head_terms = jnp.dot(attended, output_weight, preferred_element_type=jnp.float32)
    low_part = jnp.einsum(
        "rsc,rkc->rsk",
        attended.reshape(request_number, request_slot_rows, -1),
        output_down_picked,
        preferred_element_type=jnp.float32,
    )
    reduced_output = (
        lax.psum(low_part.reshape(-1, 128).astype(jnp.bfloat16), "tensor")
        .astype(jnp.float32)
        .reshape(request_number, request_slot_rows, adapter_rank_size)
        .astype(jnp.bfloat16)
    )
    head_total = lax.psum_scatter(
        head_terms.astype(jnp.bfloat16), "tensor", scatter_dimension=1, tiled=True
    ).astype(jnp.float32)
    adapter_output = jnp.einsum(
        "ibm,imf->ibf", reduced_output, oup_sel, preferred_element_type=jnp.float32
    ).reshape(row_count, -1)
    return (head_total + ADAPTER_SCALE * adapter_output).astype(jnp.bfloat16)


def solution(mesh):
    placed = (
        P("req", "tensor"),
        P(),
        P(None, "tensor"),
        P(None, "tensor"),
        P("tensor", None),
        P("req", None, "tensor"),
        P("req", None, "tensor"),
        P("req", None, None, "tensor"),
        P("req", None, "tensor"),
        P("req", None, "tensor"),
        P("req"),
        P("req"),
        P(),
        P(),
        P("req", None),
        P("req", None, "tensor"),
    )
    return jax.shard_map(
        local, mesh=mesh, in_specs=placed, out_specs=P("req", "tensor"), check_vma=False
    )
```

profile of v0, /device:TPU:1, one launch (start us, length us, event | category | flops | bytes accessed | tf_op | source)
XLA Modules:
  0.0 329.6 jit_solution(5925808227693249332)
XLA Ops:
  6.5 0.7 all-gather.10.cloned.1.call-update
  7.3 0.7 all-gather.8.cloned.1.call-update
  8.1 0.7 all-gather.6.cloned.1.call-update
  8.8 0.5 all-gather.12.cloned.1.call-update
  9.3 0.5 broadcast.279
  9.9 1.3 reduce.11
  11.3 0.1 copy.80
  11.3 0.1 reshape.501
  11.5 2.0 gather_fusion
  13.5 3.1 copy.81
  16.6 8.6 %all-to-all-start = ((bf16[2,16,128,256]{3,2,0,1:T(8,128)(2,1)}), bf16[2,16,128,256]{3,2,0,1:T(8,128)(2,1)S(1)}, u32[]{:S(2)}, u32[]{:S(2)}) async-start(bf16[2,16,128,256]{3,2,0,1:T(8,128)(2,1)} %copy.81), calls=%async_computation | async-start | bytes 4194304 | tf_op jit(solution)/shard_map/all_to_all | solution.py:167
  25.2 0.5 all-gather.14.cloned.1.call-update
  25.9 0.1 copy.110
  26.1 0.1 add.134
  26.3 43.4 %all_gather.21 = bf16[64,2,16,128]{3,2,1,0:T(8,128)(2,1)S(1)} all-gather(bf16[4,2,16,128]{3,2,1,0:T(8,128)(2,1)S(1)} %copy-done.7), channel_id=1, replica_groups=mesh['req'=16,'tensor'=8] {'req'}, dimensions={0}, use_global_device_ids=true | all-gather | bytes 557056 | tf_op jit(solution)/shard_map/all_gather | solution.py:97
  70.0 0.2 copy.182
  70.3 0.1 copy.120
  70.4 0.3 convolution_convert_fusion.4
  70.7 0.6 slice_bitcast_fusion.4
  71.3 0.1 broadcast_and_fusion
  71.5 1.8 multiply_cosine_fusion
  73.3 2.4 convolution_convert_fusion.2
  75.8 1.5 copy.82
  77.3 54.5 %all-gather.8.cloned.1.call-done = bf16[64,48,896]{2,1,0:T(8,128)(2,1)} async-done(((bf16[4,48,896]{2,1,0:T(8,128)(2,1)}), bf16[64,48,896]{2,1,0:T(8,128)(2,1)}) %all-gather.8.cloned.1.call-update) | async-done | bytes 5505040 | tf_op jit(solution)/shard_map/all_gather | solution.py:95
  131.8 3.8 %fusion.25 = bf16[4,48,896]{2,0,1:T(4,128)(2,1)S(1)} fusion(s32[4]{0:T(128)S(1)} %copy-done.11, bf16[8,8,48,896]{3,2,1,0:T(8,128)(2,1)} %bitcast.206), kind=kOutput, calls=%fused_computation.33 | convolution fusion | flops 22192384 | bytes 5849104 | tf_op jit(solution)/shard_map/dot_general | solution.py:106
  135.6 43.3 %all-gather.6.cloned.1.call-done = bf16[512,7168]{1,0:T(8,128)(2,1)} async-done(((bf16[512,896]{1,0:T(8,128)(2,1)}), bf16[512,7168]{1,0:T(8,128)(2,1)}) %all-gather.6.cloned.1.call-update) | async-done | bytes 7340048 | tf_op jit(solution)/shard_map/all_gather | solution.py:78
  178.9 4.7 %fusion = f32[512]{0:T(512)S(1)} fusion(bf16[512,7168]{1,0:T(8,128)(2,1)} %all-gather.6.cloned.1.call-done), kind=kLoop, calls=%fused_computation.3 | loop fusion | flops 11009536 | bytes 7342080 | tf_op jit(solution)/shard_map/reduce_sum | solution.py:80
  183.6 0.4 copy-done.3
  184.0 5.8 %fusion.2 = bf16[512,7168]{1,0:T(8,128)(2,1)} fusion(bf16[512,7168]{1,0:T(8,128)(2,1)S(1)} %copy-done.3, f32[7168]{0:T(1024)S(1)} %copy-done.8, f32[512]{0:T(512)S(1)} %add_rsqrt_fusion), kind=kLoop, calls=%fused_computation.5 | loop fusion | flops 14680064 | bytes 14710784 | tf_op jit(solution)/shard_map/convert_element_type | solution.py:81
  189.8 1.3 constant_dynamic-slice_fusion
  191.1 0.5 convolution_convert_fusion.3
  191.5 21.7 %psum.14 = bf16[4,128,48]{1,2,0:T(8,128)(2,1)S(1)} all-reduce(bf16[4,128,48]{1,2,0:T(8,128)(2,1)S(1)} %convolution_convert_fusion.3), channel_id=1, replica_groups=mesh['req'=16,'tensor'=8] {'tensor'}, use_global_device_ids=true, to_apply=%region_1.0 | all-reduce | flops 24576 | bytes 98304 | tf_op jit(solution)/shard_map/psum | solution.py:120
  213.2 8.6 %fusion.102 = f32[512,512]{1,0:T(8,128)S(1)} fusion(bf16[512,7168]{1,0:T(8,128)(2,1)} %fusion.2, bf16[7168,512]{1,0:T(8,128)(2,1)} %param.18), kind=kOutput, calls=%fused_computation.141 | convolution fusion | flops 3758096384 | bytes 15728640 | tf_op jit(solution)/shard_map/dot_general | solution.py:125
  221.8 0.3 fusion.20
  222.1 0.4 reshape.494
  222.5 0.6 fusion.100
  223.1 6.3 %fusion.103 = f32[512,256]{1,0:T(8,128)S(1)} fusion(bf16[512,7168]{1,0:T(8,128)(2,1)} %fusion.2, bf16[7168,256]{1,0:T(8,128)(2,1)} %param.19), kind=kOutput, calls=%fused_computation.142 | convolution fusion | flops 1879048192 | bytes 11534336 | tf_op jit(solution)/shard_map/dot_general | solution.py:134
  229.5 0.3 subtract_convert_fusion
  229.8 0.3 pad_maximum_fusion
  230.1 1.5 fusion.3
  231.6 3.2 copy-done.2
  234.9 2.8 fusion.4
  237.6 0.7 slice.61
  238.4 1.1 copy.109
  239.4 0.7 stack.31
  240.1 4.6 %fusion.22 = f32[2,1,1,128,4,128]{3,5,4,1,0,2:T(8,128)S(1)} fusion(f32[2,128,4,2048]{3,1,2,0:T(8,128)} %copy-done.2, f32[2,128,4]{1,2,0:T(4,128)S(1)} %get-tuple-element.18, pred[2,2048]{1,0:T(4,128)(4,1)S(1)} %fusion.71, bf16[2,2048,1,256]{3,1,0,2:T(8,128)(2,1)S(1)} %bitcast.191), kind=kOutput, calls=%fused_computation.32 | convolution fusion | flops 547356672 | bytes 9973760 | tf_op jit(solution)/shard_map/bvsgk,bkvd->bvsgd/dot_general | solution.py:40
  244.8 0.2 fusion.28
  245.1 0.6 fusion.70
  245.7 0.5 fusion.101
  246.2 0.2 fusion.40
  246.4 1.1 bitcast_multiply_fusion
  247.5 1.9 fusion.21
  249.4 0.3 copy.86
  249.7 9.4 %convolution_convert_fusion = bf16[512,7168]{1,0:T(8,128)(2,1)} fusion(bf16[512,7168]{1,0:T(8,128)(2,1)} %param.20, bf16[64,8,4,128]{3,2,1,0:T(4,128)(2,1)S(1)} %bitcast.200), kind=kOutput, calls=%fused_computation.6 | convolution fusion | flops 3761766400 | bytes 15204352 | tf_op jit(solution)/shard_map/dot_general | solution.py:199
  259.2 10.5 %copy.105 = bf16[512,7168]{0,1:T(8,128)(2,1)} copy(bf16[512,7168]{1,0:T(8,128)(2,1)} %convolution_convert_fusion) | data formatting | bytes 14680064
  269.7 0.6 copy-done.12
  270.3 2.5 convolution_convert_fusion.1
  272.7 2.0 fusion.31
  274.7 0.2 convolution_convert_fusion.5
  274.9 24.3 %psum.15 = bf16[4,128,16]{1,2,0:T(8,128)(2,1)S(1)} all-reduce(bf16[4,128,16]{1,2,0:T(8,128)(2,1)S(1)} %convolution_convert_fusion.5), channel_id=1, replica_groups=mesh['req'=16,'tensor'=8] {'tensor'}, use_global_device_ids=true, to_apply=%region_7.8 | all-reduce | flops 8192 | bytes 32768 | tf_op jit(solution)/shard_map/psum | solution.py:207
  299.2 1.8 convolution_multiply_fusion
  300.9 17.8 %reduce-scatter.4.cloned.1.call-done = bf16[896,512]{1,0:T(8,128)(2,1)} async-done(((bf16[7168,512]{1,0:T(8,128)(2,1)}), bf16[896,512]{1,0:T(8,128)(2,1)}) %reduce-scatter.4.cloned.1.call-update) | async-done | bytes 917520
  318.7 1.5 copy.106
  320.2 2.6 fusion.15
  (61 shorter events, 1.3 us)
Async XLA Ops:
  6.5 4.9 %copy-start = (bf16[32,128,256]{2,1,0:T(8,128)(2,1)S(1)}, bf16[32,128,256]{2,1,0:T(8,128)(2,1)}, u32[]{:S(2)}) copy-start(bf16[32,128,256]{2,1,0:T(8,128)(2,1)} %param.31) | copy-start | bytes 6291460
  6.5 19.3 %copy-start.16 = (s32[32]{0:T(128)S(1)}, s32[32]{0:T(128)}, u32[]{:S(2)}) copy-start(s32[32]{0:T(128)} %param.28) | copy-start | bytes 388
  6.5 19.7 %copy-start.7 = (bf16[4,2,16,128]{3,2,1,0:T(8,128)(2,1)S(1)}, bf16[4,2,16,128]{3,2,1,0:T(8,128)(2,1)}, u32[]{:S(2)}) copy-start(bf16[4,2,16,128]{3,2,1,0:T(8,128)(2,1)} %param.23) | copy-start | bytes 98308
  6.5 66.8 %all-gather.10.cloned.1.call-start = ((), (), s32[]{:S(2)}) async-start(), calls=%async_computation.4 | async-start | bytes 1114112 | tf_op jit(solution)/shard_map/all_gather | solution.py:96
  7.3 62.4 %copy-start.14 = (s32[4]{0:T(128)S(1)}, s32[4]{0:T(128)}, u32[]{:S(2)}) copy-start(s32[4]{0:T(128)} %param.27) | copy-start | bytes 52
  7.3 62.5 %copy-start.15 = (s32[32]{0:T(128)S(1)}, s32[32]{0:T(128)}, u32[]{:S(2)}) copy-start(s32[32]{0:T(128)} %param.29) | copy-start | bytes 388
  7.3 124.5 %all-gather.8.cloned.1.call-start = ((), (), s32[]{:S(2)}) async-start(), calls=%async_computation.3 | async-start | bytes 5849088 | tf_op jit(solution)/shard_map/all_gather | solution.py:95
  8.0 170.8 %all-gather.6.cloned.1.call-start = ((), (), s32[]{:S(2)}) async-start(), calls=%async_computation.2 | async-start | bytes 8257536 | tf_op jit(solution)/shard_map/all_gather | solution.py:78
  8.8 260.9 %all-gather.12.cloned.1.call-start = ((), (), s32[]{:S(2)}) async-start(), calls=%async_computation.5 | async-start | bytes 1114112 | tf_op jit(solution)/shard_map/all_gather | solution.py:98
  11.5 59.0 %copy-start.11 = (s32[4]{0:T(128)S(1)}, s32[4]{0:T(128)}, u32[]{:S(2)}) copy-start(s32[4]{0:T(128)} %param.26) | copy-start | bytes 52
  16.6 59.2 %all-to-all-start = ((bf16[2,16,128,256]{3,2,0,1:T(8,128)(2,1)}), bf16[2,16,128,256]{3,2,0,1:T(8,128)(2,1)S(1)}, u32[]{:S(2)}, u32[]{:S(2)}) async-start(bf16[2,16,128,256]{3,2,0,1:T(8,128)(2,1)} %copy.81), calls=%async_computation | async-start | bytes 4194304 | tf_op jit(solution)/shard_map/all_to_all | solution.py:167
  25.2 247.6 %all-gather.14.cloned.1.call-start = ((), (), s32[]{:S(2)}) async-start(), calls=%async_computation.6 | async-start | bytes 1949696 | tf_op jit(solution)/shard_map/all_gather | solution.py:99
  25.8 292.9 %reduce-scatter.4.cloned.1.call-start = ((), (), s32[]{:S(2)}) async-start(), calls=%async_computation.7 | async-start | bytes 8257536
  69.8 65.8 %copy-start.13 = (pred[4,128]{1,0:T(4,128)(4,1)}, pred[4,128]{1,0:T(4,128)(4,1)S(1)}, u32[]{:S(2)}) copy-start(pred[4,128]{1,0:T(4,128)(4,1)S(1)} %iota_compare_fusion.2) | copy-start | bytes 1540
  70.0 65.6 %copy-start.9 = (f32[64]{0:T(128)}, f32[64]{0:T(128)S(1)}, u32[]{:S(2)}) copy-start(f32[64]{0:T(128)S(1)} %multiply_power_fusion) | copy-start | bytes 772
  131.8 51.8 %copy-start.8 = (f32[7168]{0:T(1024)S(1)}, f32[7168]{0:T(1024)}, u32[]{:S(2)}) copy-start(f32[7168]{0:T(1024)} %param.17) | copy-start | bytes 86020
  178.9 5.2 %copy-start.3 = (bf16[512,7168]{1,0:T(8,128)(2,1)S(1)}, bf16[512,7168]{1,0:T(8,128)(2,1)}, u32[]{:S(2)}) copy-start(bf16[512,7168]{1,0:T(8,128)(2,1)} %all-gather.6.cloned.1.call-done) | copy-start | bytes 22020100
  223.1 6.4 %copy-start.5 = (f32[4,128,64]{2,1,0:T(8,128)S(1)}, f32[4,128,64]{2,1,0:T(8,128)}, u32[]{:S(2)}) copy-start(f32[4,128,64]{2,1,0:T(8,128)} %get-tuple-element.17) | copy-start | bytes 393220
  223.1 7.0 %copy-start.4 = (bf16[2,16,128,256]{3,2,1,0:T(8,128)(2,1)S(1)}, bf16[2,16,128,256]{3,2,1,0:T(8,128)(2,1)}, u32[]{:S(2)}) copy-start(bf16[2,16,128,256]{3,2,1,0:T(8,128)(2,1)} %copy.82) | copy-start | bytes 6291460
  229.5 8.2 %copy-start.6 = (f32[512,256]{1,0:T(8,128)}, f32[512,256]{1,0:T(8,128)S(1)}, u32[]{:S(2)}) copy-start(f32[512,256]{1,0:T(8,128)S(1)} %fusion.103) | copy-start | bytes 1572868
  231.6 3.2 copy-start.2
  240.1 5.0 %copy-start.10 = (f32[64]{0:T(128)S(1)}, f32[64]{0:T(128)}, u32[]{:S(2)}) copy-start(f32[64]{0:T(128)} %copy-done.9) | copy-start | bytes 772
  269.6 0.7 copy-start.12
  269.6 53.2 %copy-start.1 = (bf16[32,128,256]{2,1,0:T(8,128)(2,1)S(1)}, bf16[32,128,256]{2,1,0:T(8,128)(2,1)}, u32[]{:S(2)}) copy-start(bf16[32,128,256]{2,1,0:T(8,128)(2,1)} %param.31) | copy-start | bytes 6291460
Sparse Core Ops, SparseCore 0:
  9.5 61.4 all-gather.9
  73.1 58.6 all-gather.7
  133.5 45.3 all-gather.5
  180.8 40.6 all-gather.11
  223.5 44.1 all-gather.13
  270.0 48.6 reduce-scatter.3
where the time goes:
time: 330 us
  waiting for transfers between devices  119 us (36%)
  blocking collectives  89.4 us (27%)
  matrix products  46.7 us (14%)
  local copies, waits for them, and re-layouts  30.3 us (9%)
  other arithmetic  22 us (7%)
  between operations  13.8 us (4%)
  starting transfers between devices  8.78 us (3%)
    all_gather x1, waiting for transfers between devices, local(): lax.all_gather(adapter_down_maps, 'req', axis=0, tiled=True)  54.5 us
    all_gather x1, blocking collectives, local(): lax.all_gather(adapter_key_value_up, 'req', axis=0, tiled=True)  43.4 us
    all_gather x1, waiting for transfers between devices, local(): gathered = lax.all_gather(residual_input, 'tensor', axis=1, tiled=True)  43.3 us
    psum x1, blocking collectives, local(): lax.psum(low_part.reshape(-1, 128).astype(jnp.bfloat16), 'tensor')  24.3 us
    psum x1, blocking collectives, local(): lax.psum(partial_low.reshape(-1, 128).astype(jnp.bfloat16), 'tensor')  21.7 us
    unnamed x7, waiting for transfers between devices  20.9 us
    unnamed x42, local copies, waits for them, and re-layouts  18.3 us
    dot_general x5, matrix products, local(): jnp.dot(onehot, segment.reshape(block_count, -1), preferred_element_type=...  10.9 us
  transfers between devices with their start and end apart: 7, of which 3 were waited for; matrix products, arithmetic and copies ran while one was open for 27% of the time, Pallas kernels for 0%

commit v1 on v0

--- a/solution.py
+++ b/solution.py
@@ -44,6 +44,11 @@
         preferred_element_type=jnp.float32,
     )
     return (peak_scores, totals, summed)
+
+
+def gather_by_exchange(piece, axis_name, count):
+    spread = jnp.broadcast_to(piece[None], (count,) + piece.shape)
+    return lax.all_to_all(spread, axis_name, split_axis=0, concat_axis=0, tiled=True)
 
 
 def local(
@@ -75,63 +80,69 @@
     local_kv = key_value_weight.shape[1] // (2 * HEAD_SIZE)
     group_size = query_weight.shape[1] // (HEAD_SIZE * local_kv)
     page_rows = cache_page_pool.shape[1]
-    gathered = lax.all_gather(residual_input, "tensor", axis=1, tiled=True)
+    tensor_count = lax.axis_size("tensor")
+    gathered = gather_by_exchange(residual_input, "tensor", tensor_count)
     widened = gathered.astype(jnp.float32)
-    inverse = lax.rsqrt(jnp.mean(widened * widened, axis=1, keepdims=True) + EPSILON)
-    normed = (widened * inverse * input_norm_gain).astype(jnp.bfloat16)
-    empty_sel = tuple(
-        (
-            jnp.zeros((request_number,) + adapter_lookup.shape[1:], jnp.bfloat16)
-            for adapter_lookup in (
-                adapter_down_maps,
-                adapter_query_up,
-                adapter_key_value_up,
-                adapter_output_down,
-                adapter_output_up,
-            )
+    inverse = lax.rsqrt(
+        jnp.sum(widened * widened, axis=(0, 2), keepdims=True) / (tensor_count * piece_width)
+        + EPSILON
+    )
+    gain_parts = input_norm_gain.reshape(tensor_count, 1, piece_width)
+    normed_parts = (widened * inverse * gain_parts).astype(jnp.bfloat16)
+    adapter_parts = (
+        adapter_down_maps,
+        adapter_query_up,
+        adapter_key_value_up,
+        adapter_output_down,
+        adapter_output_up,
+    )
+    local_adapters = adapter_down_maps.shape[0]
+    flat_parts = [part.reshape(local_adapters, -1) for part in adapter_parts]
+    joined = jnp.concatenate(flat_parts, axis=1)
+    every_adapter = gather_by_exchange(joined, "req", holders).reshape(
+        holders * local_adapters, joined.shape[1]
+    )
+    picked = jnp.take(every_adapter, request_adapter, axis=0, mode="clip")
+    picked_parts = []
+    start = 0
+    for part, flat in zip(adapter_parts, flat_parts):
+        width = flat.shape[1]
+        picked_parts.append(
+            picked[:, start : start + width].reshape((request_number,) + part.shape[1:])
         )
-    )
-    pieces = (
-        lax.all_gather(adapter_down_maps, "req", axis=0, tiled=True),
-        lax.all_gather(adapter_query_up, "req", axis=0, tiled=True),
-        lax.all_gather(adapter_key_value_up, "req", axis=0, tiled=True),
-        lax.all_gather(adapter_output_down, "req", axis=0, tiled=True),
-        lax.all_gather(adapter_output_up, "req", axis=0, tiled=True),
-    )
-    block_count = pieces[0].shape[0]
-    adapter_ids = jnp.arange(block_count, dtype=jnp.int32)
-    onehot = (request_adapter[:, None] == adapter_ids[None, :]).astype(jnp.bfloat16)
-    down_picked, query_picked, key_value_picked, output_down_picked, oup_sel = tuple(
-        (
-            jnp.dot(onehot, segment.reshape(block_count, -1), preferred_element_type=jnp.float32)
-            .reshape(held_sel.shape)
-            .astype(jnp.bfloat16)
-            for held_sel, segment in zip(empty_sel, pieces)
-        )
-    )
+        start += width
+    down_picked, query_picked, key_value_picked, output_down_picked, oup_sel = picked_parts
     adapter_rank_size = query_picked.shape[1]
-    own_columns = lax.dynamic_slice_in_dim(
-        normed, tensor_index * piece_width, piece_width, 1
-    ).reshape(request_number, request_slot_rows, piece_width)
+    own_columns = lax.dynamic_index_in_dim(normed_parts, tensor_index, 0, keepdims=False).reshape(
+        request_number, request_slot_rows, piece_width
+    )
     partial_low = jnp.einsum(
         "rsd,rkd->rsk", own_columns, down_picked, preferred_element_type=jnp.float32
     )
     reduced_input = (
-        lax.psum(partial_low.reshape(-1, 128).astype(jnp.bfloat16), "tensor")
+        gather_by_exchange(partial_low.astype(jnp.bfloat16), "tensor", tensor_count)
         .astype(jnp.float32)
-        .reshape(request_number, request_slot_rows, 3 * adapter_rank_size)
+        .sum(axis=0)
         .astype(jnp.bfloat16)
     )
-    query_rows = jnp.dot(normed, query_weight, preferred_element_type=jnp.float32).reshape(
-        request_number, request_slot_rows, -1
-    )
+    query_rows = jnp.einsum(
+        "tsf,tfc->sc",
+        normed_parts,
+        query_weight.reshape(tensor_count, piece_width, -1),
+        preferred_element_type=jnp.float32,
+    ).reshape(request_number, request_slot_rows, -1)
     query_rows = query_rows + ADAPTER_SCALE * jnp.einsum(
         "ibm,imf->ibf",
         reduced_input[..., :adapter_rank_size],
         query_picked,
         preferred_element_type=jnp.float32,
     )
-    keyval = jnp.dot(normed, key_value_weight, preferred_element_type=jnp.float32).reshape(
+    keyval = jnp.einsum(
+        "tsf,tfc->sc",
+        normed_parts,
+        key_value_weight.reshape(tensor_count, piece_width, -1),
+        preferred_element_type=jnp.float32,
+    ).reshape(
         request_number, request_slot_rows, local_kv, 2 * HEAD_SIZE
     )
     key_add = jnp.einsum(
@@ -196,7 +207,12 @@
         live_rows[:, None, :, None, None], numerator / denominator[..., None], 0.0
     ).astype(jnp.bfloat16)
     attended = jnp.transpose(attended, (0, 2, 1, 3, 4)).reshape(row_count, -1)
-    head_terms = jnp.dot(attended, output_weight, preferred_element_type=jnp.float32)
+    head_terms = jnp.einsum(
+        "sc,ctf->tsf",
+        attended,
+        output_weight.reshape(output_weight.shape[0], tensor_count, piece_width),
+        preferred_element_type=jnp.float32,
+    )
     low_part = jnp.einsum(
         "rsc,rkc->rsk",
         attended.reshape(request_number, request_slot_rows, -1),
@@ -204,14 +220,18 @@
         preferred_element_type=jnp.float32,
     )
     reduced_output = (
-        lax.psum(low_part.reshape(-1, 128).astype(jnp.bfloat16), "tensor")
+        gather_by_exchange(low_part.astype(jnp.bfloat16), "tensor", tensor_count)
         .astype(jnp.float32)
-        .reshape(request_number, request_slot_rows, adapter_rank_size)
+        .sum(axis=0)
         .astype(jnp.bfloat16)
     )
-    head_total = lax.psum_scatter(
-        head_terms.astype(jnp.bfloat16), "tensor", scatter_dimension=1, tiled=True
-    ).astype(jnp.float32)
+    head_total = (
+        lax.all_to_all(
+            head_terms.astype(jnp.bfloat16), "tensor", split_axis=0, concat_axis=0, tiled=True
+        )
+        .astype(jnp.float32)
+        .sum(axis=0)
+    )
     adapter_output = jnp.einsum(
         "ibm,imf->ibf", reduced_output, oup_sel, preferred_element_type=jnp.float32
     ).reshape(row_count, -1)

time: 330 us -> 464 us (1.41)
  waiting for transfers between devices: 119 us -> 310 us
  blocking collectives: 89.4 us -> 0 us
  starting transfers between devices: 8.78 us -> 35.7 us
  local copies, waits for them, and re-layouts: 30.3 us -> 48.4 us
  matrix products: 46.7 us -> 29.5 us
  other arithmetic: 22 us -> 35.5 us
  between operations: 13.8 us -> 0.79 us
    all_to_all x0 -> x5, waiting for transfers between devices: none -> 279 us  [the longest x4 199 us: gather_by_exchange(): lax.all_to_all(spread, axis_name, split_axis=0, concat_axis=0, tiled=True)]
    all_gather x5 -> x0, waiting for transfers between devices: 97.8 us -> none  [the longest x1 54.5 us: local(): lax.all_gather(adapter_down_maps, 'req', axis=0, tiled=True)]
    psum x2 -> x0, blocking collectives: 46 us -> none  [the longest x1 24.3 us: local(): lax.psum(low_part.reshape(-1, 128).astype(jnp.bfloat16), 'tensor')]
    all_gather x1 -> x0, blocking collectives: 43.4 us -> none  [local(): lax.all_gather(adapter_key_value_up, 'req', axis=0, tiled=True)]
    all_to_all x1, waiting for transfers between devices: 0.01 us -> 30.8 us  [local(): lax.all_to_all(outgoing, 'req', split_axis=1, concat_axis=1, tiled=True)]
    all_to_all x0 -> x5, starting transfers between devices: none -> 27.1 us  [the longest x4 22.3 us: gather_by_exchange(): lax.all_to_all(spread, axis_name, split_axis=0, concat_axis=0, tiled=True)]
    unnamed x7 -> x0, waiting for transfers between devices: 20.9 us -> none
    reshape x0 -> x2, local copies, waits for them, and re-layouts: none -> 16.9 us  [the longest x1 10.6 us: local(): gather_by_exchange(joined, 'req', holders)]
  transfers between devices with their start and end apart: 7 -> 6, of which waited for: 3 -> 5; matrix products, arithmetic and copies ran while one was open for 27% -> 11% of each run, Pallas kernels for 0% -> 0%
where the time goes in v1:
time: 464 us; the launch traced here: 460 us
  waiting for transfers between devices  310 us (67%)
  local copies, waits for them, and re-layouts  48.4 us (10%)
  starting transfers between devices  35.7 us (8%)
  other arithmetic  35.5 us (8%)
  matrix products  29.5 us (6%)
    all_to_all x4, waiting for transfers between devices, gather_by_exchange(): lax.all_to_all(spread, axis_name, split_axis=0, concat_axis=0, tiled=True)  199 us
    all_to_all x1, waiting for transfers between devices, local(): lax.all_to_all(head_terms.astype(jnp.bfloat16), 'tensor', split_axis=0, c...  80.7 us
    all_to_all x1, waiting for transfers between devices, local(): lax.all_to_all(outgoing, 'req', split_axis=1, concat_axis=1, tiled=True)  30.8 us
    all_to_all x4, starting transfers between devices, gather_by_exchange(): lax.all_to_all(spread, axis_name, split_axis=0, concat_axis=0, tiled=True)  22.3 us
    reduce_sum x1, other arithmetic, local(): jnp.sum(widened * widened, axis=(0, 2), keepdims=True)  12.2 us
    reshape x1, local copies, waits for them, and re-layouts, local(): gather_by_exchange(joined, 'req', holders)  10.6 us
    broadcast_in_dim x4, local copies, waits for them, and re-layouts, gather_by_exchange(): spread = jnp.broadcast_to(piece[None], (count,) + piece.shape)  10.6 us
    convert_element_type x1, other arithmetic, local(): normed_parts = (widened * inverse * gain_parts).astype(jnp.bfloat16)  9.32 us
  transfers between devices with their start and end apart: 6, of which 5 were waited for; matrix products, arithmetic and copies ran while one was open for 11% of the time, Pallas kernels for 0%

profile of v1, /device:TPU:1, one launch (start us, length us, event | category | flops | bytes accessed | tf_op | source)
XLA Modules:
  0.0 460.1 jit_solution(15366551782491586483)
XLA Ops:
  0.0 0.5 broadcast.285
  0.5 1.5 reduce.13
  2.1 0.1 reshape_squeeze.3
  2.1 0.1 copy.100
  2.2 0.1 reshape.523
  2.3 2.0 gather_fusion.1
  4.3 3.1 copy.101
  7.5 8.6 %all-to-all-start.3 = ((bf16[2,16,128,256]{3,2,0,1:T(8,128)(2,1)}), bf16[2,16,128,256]{3,2,0,1:T(8,128)(2,1)S(1)}, u32[]{:S(2)}, u32[]{:S(2)}) async-start(bf16[2,16,128,256]{3,2,0,1:T(8,128)(2,1)} %copy.101), calls=%async_computation.3 | async-start | bytes 4194304 | tf_op jit(solution)/shard_map/all_to_all | solution.py:178
  16.1 0.1 copy.131
  16.2 30.8 %all-to-all-done.3 = bf16[2,16,128,256]{3,2,0,1:T(8,128)(2,1)S(1)} async-done(((bf16[2,16,128,256]{3,2,0,1:T(8,128)(2,1)}), bf16[2,16,128,256]{3,2,0,1:T(8,128)(2,1)S(1)}, u32[]{:S(2)}, u32[]{:S(2)}) %all-to-all-start.3) | async-done | bytes 2097184 | tf_op jit(solution)/shard_map/all_to_all | solution.py:178
  47.0 5.1 %broadcast_in_dim.56 = bf16[8,512,896]{2,1,0:T(8,128)(2,1)} broadcast(bf16[512,896]{1,0:T(8,128)(2,1)} %param.16), dimensions={1,2} | broadcast | bytes 8257536 | tf_op jit(solution)/shard_map/broadcast_in_dim | solution.py:50
  52.1 6.7 %all-to-all-start = ((bf16[8,512,896]{2,1,0:T(8,128)(2,1)}), bf16[8,512,896]{2,1,0:T(8,128)(2,1)}, u32[]{:S(2)}, u32[]{:S(2)}) async-start(bf16[8,512,896]{2,1,0:T(8,128)(2,1)} %broadcast_in_dim.56), calls=%async_computation | async-start | bytes 14680064 | tf_op jit(solution)/shard_map/all_to_all | solution.py:51
  58.8 0.1 constant_dynamic-update-slice_fusion.3
  59.3 82.0 %all-to-all-done = bf16[8,512,896]{2,1,0:T(8,128)(2,1)} async-done(((bf16[8,512,896]{2,1,0:T(8,128)(2,1)}), bf16[8,512,896]{2,1,0:T(8,128)(2,1)}, u32[]{:S(2)}, u32[]{:S(2)}) %all-to-all-start) | async-done | bytes 7340064 | tf_op jit(solution)/shard_map/all_to_all | solution.py:51
  141.3 4.1 broadcast_in_dim.57
  145.4 5.5 %all-to-all-start.1 = ((bf16[16,4,77824]{2,1,0:T(4,128)(2,1)}), bf16[16,4,77824]{2,1,0:T(4,128)(2,1)}, u32[]{:S(2)}, u32[]{:S(2)}) async-start(bf16[16,4,77824]{2,1,0:T(4,128)(2,1)} %broadcast_in_dim.57), calls=%async_computation.1 | async-start | bytes 19922944 | tf_op jit(solution)/shard_map/all_to_all | solution.py:51
  150.9 0.1 dynamic_slice.12
  151.1 0.1 copy.127
  151.3 0.1 add.129
  151.4 6.3 %copy.93 = bf16[8,896,256]{1,2,0:T(8,128)(2,1)} copy(bf16[8,896,256]{2,1,0:T(8,128)(2,1)} %bitcast.181) | data formatting | bytes 7340032 | tf_op jit(solution)/shard_map/reshape | solution.py:143
  158.0 0.1 broadcast_and_fusion
  158.2 1.0 multiply_cosine_fusion.1
  159.2 0.1 fusion.76
  159.2 1.5 copy.102
  160.8 12.2 %fusion = f32[512]{0:T(512)S(1)} fusion(bf16[8,512,896]{2,1,0:T(8,128)(2,1)} %all-to-all-done), kind=kLoop, calls=%fused_computation.4 | loop fusion | flops 11009536 | bytes 7342080 | tf_op jit(solution)/shard_map/reduce_sum | solution.py:87
  173.0 9.3 %fusion.2 = bf16[8,512,896]{2,0,1:T(8,128)(2,1)S(1)} fusion(f32[8,896]{1,0:T(8,128)S(1)} %mul.190, f32[512]{0:T(512)S(1)} %add_rsqrt_fusion, bf16[8,512,896]{2,1,0:T(8,128)(2,1)} %all-to-all-done), kind=kLoop, calls=%fused_computation.6 | loop fusion | flops 14680064 | bytes 14710784 | tf_op jit(solution)/shard_map/convert_element_type | solution.py:91
  182.3 1.9 constant_dynamic-slice_fusion
  184.2 1.4 copy.122
  185.7 2.9 fusion.34
  188.6 109.1 %all-to-all-done.1 = bf16[16,4,77824]{2,1,0:T(4,128)(2,1)} async-done(((bf16[16,4,77824]{2,1,0:T(4,128)(2,1)}), bf16[16,4,77824]{2,1,0:T(4,128)(2,1)}, u32[]{:S(2)}, u32[]{:S(2)}) %all-to-all-start.1) | async-done | bytes 9961504 | tf_op jit(solution)/shard_map/all_to_all | solution.py:51
  297.7 10.6 %reshape.513 = bf16[64,77824]{1,0:T(8,128)(2,1)} reshape(bf16[16,4,77824]{2,1,0:T(4,128)(2,1)} %all-to-all-done.1) | data formatting | bytes 19922944 | tf_op jit(solution)/shard_map/reshape | solution.py:102
  308.4 6.8 %gather_fusion = bf16[4,77824]{1,0:T(4,128)(2,1)S(1)} fusion(bf16[64,77824]{1,0:T(8,128)(2,1)} %reshape.513, s32[1024]{0:T(1024)S(1)} %pad_clamp_fusion.1), kind=kCustom, calls=%fused_computation | custom fusion | bytes 1245200 | tf_op jit(solution)/shard_map/jit(_take)/gather | solution.py:105
  315.1 0.1 slice.80
  315.3 0.5 convolution_convert_fusion
  315.8 0.8 broadcast_in_dim.59
  316.6 5.4 %all-to-all-start.2 = ((bf16[8,4,128,48]{2,3,1,0:T(8,128)(2,1)}), bf16[8,4,128,48]{2,3,1,0:T(8,128)(2,1)S(1)}, u32[]{:S(2)}, u32[]{:S(2)}) async-start(bf16[8,4,128,48]{2,3,1,0:T(8,128)(2,1)} %broadcast_in_dim.59), calls=%async_computation.2 | async-start | bytes 786432 | tf_op jit(solution)/shard_map/all_to_all | solution.py:51
  322.0 7.6 %all-to-all-done.2 = bf16[8,4,128,48]{2,3,1,0:T(8,128)(2,1)S(1)} async-done(((bf16[8,4,128,48]{2,3,1,0:T(8,128)(2,1)}), bf16[8,4,128,48]{2,3,1,0:T(8,128)(2,1)S(1)}, u32[]{:S(2)}, u32[]{:S(2)}) %all-to-all-start.2) | async-done | bytes 393248 | tf_op jit(solution)/shard_map/all_to_all | solution.py:51
  329.7 0.3 convolution_multiply_fusion.3
  330.0 8.5 %fusion.23 = f32[4,128,512]{2,1,0:T(8,128)S(1)} fusion(f32[4,128,512]{2,1,0:T(8,128)S(1)} %convolution_multiply_fusion.3, bf16[8,896,512,1]{2,1,0,3:T(8,128)(2,1)} %bitcast.202, bf16[4,128,896,8]{2,3,1,0:T(8,128)(2,1)} %bitcast.175), kind=kOutput, calls=%fused_computation.28 | convolution fusion | flops 3758358528 | bytes 16777216 | tf_op jit(solution)/shard_map/tsf,tfc->sc/dot_general | solution.py:128
  338.5 0.4 reshape.516
  338.9 0.6 fusion.94
  339.5 0.3 subtract_convert_fusion
  339.8 0.3 pad_maximum_fusion
  340.1 0.4 copy-done.4
  340.5 1.5 fusion.3
  341.9 2.3 fusion.31
  344.2 2.2 fusion.13
  346.5 0.2 fusion.39
  346.8 1.2 fusion.69
  348.0 0.5 fusion.96
  348.5 0.2 fusion.44
  348.8 1.1 bitcast_multiply_fusion
  349.8 1.9 fusion.30
  351.7 0.3 copy.106
  352.0 0.2 reshape.559
  352.3 0.2 convolution_convert_fusion.1
  352.4 0.7 broadcast_in_dim.69
  353.1 4.8 %all-to-all-start.5 = ((bf16[8,4,128,16]{2,3,1,0:T(8,128)(2,1)}), bf16[8,4,128,16]{2,3,1,0:T(8,128)(2,1)S(1)}, u32[]{:S(2)}, u32[]{:S(2)}) async-start(bf16[8,4,128,16]{2,3,1,0:T(8,128)(2,1)} %broadcast_in_dim.69), calls=%async_computation.5 | async-start | bytes 262144 | tf_op jit(solution)/shard_map/all_to_all | solution.py:51
  357.9 9.1 %convert_bitcast_fusion = bf16[8,512,896]{2,1,0:T(8,128)(2,1)} fusion(bf16[512,512,1]{1,0,2:T(8,128)(2,1)S(1)} %reshape.559, bf16[64,8,8,896]{3,2,1,0:T(8,128)(2,1)} %bitcast.203), kind=kOutput, calls=%fused_computation.14 | convolution fusion | flops 3761766400 | bytes 15204352 | tf_op jit(solution)/shard_map/sc,ctf->tsf/dot_general | solution.py:210
  367.0 4.8 %all-to-all-start.4 = ((bf16[8,512,896]{2,1,0:T(8,128)(2,1)}), bf16[8,512,896]{2,1,0:T(8,128)(2,1)}, u32[]{:S(2)}, u32[]{:S(2)}) async-start(bf16[8,512,896]{2,1,0:T(8,128)(2,1)} %convert_bitcast_fusion), calls=%async_computation.4 | async-start | bytes 14680064 | tf_op jit(solution)/shard_map/all_to_all | solution.py:229
  371.9 1.7 convolution_multiply_fusion
  373.6 80.7 %all-to-all-done.4 = bf16[8,512,896]{2,1,0:T(8,128)(2,1)} async-done(((bf16[8,512,896]{2,1,0:T(8,128)(2,1)}), bf16[8,512,896]{2,1,0:T(8,128)(2,1)}, u32[]{:S(2)}, u32[]{:S(2)}) %all-to-all-start.4) | async-done | bytes 7340064 | tf_op jit(solution)/shard_map/all_to_all | solution.py:229
  454.3 4.4 convert_reduce_fusion
  458.7 1.1 fusion.19
  (68 shorter events, 1.3 us)
Async XLA Ops:
  0.0 2.3 copy-start
  0.0 16.1 %copy-start.7 = (bf16[4,48,896]{2,1,0:T(8,128)(2,1)S(1)}, bf16[4,48,896]{2,1,0:T(8,128)(2,1)}, u32[]{:S(2)}) copy-start(bf16[4,48,896]{2,1,0:T(8,128)(2,1)} %param.21) | copy-start | bytes 1032196
  7.5 39.6 %all-to-all-start.3 = ((bf16[2,16,128,256]{3,2,0,1:T(8,128)(2,1)}), bf16[2,16,128,256]{3,2,0,1:T(8,128)(2,1)S(1)}, u32[]{:S(2)}, u32[]{:S(2)}) async-start(bf16[2,16,128,256]{3,2,0,1:T(8,128)(2,1)} %copy.101), calls=%async_computation.3 | async-start | bytes 4194304 | tf_op jit(solution)/shard_map/all_to_all | solution.py:178
  52.1 6.8 %copy-start.10 = (bf16[4,16,512]{2,1,0:T(8,128)(2,1)S(1)}, bf16[4,16,512]{2,1,0:T(8,128)(2,1)}, u32[]{:S(2)}) copy-start(bf16[4,16,512]{2,1,0:T(8,128)(2,1)} %param.22) | copy-start | bytes 196612
  52.1 6.9 %copy-start.11 = (bf16[4,16,512]{2,1,0:T(8,128)(2,1)S(1)}, bf16[4,16,512]{2,1,0:T(8,128)(2,1)}, u32[]{:S(2)}) copy-start(bf16[4,16,512]{2,1,0:T(8,128)(2,1)} %param.24) | copy-start | bytes 196612
  52.1 6.9 %copy-start.9 = (bf16[4,16,896]{2,1,0:T(8,128)(2,1)S(1)}, bf16[4,16,896]{2,1,0:T(8,128)(2,1)}, u32[]{:S(2)}) copy-start(bf16[4,16,896]{2,1,0:T(8,128)(2,1)} %param.25) | copy-start | bytes 344068
  52.1 7.0 %copy-start.12 = (bf16[4,2,16,128]{3,2,1,0:T(8,128)(2,1)S(1)}, bf16[4,2,16,128]{3,2,1,0:T(8,128)(2,1)}, u32[]{:S(2)}) copy-start(bf16[4,2,16,128]{3,2,1,0:T(8,128)(2,1)} %param.23) | copy-start | bytes 98308
  52.1 89.2 %all-to-all-start = ((bf16[8,512,896]{2,1,0:T(8,128)(2,1)}), bf16[8,512,896]{2,1,0:T(8,128)(2,1)}, u32[]{:S(2)}, u32[]{:S(2)}) async-start(bf16[8,512,896]{2,1,0:T(8,128)(2,1)} %broadcast_in_dim.56), calls=%async_computation | async-start | bytes 14680064 | tf_op jit(solution)/shard_map/all_to_all | solution.py:51
  145.4 5.5 %copy-start.15 = (s32[32]{0:T(128)S(1)}, s32[32]{0:T(128)}, u32[]{:S(2)}) copy-start(s32[32]{0:T(128)} %param.29) | copy-start | bytes 388
  145.4 5.6 %copy-start.16 = (s32[32]{0:T(128)S(1)}, s32[32]{0:T(128)}, u32[]{:S(2)}) copy-start(s32[32]{0:T(128)} %param.28) | copy-start | bytes 388
  145.4 5.7 %copy-start.13 = (f32[7168]{0:T(1024)S(1)}, f32[7168]{0:T(1024)}, u32[]{:S(2)}) copy-start(f32[7168]{0:T(1024)} %param.17) | copy-start | bytes 86020
  145.4 152.4 %all-to-all-start.1 = ((bf16[16,4,77824]{2,1,0:T(4,128)(2,1)}), bf16[16,4,77824]{2,1,0:T(4,128)(2,1)}, u32[]{:S(2)}, u32[]{:S(2)}) async-start(bf16[16,4,77824]{2,1,0:T(4,128)(2,1)} %broadcast_in_dim.57), calls=%async_computation.1 | async-start | bytes 19922944 | tf_op jit(solution)/shard_map/all_to_all | solution.py:51
  150.9 6.8 %copy-start.14 = (s32[4]{0:T(128)S(1)}, s32[4]{0:T(128)}, u32[]{:S(2)}) copy-start(s32[4]{0:T(128)} %param.26) | copy-start | bytes 52
  150.9 6.9 %copy-start.17 = (s32[4]{0:T(128)S(1)}, s32[4]{0:T(128)}, u32[]{:S(2)}) copy-start(s32[4]{0:T(128)} %param.27) | copy-start | bytes 52
  173.0 12.7 %copy-start.5 = (bf16[8,896,256]{1,2,0:T(8,128)(2,1)S(1)}, bf16[8,896,256]{1,2,0:T(8,128)(2,1)}, u32[]{:S(2)}) copy-start(bf16[8,896,256]{1,2,0:T(8,128)(2,1)} %copy.93) | copy-start | bytes 11010052
  182.3 3.3 copy-start.2
  188.6 126.7 %copy-start.6 = (bf16[1,512,896]{2,1,0:T(8,128)(2,1)S(1)}, bf16[1,512,896]{2,1,0:T(8,128)(2,1)}, u32[]{:S(2)}) copy-start(bf16[1,512,896]{2,1,0:T(8,128)(2,1)} %copy.122) | copy-start | bytes 2752516
  316.6 13.1 %all-to-all-start.2 = ((bf16[8,4,128,48]{2,3,1,0:T(8,128)(2,1)}), bf16[8,4,128,48]{2,3,1,0:T(8,128)(2,1)S(1)}, u32[]{:S(2)}, u32[]{:S(2)}) async-start(bf16[8,4,128,48]{2,3,1,0:T(8,128)(2,1)} %broadcast_in_dim.59), calls=%async_computation.2 | async-start | bytes 786432 | tf_op jit(solution)/shard_map/all_to_all | solution.py:51
  338.9 1.6 copy-start.4
  344.2 2.3 copy-start.8
  353.1 13.9 %all-to-all-start.5 = ((bf16[8,4,128,16]{2,3,1,0:T(8,128)(2,1)}), bf16[8,4,128,16]{2,3,1,0:T(8,128)(2,1)S(1)}, u32[]{:S(2)}, u32[]{:S(2)}) async-start(bf16[8,4,128,16]{2,3,1,0:T(8,128)(2,1)} %broadcast_in_dim.69), calls=%async_computation.5 | async-start | bytes 262144 | tf_op jit(solution)/shard_map/all_to_all | solution.py:51
  367.0 87.3 %all-to-all-start.4 = ((bf16[8,512,896]{2,1,0:T(8,128)(2,1)}), bf16[8,512,896]{2,1,0:T(8,128)(2,1)}, u32[]{:S(2)}, u32[]{:S(2)}) async-start(bf16[8,512,896]{2,1,0:T(8,128)(2,1)} %convert_bitcast_fusion), calls=%async_computation.4 | async-start | bytes 14680064 | tf_op jit(solution)/shard_map/all_to_all | solution.py:229
  371.9 87.9 %copy-start.1 = (bf16[32,128,256]{2,1,0:T(8,128)(2,1)S(1)}, bf16[32,128,256]{2,1,0:T(8,128)(2,1)}, u32[]{:S(2)}) copy-start(bf16[32,128,256]{2,1,0:T(8,128)(2,1)} %param.31) | copy-start | bytes 6291460
  454.3 4.4 copy-start.3

commit v2 on v1

--- a/solution.py
+++ b/solution.py
@@ -81,7 +81,7 @@
     group_size = query_weight.shape[1] // (HEAD_SIZE * local_kv)
     page_rows = cache_page_pool.shape[1]
     tensor_count = lax.axis_size("tensor")
-    gathered = gather_by_exchange(residual_input, "tensor", tensor_count)
+    gathered = lax.all_gather(residual_input, "tensor", axis=0, tiled=False)
     widened = gathered.astype(jnp.float32)
     inverse = lax.rsqrt(
         jnp.sum(widened * widened, axis=(0, 2), keepdims=True) / (tensor_count * piece_width)
@@ -99,7 +99,7 @@
     local_adapters = adapter_down_maps.shape[0]
     flat_parts = [part.reshape(local_adapters, -1) for part in adapter_parts]
     joined = jnp.concatenate(flat_parts, axis=1)
-    every_adapter = gather_by_exchange(joined, "req", holders).reshape(
+    every_adapter = lax.all_gather(joined, "req", axis=0, tiled=False).reshape(
         holders * local_adapters, joined.shape[1]
     )
     picked = jnp.take(every_adapter, request_adapter, axis=0, mode="clip")
@@ -225,13 +225,9 @@
         .sum(axis=0)
         .astype(jnp.bfloat16)
     )
-    head_total = (
-        lax.all_to_all(
-            head_terms.astype(jnp.bfloat16), "tensor", split_axis=0, concat_axis=0, tiled=True
-        )
-        .astype(jnp.float32)
-        .sum(axis=0)
-    )
+    head_total = lax.psum_scatter(
+        head_terms.astype(jnp.bfloat16), "tensor", scatter_dimension=0, tiled=False
+    ).astype(jnp.float32)
     adapter_output = jnp.einsum(
         "ibm,imf->ibf", reduced_output, oup_sel, preferred_element_type=jnp.float32
     ).reshape(row_count, -1)

time: 464 us -> 251 us (0.54)
  waiting for transfers between devices: 310 us -> 119 us
  starting transfers between devices: 35.7 us -> 18.2 us
  other arithmetic: 35.5 us -> 19.9 us
  between operations: 0.79 us -> 13.5 us
  matrix products: 29.5 us -> 36.1 us
  local copies, waits for them, and re-layouts: 48.4 us -> 43.2 us
    all_to_all x4 -> x2, waiting for transfers between devices: 199 us -> 13.1 us  [gather_by_exchange(): lax.all_to_all(spread, axis_name, split_axis=0, concat_axis=0, tiled=True)]
    all_to_all x1 -> x0, waiting for transfers between devices: 80.7 us -> none  [local(): lax.all_to_all(head_terms.astype(jnp.bfloat16), 'tensor', split_axis=0, c...]
    all_gather x0 -> x2, waiting for transfers between devices: none -> 50 us  [the longest x1 50 us: local(): lax.all_gather(joined, 'req', axis=0, tiled=False)]
    reduce_scatter x0 -> x1, waiting for transfers between devices: none -> 32.7 us  [local(): lax.psum_scatter(head_terms.astype(jnp.bfloat16), 'tensor', scatter_dimen...]
    unnamed x50 -> x40, local copies, waits for them, and re-layouts: 3.06 us -> 17.5 us
    all_to_all x4 -> x2, starting transfers between devices: 22.3 us -> 9.59 us  [gather_by_exchange(): lax.all_to_all(spread, axis_name, split_axis=0, concat_axis=0, tiled=True)]
    reshape x1 -> x0, local copies, waits for them, and re-layouts: 10.6 us -> none  [local(): gather_by_exchange(joined, 'req', holders)]
    broadcast_in_dim x4 -> x2, local copies, waits for them, and re-layouts: 10.6 us -> 1.48 us  [gather_by_exchange(): spread = jnp.broadcast_to(piece[None], (count,) + piece.shape)]
  transfers between devices with their start and end apart: 6 -> 6, of which waited for: 5 -> 5; matrix products, arithmetic and copies ran while one was open for 11% -> 20% of each run, Pallas kernels for 0% -> 0%
where the time goes in v2:
time: 251 us; the launch traced here: 250 us
  waiting for transfers between devices  119 us (47%)
  local copies, waits for them, and re-layouts  43.2 us (17%)
  matrix products  36.1 us (14%)
  other arithmetic  19.9 us (8%)
  starting transfers between devices  18.2 us (7%)
  between operations  13.5 us (5%)
    all_gather x1, waiting for transfers between devices, local(): lax.all_gather(joined, 'req', axis=0, tiled=False)  50 us
    reduce_scatter x1, waiting for transfers between devices, local(): lax.psum_scatter(head_terms.astype(jnp.bfloat16), 'tensor', scatter_dimen...  32.7 us
    all_to_all x1, waiting for transfers between devices, local(): lax.all_to_all(outgoing, 'req', split_axis=1, concat_axis=1, tiled=True)  22.6 us
    unnamed x40, local copies, waits for them, and re-layouts  17.5 us
    all_to_all x2, waiting for transfers between devices, gather_by_exchange(): lax.all_to_all(spread, axis_name, split_axis=0, concat_axis=0, tiled=True)  13.1 us
    dot_general x1, matrix products, local(): jnp.einsum('sc,ctf->tsf', attended, output_weight.reshape(output_weight.s...  10.3 us
    all_to_all x2, starting transfers between devices, gather_by_exchange(): lax.all_to_all(spread, axis_name, split_axis=0, concat_axis=0, tiled=True)  9.59 us
    all_to_all x1, starting transfers between devices, local(): lax.all_to_all(outgoing, 'req', split_axis=1, concat_axis=1, tiled=True)  8.59 us
  transfers between devices with their start and end apart: 6, of which 5 were waited for; matrix products, arithmetic and copies ran while one was open for 20% of the time, Pallas kernels for 0%

profile of v2, /device:TPU:1, one launch (start us, length us, event | category | flops | bytes accessed | tf_op | source)
XLA Modules:
  0.0 250.1 jit_solution(4971301358374243776)
XLA Ops:
  6.5 0.7 all-gather.6.cloned.1.call-update
  7.3 0.9 copy.134
  8.2 0.9 copy.136
  9.1 0.9 copy.137
  10.0 1.1 copy.133
  11.2 0.1 constant_dynamic-update-slice_fusion.3
  11.4 0.8 bitcast_dynamic-update-slice_fusion
  12.3 0.8 copy-done.4
  13.1 0.5 broadcast.283
  13.6 1.3 reduce.13
  14.9 0.1 reshape_squeeze.3
  15.0 0.1 copy.101
  15.1 0.1 reshape.523
  15.2 2.0 gather_fusion.1
  17.3 3.1 %copy.102 = bf16[2,16,128,256]{3,2,0,1:T(8,128)(2,1)} copy(bf16[2,16,128,256]{3,2,1,0:T(8,128)(2,1)} %bitcast.194) | data formatting | bytes 4194304 | tf_op jit(solution)/shard_map/reshape | solution.py:175
  20.4 8.6 %all-to-all-start.1 = ((bf16[2,16,128,256]{3,2,0,1:T(8,128)(2,1)}), bf16[2,16,128,256]{3,2,0,1:T(8,128)(2,1)S(1)}, u32[]{:S(2)}, u32[]{:S(2)}) async-start(bf16[2,16,128,256]{3,2,0,1:T(8,128)(2,1)} %copy.102), calls=%async_computation.1 | async-start | bytes 4194304 | tf_op jit(solution)/shard_map/all_to_all | solution.py:178
  29.1 0.1 dynamic-slice_bitcast_fusion
  29.3 0.1 copy.129
  29.5 0.1 add.131
  29.6 6.3 %copy.94 = bf16[8,896,256]{1,2,0:T(8,128)(2,1)} copy(bf16[8,896,256]{2,1,0:T(8,128)(2,1)} %bitcast.199) | data formatting | bytes 7340032 | tf_op jit(solution)/shard_map/reshape | solution.py:143
  35.9 0.1 fusion.74
  36.1 0.1 broadcast_and_fusion
  36.3 1.0 multiply_cosine_fusion.1
  37.3 0.1 fusion.66
  37.4 22.6 %all-to-all-done.1 = bf16[2,16,128,256]{3,2,0,1:T(8,128)(2,1)S(1)} async-done(((bf16[2,16,128,256]{3,2,0,1:T(8,128)(2,1)}), bf16[2,16,128,256]{3,2,0,1:T(8,128)(2,1)S(1)}, u32[]{:S(2)}, u32[]{:S(2)}) %all-to-all-start.1) | async-done | bytes 2097184 | tf_op jit(solution)/shard_map/all_to_all | solution.py:178
  59.9 1.5 copy.103
  61.5 4.7 %fusion = f32[512]{0:T(512)S(1)} fusion(bf16[8,512,896]{2,1,0:T(8,128)(2,1)} %bitcast.189), kind=kLoop, calls=%fused_computation.4 | loop fusion | flops 11009536 | bytes 7342080 | tf_op jit(solution)/shard_map/reduce_sum | solution.py:87
  66.2 0.4 copy-done.2
  66.7 5.2 %fusion.2 = bf16[8,512,896]{2,1,0:T(8,128)(2,1)} fusion(f32[8,896]{1,0:T(8,128)S(1)} %mul.190, f32[512]{0:T(512)S(1)} %add_rsqrt_fusion, bf16[4096,896]{1,0:T(8,128)(2,1)S(1)} %copy-done.2), kind=kLoop, calls=%fused_computation.6 | loop fusion | flops 14680064 | bytes 14710784 | tf_op jit(solution)/shard_map/convert_element_type | solution.py:91
  71.9 1.3 constant_dynamic-slice_fusion
  73.1 7.3 %fusion.23 = f32[4,128,1,256]{3,1,0,2:T(8,128)} fusion(bf16[4,128,896,8]{2,1,0,3:T(8,128)(2,1)} %bitcast.190, bf16[8,896,256]{1,2,0:T(8,128)(2,1)} %copy.94), kind=kOutput, calls=%fused_computation.33 | convolution fusion | flops 1879048192 | bytes 11534336 | tf_op jit(solution)/shard_map/tsf,tfc->sc/dot_general | solution.py:140
  80.4 7.3 %convolution_bitcast_fusion = f32[4,128,512]{2,1,0:T(8,128)} fusion(bf16[4,128,896,8]{2,1,0,3:T(8,128)(2,1)S(1)} %bitcast.193, bf16[8,896,512,1]{2,1,3,0:T(8,128)(2,1)} %bitcast.221), kind=kOutput, calls=%fused_computation.23 | convolution fusion | flops 3758096384 | bytes 15728640 | tf_op jit(solution)/shard_map/tsf,tfc->sc/dot_general | solution.py:128
  87.7 50.0 %all-gather.8.cloned.1.call-done = bf16[16,4,77824]{2,1,0:T(4,128)(2,1)} async-done(((bf16[1,4,77824]{2,1,0:T(4,128)(2,1)}), bf16[16,4,77824]{2,1,0:T(4,128)(2,1)}) %all-gather.8.cloned.1.call-update) | async-done | bytes 9961488 | tf_op jit(solution)/shard_map/all_gather | solution.py:102
  137.7 10.6 %reshape.557 = bf16[64,77824]{1,0:T(8,128)(2,1)} reshape(bf16[16,4,77824]{2,1,0:T(4,128)(2,1)} %all-gather.8.cloned.1.call-done) | data formatting | bytes 19922944
  148.3 6.8 %gather_fusion = bf16[4,77824]{1,0:T(4,128)(2,1)S(1)} fusion(bf16[64,77824]{1,0:T(8,128)(2,1)} %reshape.557, s32[1024]{0:T(1024)S(1)} %pad_clamp_fusion.1), kind=kCustom, calls=%fused_computation | custom fusion | bytes 1245200 | tf_op jit(solution)/shard_map/jit(_take)/gather | solution.py:105
  155.1 0.1 slice.80
  155.2 0.5 convolution_convert_fusion
  155.7 0.8 broadcast_in_dim.53
  156.5 5.1 %all-to-all-start = ((bf16[8,4,128,48]{2,3,1,0:T(8,128)(2,1)}), bf16[8,4,128,48]{2,3,1,0:T(8,128)(2,1)S(1)}, u32[]{:S(2)}, u32[]{:S(2)}) async-start(bf16[8,4,128,48]{2,3,1,0:T(8,128)(2,1)} %broadcast_in_dim.53), calls=%async_computation | async-start | bytes 786432 | tf_op jit(solution)/shard_map/all_to_all | solution.py:51
  161.7 7.6 %all-to-all-done = bf16[8,4,128,48]{2,3,1,0:T(8,128)(2,1)S(1)} async-done(((bf16[8,4,128,48]{2,3,1,0:T(8,128)(2,1)}), bf16[8,4,128,48]{2,3,1,0:T(8,128)(2,1)S(1)}, u32[]{:S(2)}, u32[]{:S(2)}) %all-to-all-start) | async-done | bytes 393248 | tf_op jit(solution)/shard_map/all_to_all | solution.py:51
  169.3 1.6 fusion.21
  170.9 0.4 reshape.516
  171.3 0.6 fusion.84
  171.9 0.3 subtract_convert_fusion
  172.2 0.3 pad_maximum_fusion
  172.5 2.7 %fusion.3 = (f32[2,128,4]{1,2,0:T(4,128)S(1)}, f32[2,128,4,2048]{3,1,2,0:T(8,128)S(1)}) fusion(pred[2,2048]{1,0:T(4,128)(4,1)S(1)} %fusion.66, bf16[2,2048,1,256]{3,1,0,2:T(8,128)(2,1)} %bitcast.197, bf16[4,128,1,4,128]{4,1,3,0,2:T(8,128)(2,1)S(1)} %pad_maximum_fusion), kind=kOutput, calls=%fused_computation.9 | convolution fusion | flops 543161344 | bytes 9711616 | tf_op jit(solution)/shard_map/bsvgd,bkvd->bvsgk/dot_general | solution.py:32
  175.2 2.3 fusion.26
  177.5 2.2 fusion.9
  179.7 0.2 fusion.29
  180.0 1.2 fusion.59
  181.3 0.5 fusion.86
  181.8 0.2 fusion.34
  182.1 0.1 bitcast_multiply_fusion
  182.2 1.5 fusion.22
  183.7 0.3 copy.107
  184.0 1.0 reshape.566
  185.0 10.3 %convert_bitcast_fusion = bf16[8,512,896]{2,1,0:T(8,128)(2,1)} fusion(bf16[512,512,1]{1,0,2:T(8,128)(2,1)} %reshape.566, bf16[64,8,8,896]{3,2,1,0:T(8,128)(2,1)} %bitcast.222), kind=kOutput, calls=%fused_computation.13 | convolution fusion | flops 3761766400 | bytes 15204352 | tf_op jit(solution)/shard_map/sc,ctf->tsf/dot_general | solution.py:210
  195.4 0.2 convolution_convert_fusion.1
  195.5 0.7 broadcast_in_dim.99
  196.2 4.5 %all-to-all-start.2 = ((bf16[8,4,128,16]{2,3,1,0:T(8,128)(2,1)}), bf16[8,4,128,16]{2,3,1,0:T(8,128)(2,1)S(1)}, u32[]{:S(2)}, u32[]{:S(2)}) async-start(bf16[8,4,128,16]{2,3,1,0:T(8,128)(2,1)} %broadcast_in_dim.99), calls=%async_computation.3 | async-start | bytes 262144 | tf_op jit(solution)/shard_map/all_to_all | solution.py:51
  200.8 5.5 %all-to-all-done.2 = bf16[8,4,128,16]{2,3,1,0:T(8,128)(2,1)S(1)} async-done(((bf16[8,4,128,16]{2,3,1,0:T(8,128)(2,1)}), bf16[8,4,128,16]{2,3,1,0:T(8,128)(2,1)S(1)}, u32[]{:S(2)}, u32[]{:S(2)}) %all-to-all-start.2) | async-done | bytes 131104 | tf_op jit(solution)/shard_map/all_to_all | solution.py:51
  206.3 1.7 convolution_multiply_fusion
  208.0 32.7 %reduce-scatter.2.cloned.1.call-done = bf16[1,512,896]{2,1,0:T(8,128)(2,1)} async-done(((bf16[8,512,896]{2,1,0:T(8,128)(2,1)}), bf16[1,512,896]{2,1,0:T(8,128)(2,1)}) %reduce-scatter.2.cloned.1.call-update) | async-done | bytes 917520 | tf_op jit(solution)/shard_map/reduce_scatter | solution.py:228
  240.7 2.8 %fusion.16 = bf16[512,896]{1,0:T(8,128)(2,1)} fusion(f32[4,128,896]{2,1,0:T(8,128)} %convolution_multiply_fusion, bf16[1,512,896]{2,1,0:T(8,128)(2,1)} %reduce-scatter.2.cloned.1.call-done), kind=kLoop, calls=%fused_computation.21 | loop fusion | flops 1376256 | bytes 3670016 | tf_op jit(solution)/shard_map/convert_element_type | solution.py:234
  (58 shorter events, 1.1 us)
Async XLA Ops:
  6.5 8.7 %copy-start = (bf16[32,128,256]{2,1,0:T(8,128)(2,1)S(1)}, bf16[32,128,256]{2,1,0:T(8,128)(2,1)}, u32[]{:S(2)}) copy-start(bf16[32,128,256]{2,1,0:T(8,128)(2,1)} %param.31) | copy-start | bytes 6291460
  6.5 54.9 %all-gather.6.cloned.1.call-start = ((), (), s32[]{:S(2)}) async-start(), calls=%async_computation.5 | async-start | bytes 8257536 | tf_op jit(solution)/shard_map/all_gather | solution.py:84
  7.3 130.4 %all-gather.8.cloned.1.call-start = ((), (), s32[]{:S(2)}) async-start(), calls=%async_computation.6 | async-start | bytes 10584064 | tf_op jit(solution)/shard_map/all_gather | solution.py:102
  11.2 17.9 %copy-start.7 = (s32[4]{0:T(128)S(1)}, s32[4]{0:T(128)}, u32[]{:S(2)}) copy-start(s32[4]{0:T(128)} %param.26) | copy-start | bytes 52
  11.2 17.9 %copy-start.8 = (s32[32]{0:T(128)S(1)}, s32[32]{0:T(128)}, u32[]{:S(2)}) copy-start(s32[32]{0:T(128)} %param.28) | copy-start | bytes 388
  11.2 18.0 %copy-start.9 = (s32[32]{0:T(128)S(1)}, s32[32]{0:T(128)}, u32[]{:S(2)}) copy-start(s32[32]{0:T(128)} %param.29) | copy-start | bytes 388
  11.2 18.4 %copy-start.6 = (f32[7168]{0:T(1024)S(1)}, f32[7168]{0:T(1024)}, u32[]{:S(2)}) copy-start(f32[7168]{0:T(1024)} %param.17) | copy-start | bytes 86020
  12.3 0.8 copy-start.4
  17.3 18.6 %copy-start.10 = (s32[4]{0:T(128)S(1)}, s32[4]{0:T(128)}, u32[]{:S(2)}) copy-start(s32[4]{0:T(128)} %param.27) | copy-start | bytes 52
  20.4 39.5 %all-to-all-start.1 = ((bf16[2,16,128,256]{3,2,0,1:T(8,128)(2,1)}), bf16[2,16,128,256]{3,2,0,1:T(8,128)(2,1)S(1)}, u32[]{:S(2)}, u32[]{:S(2)}) async-start(bf16[2,16,128,256]{3,2,0,1:T(8,128)(2,1)} %copy.102), calls=%async_computation.1 | async-start | bytes 4194304 | tf_op jit(solution)/shard_map/all_to_all | solution.py:178
  61.5 5.2 %copy-start.2 = (bf16[4096,896]{1,0:T(8,128)(2,1)S(1)}, bf16[4096,896]{1,0:T(8,128)(2,1)}, u32[]{:S(2)}) copy-start(bf16[4096,896]{1,0:T(8,128)(2,1)} %all-gather.6.cloned.1.call-done) | copy-start | bytes 22020100
  73.1 7.3 %slice-start = ((s8[7340032]{0:T(1024)(128)(4,1)}), s8[4194304]{0:T(1024)(128)(4,1)S(1)}, s32[]{:S(2)}) async-start(s8[7340032]{0:T(1024)(128)(4,1)} %bitcast.191), calls=%async_computation.7 | async-start | bytes 8388608
  73.1 7.3 %slice-start.1 = ((s8[7340032]{0:T(1024)(128)(4,1)}), s8[3145728]{0:T(1024)(128)(4,1)S(1)}, s32[]{:S(2)}) async-start(s8[7340032]{0:T(1024)(128)(4,1)} %bitcast.191), calls=%async_computation.8 | async-start | bytes 6291456
  156.5 12.8 %all-to-all-start = ((bf16[8,4,128,48]{2,3,1,0:T(8,128)(2,1)}), bf16[8,4,128,48]{2,3,1,0:T(8,128)(2,1)S(1)}, u32[]{:S(2)}, u32[]{:S(2)}) async-start(bf16[8,4,128,48]{2,3,1,0:T(8,128)(2,1)} %broadcast_in_dim.53), calls=%async_computation | async-start | bytes 786432 | tf_op jit(solution)/shard_map/all_to_all | solution.py:51
  161.6 79.1 %reduce-scatter.2.cloned.1.call-start = ((), (), s32[]{:S(2)}) async-start(), calls=%async_computation.4 | async-start | bytes 8257536 | tf_op jit(solution)/shard_map/reduce_scatter | solution.py:228
  171.9 3.3 %copy-start.3 = (bf16[2,16,128,256]{3,2,1,0:T(8,128)(2,1)S(1)}, bf16[2,16,128,256]{3,2,1,0:T(8,128)(2,1)}, u32[]{:S(2)}) copy-start(bf16[2,16,128,256]{3,2,1,0:T(8,128)(2,1)} %copy.103) | copy-start | bytes 6291460
  177.5 2.2 copy-start.5
  185.0 58.5 %copy-start.1 = (bf16[32,128,256]{2,1,0:T(8,128)(2,1)S(1)}, bf16[32,128,256]{2,1,0:T(8,128)(2,1)}, u32[]{:S(2)}) copy-start(bf16[32,128,256]{2,1,0:T(8,128)(2,1)} %param.31) | copy-start | bytes 6291460
  196.2 10.0 %all-to-all-start.2 = ((bf16[8,4,128,16]{2,3,1,0:T(8,128)(2,1)}), bf16[8,4,128,16]{2,3,1,0:T(8,128)(2,1)S(1)}, u32[]{:S(2)}, u32[]{:S(2)}) async-start(bf16[8,4,128,16]{2,3,1,0:T(8,128)(2,1)} %broadcast_in_dim.99), calls=%async_computation.3 | async-start | bytes 262144 | tf_op jit(solution)/shard_map/all_to_all | solution.py:51
Sparse Core Ops, SparseCore 0:
  9.0 48.8 all-gather.5
  60.0 77.6 all-gather.7
  195.5 45.2 reduce-scatter.1

commit v3 on v2

--- a/solution.py
+++ b/solution.py
@@ -70,6 +70,7 @@
     cache_page_pool,
 ):
     holders = lax.axis_size("req")
+    tensor_count = lax.axis_size("tensor")
     req_index = lax.axis_index("req")
     tensor_index = lax.axis_index("tensor")
     request_number = request_adapter.shape[0]
@@ -81,14 +82,10 @@
     group_size = query_weight.shape[1] // (HEAD_SIZE * local_kv)
     page_rows = cache_page_pool.shape[1]
     tensor_count = lax.axis_size("tensor")
-    gathered = lax.all_gather(residual_input, "tensor", axis=0, tiled=False)
+    gathered = lax.all_gather(residual_input, "tensor", axis=1, tiled=True)
     widened = gathered.astype(jnp.float32)
-    inverse = lax.rsqrt(
-        jnp.sum(widened * widened, axis=(0, 2), keepdims=True) / (tensor_count * piece_width)
-        + EPSILON
-    )
-    gain_parts = input_norm_gain.reshape(tensor_count, 1, piece_width)
-    normed_parts = (widened * inverse * gain_parts).astype(jnp.bfloat16)
+    inverse = lax.rsqrt(jnp.mean(widened * widened, axis=1, keepdims=True) + EPSILON)
+    normed = (widened * inverse * input_norm_gain).astype(jnp.bfloat16)
     adapter_parts = (
         adapter_down_maps,
         adapter_query_up,
@@ -99,10 +96,13 @@
     local_adapters = adapter_down_maps.shape[0]
     flat_parts = [part.reshape(local_adapters, -1) for part in adapter_parts]
     joined = jnp.concatenate(flat_parts, axis=1)
-    every_adapter = lax.all_gather(joined, "req", axis=0, tiled=False).reshape(
-        holders * local_adapters, joined.shape[1]
-    )
-    picked = jnp.take(every_adapter, request_adapter, axis=0, mode="clip")
+    lane_rows = joined.shape[1] // 128
+    every_adapter = lax.all_gather(
+        joined.reshape(local_adapters, lane_rows, 128), "req", axis=0, tiled=True
+    )
+    picked = jnp.take(every_adapter, request_adapter, axis=0, mode="clip").reshape(
+        request_number, -1
+    )
     picked_parts = []
     start = 0
     for part, flat in zip(adapter_parts, flat_parts):
@@ -113,9 +113,9 @@
         start += width
     down_picked, query_picked, key_value_picked, output_down_picked, oup_sel = picked_parts
     adapter_rank_size = query_picked.shape[1]
-    own_columns = lax.dynamic_index_in_dim(normed_parts, tensor_index, 0, keepdims=False).reshape(
-        request_number, request_slot_rows, piece_width
-    )
+    own_columns = lax.dynamic_slice_in_dim(
+        normed, tensor_index * piece_width, piece_width, 1
+    ).reshape(request_number, request_slot_rows, piece_width)
     partial_low = jnp.einsum(
         "rsd,rkd->rsk", own_columns, down_picked, preferred_element_type=jnp.float32
     )
@@ -125,24 +125,14 @@
         .sum(axis=0)
         .astype(jnp.bfloat16)
     )
-    query_rows = jnp.einsum(
-        "tsf,tfc->sc",
-        normed_parts,
-        query_weight.reshape(tensor_count, piece_width, -1),
-        preferred_element_type=jnp.float32,
-    ).reshape(request_number, request_slot_rows, -1)
+    query_rows = jnp.dot(normed, query_weight, preferred_element_type=jnp.float32).reshape(request_number, request_slot_rows, -1)
     query_rows = query_rows + ADAPTER_SCALE * jnp.einsum(
         "ibm,imf->ibf",
         reduced_input[..., :adapter_rank_size],
         query_picked,
         preferred_element_type=jnp.float32,
     )
-    keyval = jnp.einsum(
-        "tsf,tfc->sc",
-        normed_parts,
-        key_value_weight.reshape(tensor_count, piece_width, -1),
-        preferred_element_type=jnp.float32,
-    ).reshape(
+    keyval = jnp.dot(normed, key_value_weight, preferred_element_type=jnp.float32).reshape(
         request_number, request_slot_rows, local_kv, 2 * HEAD_SIZE
     )
     key_add = jnp.einsum(

time: 251 us -> 240 us (0.956)
  local copies, waits for them, and re-layouts: 43.2 us -> 26.6 us
    unnamed x40 -> x54, local copies, waits for them, and re-layouts: 17.5 us -> 8.75 us
    reshape x1 -> x0, local copies, waits for them, and re-layouts: 6.26 us -> none  [local(): key_value_weight.reshape(tensor_count, piece_width, -1)]
    all_to_all x1, waiting for transfers between devices: 22.6 us -> 27.7 us  [local(): lax.all_to_all(outgoing, 'req', split_axis=1, concat_axis=1, tiled=True)]
    all_gather x2, waiting for transfers between devices: 50 us -> 47.2 us  [the longest x1 47.2 us: local(): lax.all_gather(joined.reshape(local_adapters, lane_rows, 128), 'req', axi...]
  transfers between devices with their start and end apart: 6 -> 6, of which waited for: 5 -> 5; matrix products, arithmetic and copies ran while one was open for 20% -> 21% of each run, Pallas kernels for 0% -> 0%
where the time goes in v3:
time: 240 us; the launch traced here: 239 us
  waiting for transfers between devices  120 us (50%)
  matrix products  38.3 us (16%)
  local copies, waits for them, and re-layouts  26.6 us (11%)
  other arithmetic  22 us (9%)
  starting transfers between devices  18.3 us (8%)
  between operations  13.5 us (6%)
    all_gather x1, waiting for transfers between devices, local(): lax.all_gather(joined.reshape(local_adapters, lane_rows, 128), 'req', axi...  47.2 us
    reduce_scatter x1, waiting for transfers between devices, local(): lax.psum_scatter(head_terms.astype(jnp.bfloat16), 'tensor', scatter_dimen...  32.3 us
    all_to_all x1, waiting for transfers between devices, local(): lax.all_to_all(outgoing, 'req', split_axis=1, concat_axis=1, tiled=True)  27.7 us
    all_to_all x2, waiting for transfers between devices, gather_by_exchange(): lax.all_to_all(spread, axis_name, split_axis=0, concat_axis=0, tiled=True)  12.3 us
    dot_general x1, matrix products, local(): jnp.einsum('sc,ctf->tsf', attended, output_weight.reshape(output_weight.s...  10.3 us
    dot_general x1, matrix products, local(): jnp.dot(normed, query_weight, preferred_element_type=jnp.float32)  10.2 us
    all_to_all x2, starting transfers between devices, gather_by_exchange(): lax.all_to_all(spread, axis_name, split_axis=0, concat_axis=0, tiled=True)  9.59 us
    unnamed x54, local copies, waits for them, and re-layouts  8.75 us
  transfers between devices with their start and end apart: 6, of which 5 were waited for; matrix products, arithmetic and copies ran while one was open for 21% of the time, Pallas kernels for 0%

profile of v3, /device:TPU:1, one launch (start us, length us, event | category | flops | bytes accessed | tf_op | source)
XLA Modules:
  0.0 239.0 jit_solution(7470097083565520807)
XLA Ops:
  6.5 0.7 all-gather.3.cloned.1.call-update
  7.3 0.9 copy.103
  8.2 0.9 copy.105
  9.1 0.9 copy.106
  10.0 1.1 copy.102
  11.2 0.1 constant_dynamic-update-slice_fusion.3
  11.3 0.8 bitcast_dynamic-update-slice_fusion
  12.3 0.9 copy.146
  13.2 0.5 broadcast.284
  13.7 1.2 reduce.13
  15.0 0.1 copy.72
  15.1 0.1 reshape.517
  15.2 2.0 gather_fusion.1
  17.2 3.1 %copy.73 = bf16[2,16,128,256]{3,2,0,1:T(8,128)(2,1)} copy(bf16[2,16,128,256]{3,2,1,0:T(8,128)(2,1)} %bitcast.165) | data formatting | bytes 4194304 | tf_op jit(solution)/shard_map/reshape | solution.py:165
  20.4 8.7 %all-to-all-start.1 = ((bf16[2,16,128,256]{3,2,0,1:T(8,128)(2,1)}), bf16[2,16,128,256]{3,2,0,1:T(8,128)(2,1)S(1)}, u32[]{:S(2)}, u32[]{:S(2)}) async-start(bf16[2,16,128,256]{3,2,0,1:T(8,128)(2,1)} %copy.73), calls=%async_computation.1 | async-start | bytes 4194304 | tf_op jit(solution)/shard_map/all_to_all | solution.py:168
  29.4 0.1 copy.98
  29.6 0.1 add.130
  30.0 0.8 broadcast_and_fusion
  30.7 1.0 multiply_cosine_fusion
  31.7 0.7 fusion.61
  32.4 27.7 %all-to-all-done.1 = bf16[2,16,128,256]{3,2,0,1:T(8,128)(2,1)S(1)} async-done(((bf16[2,16,128,256]{3,2,0,1:T(8,128)(2,1)}), bf16[2,16,128,256]{3,2,0,1:T(8,128)(2,1)S(1)}, u32[]{:S(2)}, u32[]{:S(2)}) %all-to-all-start.1) | async-done | bytes 2097184 | tf_op jit(solution)/shard_map/all_to_all | solution.py:168
  60.0 1.6 copy.74
  61.6 4.7 %fusion = f32[512]{0:T(512)S(1)} fusion(bf16[512,7168]{1,0:T(8,128)(2,1)} %all-gather.3.cloned.1.call-done), kind=kLoop, calls=%fused_computation.4 | loop fusion | flops 11009536 | bytes 7342080 | tf_op jit(solution)/shard_map/reduce_sum | solution.py:87
  66.4 0.4 copy-done.2
  66.8 5.8 %fusion.2 = bf16[512,7168]{1,0:T(8,128)(2,1)} fusion(bf16[512,7168]{1,0:T(8,128)(2,1)S(1)} %copy-done.2, f32[7168]{0:T(1024)S(1)} %copy-done.9, f32[512]{0:T(512)S(1)} %add_rsqrt_fusion), kind=kLoop, calls=%fused_computation.6 | loop fusion | flops 14680064 | bytes 14710784 | tf_op jit(solution)/shard_map/convert_element_type | solution.py:88
  72.6 6.2 %fusion.83 = f32[512,256]{1,0:T(8,128)S(1)} fusion(bf16[512,7168]{1,0:T(8,128)(2,1)} %fusion.2, bf16[7168,256]{1,0:T(8,128)(2,1)} %param.19), kind=kOutput, calls=%fused_computation.131 | convolution fusion | flops 1879048192 | bytes 11534336 | tf_op jit(solution)/shard_map/dot_general | solution.py:135
  78.8 0.1 copy.95
  79.0 1.3 constant_dynamic-slice_fusion
  80.3 10.2 %fusion.82 = f32[512,512]{1,0:T(8,128)} fusion(bf16[512,7168]{1,0:T(8,128)(2,1)} %fusion.2, bf16[7168,512]{1,0:T(8,128)(2,1)} %param.18), kind=kOutput, calls=%fused_computation.130 | convolution fusion | flops 3758096384 | bytes 15728640 | tf_op jit(solution)/shard_map/dot_general | solution.py:128
  90.5 47.2 %all-gather.5.cloned.1.call-done = bf16[64,608,128]{2,1,0:T(8,128)(2,1)} async-done(((bf16[4,608,128]{2,1,0:T(8,128)(2,1)}), bf16[64,608,128]{2,1,0:T(8,128)(2,1)}) %all-gather.5.cloned.1.call-update) | async-done | bytes 9961488 | tf_op jit(solution)/shard_map/all_gather | solution.py:100
  137.7 4.5 %gather_fusion = bf16[4,608,128]{2,1,0:T(8,128)(2,1)S(1)} fusion(bf16[64,608,128]{2,1,0:T(8,128)(2,1)} %all-gather.5.cloned.1.call-done, s32[1024]{0:T(1024)S(1)} %pad_clamp_fusion.1), kind=kCustom, calls=%fused_computation | custom fusion | bytes 1245200 | tf_op jit(solution)/shard_map/jit(_take)/gather | solution.py:103
  142.2 0.3 copy.145
  142.5 0.1 slice.80
  142.6 0.5 convolution_convert_fusion
  143.1 0.8 broadcast_in_dim.53
  143.9 5.1 %all-to-all-start = ((bf16[8,4,128,48]{2,3,1,0:T(8,128)(2,1)}), bf16[8,4,128,48]{2,3,1,0:T(8,128)(2,1)S(1)}, u32[]{:S(2)}, u32[]{:S(2)}) async-start(bf16[8,4,128,48]{2,3,1,0:T(8,128)(2,1)} %broadcast_in_dim.53), calls=%async_computation | async-start | bytes 786432 | tf_op jit(solution)/shard_map/all_to_all | solution.py:51
  149.0 0.7 fusion.80
  149.7 0.6 copy.111
  150.3 6.4 %all-to-all-done = bf16[8,4,128,48]{2,3,1,0:T(8,128)(2,1)S(1)} async-done(((bf16[8,4,128,48]{2,3,1,0:T(8,128)(2,1)}), bf16[8,4,128,48]{2,3,1,0:T(8,128)(2,1)S(1)}, u32[]{:S(2)}, u32[]{:S(2)}) %all-to-all-start) | async-done | bytes 393248 | tf_op jit(solution)/shard_map/all_to_all | solution.py:51
  156.7 1.6 fusion.19
  158.3 0.4 reshape.510
  158.7 0.6 fusion.79
  159.3 0.3 subtract_convert_fusion
  159.6 0.3 pad_maximum_fusion
  160.0 2.7 %fusion.3 = (f32[2,128,4]{1,2,0:T(4,128)S(1)}, f32[2,128,4,2048]{3,1,2,0:T(8,128)S(1)}) fusion(pred[2,2048]{1,0:T(4,128)(4,1)S(1)} %copy-done.7, bf16[2,2048,1,256]{3,1,0,2:T(8,128)(2,1)} %bitcast.166, bf16[4,128,1,4,128]{4,1,3,0,2:T(8,128)(2,1)S(1)} %pad_maximum_fusion), kind=kOutput, calls=%fused_computation.9 | convolution fusion | flops 543161344 | bytes 9711616 | tf_op jit(solution)/shard_map/bsvgd,bkvd->bvsgk/dot_general | solution.py:32
  162.6 2.3 fusion.21
  164.9 2.2 fusion.9
  167.2 0.2 fusion.24
  167.4 0.6 fusion.60
  168.1 0.5 fusion.81
  168.6 0.2 fusion.29
  168.9 1.1 bitcast_multiply_fusion
  169.9 1.9 fusion.20
  171.9 0.3 copy.78
  172.2 1.0 reshape.550
  173.2 10.3 %convert_bitcast_fusion = bf16[8,512,896]{2,1,0:T(8,128)(2,1)} fusion(bf16[512,512,1]{1,0,2:T(8,128)(2,1)} %reshape.550, bf16[64,8,8,896]{3,2,1,0:T(8,128)(2,1)} %bitcast.200), kind=kOutput, calls=%fused_computation.13 | convolution fusion | flops 3761766400 | bytes 15204352 | tf_op jit(solution)/shard_map/sc,ctf->tsf/dot_general | solution.py:200
  183.5 0.8 copy-done.5
  184.3 0.2 convolution_convert_fusion.1
  184.5 0.7 broadcast_in_dim.100
  185.2 4.5 %all-to-all-start.2 = ((bf16[8,4,128,16]{2,3,1,0:T(8,128)(2,1)}), bf16[8,4,128,16]{2,3,1,0:T(8,128)(2,1)S(1)}, u32[]{:S(2)}, u32[]{:S(2)}) async-start(bf16[8,4,128,16]{2,3,1,0:T(8,128)(2,1)} %broadcast_in_dim.100), calls=%async_computation.3 | async-start | bytes 262144 | tf_op jit(solution)/shard_map/all_to_all | solution.py:51
  189.7 5.8 %all-to-all-done.2 = bf16[8,4,128,16]{2,3,1,0:T(8,128)(2,1)S(1)} async-done(((bf16[8,4,128,16]{2,3,1,0:T(8,128)(2,1)}), bf16[8,4,128,16]{2,3,1,0:T(8,128)(2,1)S(1)}, u32[]{:S(2)}, u32[]{:S(2)}) %all-to-all-start.2) | async-done | bytes 131104 | tf_op jit(solution)/shard_map/all_to_all | solution.py:51
  195.6 1.8 convolution_multiply_fusion
  197.4 32.3 %reduce-scatter.2.cloned.1.call-done = bf16[1,512,896]{2,1,0:T(8,128)(2,1)} async-done(((bf16[8,512,896]{2,1,0:T(8,128)(2,1)}), bf16[1,512,896]{2,1,0:T(8,128)(2,1)}) %reduce-scatter.2.cloned.1.call-update) | async-done | bytes 917520 | tf_op jit(solution)/shard_map/reduce_scatter | solution.py:218
  229.7 2.8 %fusion.14 = bf16[512,896]{1,0:T(8,128)(2,1)} fusion(f32[4,128,896]{2,1,0:T(8,128)} %convolution_multiply_fusion, bf16[1,512,896]{2,1,0:T(8,128)(2,1)} %reduce-scatter.2.cloned.1.call-done), kind=kLoop, calls=%fused_computation.19 | loop fusion | flops 1376256 | bytes 3670016 | tf_op jit(solution)/shard_map/convert_element_type | solution.py:224
  (70 shorter events, 1.3 us)
Async XLA Ops:
  6.5 8.6 %copy-start = (bf16[32,128,256]{2,1,0:T(8,128)(2,1)S(1)}, bf16[32,128,256]{2,1,0:T(8,128)(2,1)}, u32[]{:S(2)}) copy-start(bf16[32,128,256]{2,1,0:T(8,128)(2,1)} %param.31) | copy-start | bytes 6291460
  6.5 55.1 %all-gather.3.cloned.1.call-start = ((), (), s32[]{:S(2)}) async-start(), calls=%async_computation.4 | async-start | bytes 8257536 | tf_op jit(solution)/shard_map/all_gather | solution.py:85
  7.3 130.4 %all-gather.5.cloned.1.call-start = ((), (), s32[]{:S(2)}) async-start(), calls=%async_computation.5 | async-start | bytes 10584064 | tf_op jit(solution)/shard_map/all_gather | solution.py:100
  12.2 16.9 %copy-start.15 = (s32[4]{0:T(128)S(1)}, s32[4]{0:T(128)}, u32[]{:S(2)}) copy-start(s32[4]{0:T(128)} %param.26) | copy-start | bytes 52
  12.2 17.0 %copy-start.16 = (s32[32]{0:T(128)S(1)}, s32[32]{0:T(128)}, u32[]{:S(2)}) copy-start(s32[32]{0:T(128)} %param.28) | copy-start | bytes 388
  12.2 17.1 %copy-start.17 = (s32[32]{0:T(128)S(1)}, s32[32]{0:T(128)}, u32[]{:S(2)}) copy-start(s32[32]{0:T(128)} %param.29) | copy-start | bytes 388
  12.2 17.5 %copy-start.18 = (s32[4]{0:T(128)S(1)}, s32[4]{0:T(128)}, u32[]{:S(2)}) copy-start(s32[4]{0:T(128)} %param.27) | copy-start | bytes 52
  20.4 46.0 %copy-start.9 = (f32[7168]{0:T(1024)S(1)}, f32[7168]{0:T(1024)}, u32[]{:S(2)}) copy-start(f32[7168]{0:T(1024)} %param.17) | copy-start | bytes 86020
  20.4 39.7 %all-to-all-start.1 = ((bf16[2,16,128,256]{3,2,0,1:T(8,128)(2,1)}), bf16[2,16,128,256]{3,2,0,1:T(8,128)(2,1)S(1)}, u32[]{:S(2)}, u32[]{:S(2)}) async-start(bf16[2,16,128,256]{3,2,0,1:T(8,128)(2,1)} %copy.73), calls=%async_computation.1 | async-start | bytes 4194304 | tf_op jit(solution)/shard_map/all_to_all | solution.py:168
  29.1 32.5 %copy-start.12 = (f32[64]{0:T(128)}, f32[64]{0:T(128)S(1)}, u32[]{:S(2)}) copy-start(f32[64]{0:T(128)S(1)} %multiply_power_fusion) | copy-start | bytes 772
  29.7 42.8 %copy-start.14 = (pred[4,128]{1,0:T(4,128)(4,1)}, pred[4,128]{1,0:T(4,128)(4,1)S(1)}, u32[]{:S(2)}) copy-start(pred[4,128]{1,0:T(4,128)(4,1)S(1)} %iota_compare_fusion.1) | copy-start | bytes 1540
  29.9 42.7 %copy-start.10 = (f32[4,128]{1,0:T(4,128)}, f32[4,128]{1,0:T(4,128)S(1)}, u32[]{:S(2)}) copy-start(f32[4,128]{1,0:T(4,128)S(1)} %add_convert_fusion.1) | copy-start | bytes 6148
  61.6 5.2 %copy-start.2 = (bf16[512,7168]{1,0:T(8,128)(2,1)S(1)}, bf16[512,7168]{1,0:T(8,128)(2,1)}, u32[]{:S(2)}) copy-start(bf16[512,7168]{1,0:T(8,128)(2,1)} %all-gather.3.cloned.1.call-done) | copy-start | bytes 22020100
  78.8 11.7 %copy-start.6 = (f32[512,256]{1,0:T(8,128)}, f32[512,256]{1,0:T(8,128)S(1)}, u32[]{:S(2)}) copy-start(f32[512,256]{1,0:T(8,128)S(1)} %fusion.83) | copy-start | bytes 1572868
  143.9 12.8 %all-to-all-start = ((bf16[8,4,128,48]{2,3,1,0:T(8,128)(2,1)}), bf16[8,4,128,48]{2,3,1,0:T(8,128)(2,1)S(1)}, u32[]{:S(2)}, u32[]{:S(2)}) async-start(bf16[8,4,128,48]{2,3,1,0:T(8,128)(2,1)} %broadcast_in_dim.53), calls=%async_computation | async-start | bytes 786432 | tf_op jit(solution)/shard_map/all_to_all | solution.py:51
  149.0 80.7 %reduce-scatter.2.cloned.1.call-start = ((), (), s32[]{:S(2)}) async-start(), calls=%async_computation.6 | async-start | bytes 8257536 | tf_op jit(solution)/shard_map/reduce_scatter | solution.py:218
  158.7 1.3 copy-start.7
  159.3 3.3 %copy-start.3 = (bf16[2,16,128,256]{3,2,1,0:T(8,128)(2,1)S(1)}, bf16[2,16,128,256]{3,2,1,0:T(8,128)(2,1)}, u32[]{:S(2)}) copy-start(bf16[2,16,128,256]{3,2,1,0:T(8,128)(2,1)} %copy.74) | copy-start | bytes 6291460
  164.9 2.2 copy-start.8
  164.9 2.5 %copy-start.11 = (f32[4,128]{1,0:T(4,128)S(1)}, f32[4,128]{1,0:T(4,128)}, u32[]{:S(2)}) copy-start(f32[4,128]{1,0:T(4,128)} %copy-done.10) | copy-start | bytes 6148
  164.9 2.5 %copy-start.13 = (f32[64]{0:T(128)S(1)}, f32[64]{0:T(128)}, u32[]{:S(2)}) copy-start(f32[64]{0:T(128)} %copy-done.12) | copy-start | bytes 772
  164.9 3.1 %copy-start.4 = (pred[4,128,128]{1,2,0:T(8,128)(4,1)S(1)}, pred[4,128,128]{1,2,0:T(8,128)(4,1)}, u32[]{:S(2)}) copy-start(pred[4,128,128]{1,2,0:T(8,128)(4,1)} %broadcast_and_fusion) | copy-start | bytes 196612
  173.2 59.3 %copy-start.1 = (bf16[32,128,256]{2,1,0:T(8,128)(2,1)S(1)}, bf16[32,128,256]{2,1,0:T(8,128)(2,1)}, u32[]{:S(2)}) copy-start(bf16[32,128,256]{2,1,0:T(8,128)(2,1)} %param.31) | copy-start | bytes 6291460
  183.5 0.8 copy-start.5
  185.2 10.4 %all-to-all-start.2 = ((bf16[8,4,128,16]{2,3,1,0:T(8,128)(2,1)}), bf16[8,4,128,16]{2,3,1,0:T(8,128)(2,1)S(1)}, u32[]{:S(2)}, u32[]{:S(2)}) async-start(bf16[8,4,128,16]{2,3,1,0:T(8,128)(2,1)} %broadcast_in_dim.100), calls=%async_computation.3 | async-start | bytes 262144 | tf_op jit(solution)/shard_map/all_to_all | solution.py:51
Sparse Core Ops, SparseCore 0:
  9.0 48.7 all-gather.2
  60.0 77.6 all-gather.4
  183.6 45.9 reduce-scatter.1

commit v4 on v3

--- a/solution.py
+++ b/solution.py
@@ -83,35 +83,39 @@
     page_rows = cache_page_pool.shape[1]
     tensor_count = lax.axis_size("tensor")
     gathered = lax.all_gather(residual_input, "tensor", axis=1, tiled=True)
+    local_adapters = adapter_down_maps.shape[0]
+
+    def pick_adapters(parts, by_exchange):
+        flat_parts = [part.reshape(local_adapters, -1) for part in parts]
+        joined = jnp.concatenate(flat_parts, axis=1)
+        joined = joined.reshape(local_adapters, joined.shape[1] // 128, 128)
+        if by_exchange:
+            every_adapter = gather_by_exchange(joined, "req", holders).reshape(
+                (holders * local_adapters,) + joined.shape[1:]
+            )
+        else:
+            every_adapter = lax.all_gather(joined, "req", axis=0, tiled=True)
+        picked = jnp.take(every_adapter, request_adapter, axis=0, mode="clip").reshape(
+            request_number, -1
+        )
+        picked_parts = []
+        start = 0
+        for part, flat in zip(parts, flat_parts):
+            width = flat.shape[1]
+            picked_parts.append(
+                picked[:, start : start + width].reshape((request_number,) + part.shape[1:])
+            )
+            start += width
+        return picked_parts
+
+    query_picked, key_value_picked, output_down_picked, oup_sel = pick_adapters(
+        (adapter_query_up, adapter_key_value_up, adapter_output_down, adapter_output_up), True
+    )
+    gathered, held_down = lax.optimization_barrier((gathered, adapter_down_maps))
+    (down_picked,) = pick_adapters((held_down,), False)
     widened = gathered.astype(jnp.float32)
     inverse = lax.rsqrt(jnp.mean(widened * widened, axis=1, keepdims=True) + EPSILON)
     normed = (widened * inverse * input_norm_gain).astype(jnp.bfloat16)
-    adapter_parts = (
-        adapter_down_maps,
-        adapter_query_up,
-        adapter_key_value_up,
-        adapter_output_down,
-        adapter_output_up,
-    )
-    local_adapters = adapter_down_maps.shape[0]
-    flat_parts = [part.reshape(local_adapters, -1) for part in adapter_parts]
-    joined = jnp.concatenate(flat_parts, axis=1)
-    lane_rows = joined.shape[1] // 128
-    every_adapter = lax.all_gather(
-        joined.reshape(local_adapters, lane_rows, 128), "req", axis=0, tiled=True
-    )
-    picked = jnp.take(every_adapter, request_adapter, axis=0, mode="clip").reshape(
-        request_number, -1
-    )
-    picked_parts = []
-    start = 0
-    for part, flat in zip(adapter_parts, flat_parts):
-        width = flat.shape[1]
-        picked_parts.append(
-            picked[:, start : start + width].reshape((request_number,) + part.shape[1:])
-        )
-        start += width
-    down_picked, query_picked, key_value_picked, output_down_picked, oup_sel = picked_parts
     adapter_rank_size = query_picked.shape[1]
     own_columns = lax.dynamic_slice_in_dim(
         normed, tensor_index * piece_width, piece_width, 1

time: 240 us -> 269 us (1.12)
  waiting for transfers between devices: 120 us -> 144 us
  starting transfers between devices: 18.3 us -> 26.6 us
  matrix products: 38.3 us -> 34.9 us
    all_to_all x2 -> x3, waiting for transfers between devices: 12.3 us -> 76.3 us  [gather_by_exchange(): lax.all_to_all(spread, axis_name, split_axis=0, concat_axis=0, tiled=True)]
    all_gather x1, waiting for transfers between devices: 47.2 us -> 0.01 us  [pick_adapters(): every_adapter = lax.all_gather(joined, 'req', axis=0, tiled=True)]
    all_gather x1, waiting for transfers between devices: 0.01 us -> 34.6 us  [local(): gathered = lax.all_gather(residual_input, 'tensor', axis=1, tiled=True)]
    all_to_all x1, waiting for transfers between devices: 27.7 us -> 0.01 us  [local(): lax.all_to_all(outgoing, 'req', split_axis=1, concat_axis=1, tiled=True)]
    all_to_all x2 -> x3, starting transfers between devices: 9.59 us -> 18 us  [gather_by_exchange(): lax.all_to_all(spread, axis_name, split_axis=0, concat_axis=0, tiled=True)]
    unnamed x54 -> x60, local copies, waits for them, and re-layouts: 8.75 us -> 4.72 us
    dot_general x1, matrix products: 10.2 us -> 7.2 us  [local(): jnp.dot(normed, query_weight, preferred_element_type=jnp.float32)]
    broadcast_in_dim x2 -> x3, local copies, waits for them, and re-layouts: 1.48 us -> 4.42 us  [gather_by_exchange(): spread = jnp.broadcast_to(piece[None], (count,) + piece.shape)]
  transfers between devices with their start and end apart: 6 -> 7, of which waited for: 5 -> 5; matrix products, arithmetic and copies ran while one was open for 21% -> 18% of each run, Pallas kernels for 0% -> 0%
where the time goes in v4:
time: 269 us; the launch traced here: 268 us
  waiting for transfers between devices  144 us (54%)
  matrix products  34.9 us (13%)
  starting transfers between devices  26.6 us (10%)
  local copies, waits for them, and re-layouts  26.4 us (10%)
  other arithmetic  21.8 us (8%)
  between operations  13.7 us (5%)
    all_to_all x3, waiting for transfers between devices, gather_by_exchange(): lax.all_to_all(spread, axis_name, split_axis=0, concat_axis=0, tiled=True)  76.3 us
    all_gather x1, waiting for transfers between devices, local(): gathered = lax.all_gather(residual_input, 'tensor', axis=1, tiled=True)  34.6 us
    reduce_scatter x1, waiting for transfers between devices, local(): lax.psum_scatter(head_terms.astype(jnp.bfloat16), 'tensor', scatter_dimen...  32.5 us
    all_to_all x3, starting transfers between devices, gather_by_exchange(): lax.all_to_all(spread, axis_name, split_axis=0, concat_axis=0, tiled=True)  18 us
    dot_general x1, matrix products, local(): jnp.einsum('sc,ctf->tsf', attended, output_weight.reshape(output_weight.s...  9.25 us
    all_to_all x1, starting transfers between devices, local(): lax.all_to_all(outgoing, 'req', split_axis=1, concat_axis=1, tiled=True)  8.59 us
    dot_general x1, matrix products, local(): jnp.dot(normed, query_weight, preferred_element_type=jnp.float32)  7.2 us
    dot_general x1, matrix products, local(): jnp.dot(normed, key_value_weight, preferred_element_type=jnp.float32)  6.21 us
  transfers between devices with their start and end apart: 7, of which 5 were waited for; matrix products, arithmetic and copies ran while one was open for 18% of the time, Pallas kernels for 0%

profile of v4, /device:TPU:1, one launch (start us, length us, event | category | flops | bytes accessed | tf_op | source)
XLA Modules:
  0.0 267.6 jit_solution(96260062266704949)
XLA Ops:
  6.6 0.7 all-gather.3.cloned.1.call-update
  7.3 0.5 broadcast.286
  7.8 1.3 reduce.13
  9.1 0.1 reshape_squeeze.3
  9.2 0.1 copy.72
  9.3 0.1 reshape.510
  9.4 2.1 gather_fusion.2
  11.5 3.1 %copy.73 = bf16[2,16,128,256]{3,2,0,1:T(8,128)(2,1)} copy(bf16[2,16,128,256]{3,2,1,0:T(8,128)(2,1)} %bitcast.163) | data formatting | bytes 4194304 | tf_op jit(solution)/shard_map/reshape | solution.py:169
  14.6 8.6 %all-to-all-start.2 = ((bf16[2,16,128,256]{3,2,0,1:T(8,128)(2,1)}), bf16[2,16,128,256]{3,2,0,1:T(8,128)(2,1)S(1)}, u32[]{:S(2)}, u32[]{:S(2)}) async-start(bf16[2,16,128,256]{3,2,0,1:T(8,128)(2,1)} %copy.73), calls=%async_computation.2 | async-start | bytes 4194304 | tf_op jit(solution)/shard_map/all_to_all | solution.py:172
  23.3 34.6 %all-gather.3.cloned.1.call-done = bf16[512,7168]{1,0:T(8,128)(2,1)} async-done(((bf16[512,896]{1,0:T(8,128)(2,1)}), bf16[512,7168]{1,0:T(8,128)(2,1)}) %all-gather.3.cloned.1.call-update) | async-done | bytes 7340048 | tf_op jit(solution)/shard_map/all_gather | solution.py:85
  57.9 1.1 reshape_reshape.6
  59.3 0.1 maximum_bitcast_fusion
  59.5 2.9 %broadcast_in_dim.65 = bf16[16,4,272,128]{3,2,1,0:T(8,128)(2,1)} broadcast(bf16[4,272,128]{2,1,0:T(8,128)(2,1)S(1)} %bitcast.170), dimensions={1,2,3} | broadcast | bytes 4734976 | tf_op jit(solution)/shard_map/broadcast_in_dim | solution.py:50
  62.4 6.7 %all-to-all-start.1 = ((bf16[16,4,272,128]{3,2,1,0:T(8,128)(2,1)}), bf16[16,4,272,128]{3,2,1,0:T(8,128)(2,1)}, u32[]{:S(2)}, u32[]{:S(2)}) async-start(bf16[16,4,272,128]{3,2,1,0:T(8,128)(2,1)} %broadcast_in_dim.65), calls=%async_computation.1 | async-start | bytes 8912896 | tf_op jit(solution)/shard_map/all_to_all | solution.py:51
  69.2 0.1 dynamic_slice.11
  69.4 0.1 copy.98
  69.6 0.1 add.130
  69.8 0.1 fusion.67
  70.0 0.1 broadcast_and_fusion
  70.2 1.0 multiply_cosine_fusion
  71.2 0.7 fusion.59
  71.9 1.6 copy.74
  73.4 69.3 %all-to-all-done.1 = bf16[16,4,272,128]{3,2,1,0:T(8,128)(2,1)} async-done(((bf16[16,4,272,128]{3,2,1,0:T(8,128)(2,1)}), bf16[16,4,272,128]{3,2,1,0:T(8,128)(2,1)}, u32[]{:S(2)}, u32[]{:S(2)}) %all-to-all-start.1) | async-done | bytes 4456480 | tf_op jit(solution)/shard_map/all_to_all | solution.py:51
  142.8 2.9 %gather_fusion.1 = bf16[4,272,128]{2,1,0:T(8,128)(2,1)S(1)} fusion(bf16[64,272,128]{2,1,0:T(8,128)(2,1)} %bitcast.2, s32[1024]{0:T(1024)S(1)} %pad_clamp_fusion.1), kind=kCustom, calls=%fused_computation.1 | custom fusion | bytes 557072 | tf_op jit(solution)/shard_map/jit(_take)/gather | solution.py:98
  145.6 0.1 copy.139
  145.8 0.6 copy.109
  146.4 0.7 fusion.78
  147.1 4.8 %fusion = f32[512]{0:T(512)S(1)} fusion(bf16[512,7168]{1,0:T(8,128)(2,1)} %all-gather.3.cloned.1.call-done), kind=kLoop, calls=%fused_computation.5 | loop fusion | flops 11009536 | bytes 7342080 | tf_op jit(solution)/shard_map/reduce_sum | solution.py:117
  151.8 5.9 %fusion.2 = bf16[512,7168]{1,0:T(8,128)(2,1)S(1)} fusion(bf16[512,7168]{1,0:T(8,128)(2,1)} %all-gather.3.cloned.1.call-done, f32[7168]{0:T(1024)S(1)} %copy-done.14, f32[512]{0:T(512)S(1)} %add_rsqrt_fusion), kind=kLoop, calls=%fused_computation.7 | loop fusion | flops 14680064 | bytes 14710784 | tf_op jit(solution)/shard_map/convert_element_type | solution.py:118
  157.8 0.1 constant_dynamic-slice_fusion
  157.8 2.9 %copy-done.2 = bf16[512,7168]{1,0:T(8,128)(2,1)} copy-done((bf16[512,7168]{1,0:T(8,128)(2,1)}, bf16[512,7168]{1,0:T(8,128)(2,1)S(1)}, u32[]{:S(2)}) %copy-start.2) | copy-done | bytes 7340056
  160.7 7.2 %fusion.80 = f32[512,512]{1,0:T(8,128)} fusion(bf16[512,7168]{1,0:T(8,128)(2,1)S(1)} %fusion.2, bf16[7168,512]{1,0:T(8,128)(2,1)} %param.18), kind=kOutput, calls=%fused_computation.126 | convolution fusion | flops 3758096384 | bytes 15728640 | tf_op jit(solution)/shard_map/dot_general | solution.py:132
  167.9 3.2 %gather_fusion = bf16[4,336,128]{2,1,0:T(8,128)(2,1)S(1)} fusion(bf16[64,336,128]{2,1,0:T(8,128)(2,1)} %all-gather.5.cloned.1.call-done, s32[1024]{0:T(1024)S(1)} %pad_clamp_fusion.1), kind=kCustom, calls=%fused_computation | custom fusion | bytes 688144 | tf_op jit(solution)/shard_map/jit(_take)/gather | solution.py:98
  171.1 0.4 reshape_reshape.7
  171.4 0.5 convolution_convert_fusion
  171.9 0.8 broadcast_in_dim.59
  172.7 6.7 %all-to-all-start = ((bf16[8,4,128,48]{2,3,1,0:T(8,128)(2,1)}), bf16[8,4,128,48]{2,3,1,0:T(8,128)(2,1)S(1)}, u32[]{:S(2)}, u32[]{:S(2)}) async-start(bf16[8,4,128,48]{2,3,1,0:T(8,128)(2,1)} %broadcast_in_dim.59), calls=%async_computation | async-start | bytes 786432 | tf_op jit(solution)/shard_map/all_to_all | solution.py:51
  179.5 6.2 %fusion.81 = f32[512,256]{1,0:T(8,128)S(1)} fusion(bf16[512,7168]{1,0:T(8,128)(2,1)} %copy-done.2, bf16[7168,256]{1,0:T(8,128)(2,1)} %param.19), kind=kOutput, calls=%fused_computation.127 | convolution fusion | flops 1879048192 | bytes 11534336 | tf_op jit(solution)/shard_map/dot_general | solution.py:139
  185.7 0.1 copy.95
  185.9 1.3 all-to-all-done
  187.3 1.6 fusion.19
  188.8 0.4 reshape.503
  189.2 0.6 fusion.77
  189.8 0.3 subtract_convert_fusion
  190.2 0.3 pad_maximum_fusion
  190.5 2.7 %fusion.3 = (f32[2,128,4]{1,2,0:T(4,128)S(1)}, f32[2,128,4,2048]{3,1,2,0:T(8,128)S(1)}) fusion(pred[2,2048]{1,0:T(4,128)(4,1)S(1)} %copy-done.8, bf16[2,2048,1,256]{3,1,0,2:T(8,128)(2,1)} %bitcast.164, bf16[4,128,1,4,128]{4,1,3,0,2:T(8,128)(2,1)S(1)} %pad_maximum_fusion), kind=kOutput, calls=%fused_computation.10 | convolution fusion | flops 543161344 | bytes 9711616 | tf_op jit(solution)/shard_map/bsvgd,bkvd->bvsgk/dot_general | solution.py:32
  193.2 2.3 fusion.21
  195.5 2.2 fusion.9
  197.7 1.0 fusion.24
  198.7 0.6 fusion.58
  199.3 0.5 fusion.79
  199.9 0.2 fusion.29
  200.1 1.1 bitcast_multiply_fusion
  201.2 1.9 fusion.20
  203.1 0.3 copy.78
  203.4 0.2 reshape.552
  203.6 9.3 %convert_bitcast_fusion = bf16[8,512,896]{2,1,0:T(8,128)(2,1)} fusion(bf16[512,512,1]{1,0,2:T(8,128)(2,1)S(1)} %reshape.552, bf16[64,8,8,896]{3,2,1,0:T(8,128)(2,1)} %bitcast.194), kind=kOutput, calls=%fused_computation.14 | convolution fusion | flops 3761766400 | bytes 15204352 | tf_op jit(solution)/shard_map/sc,ctf->tsf/dot_general | solution.py:204
  212.9 0.2 convolution_convert_fusion.1
  213.1 0.7 broadcast_in_dim.111
  213.8 4.5 %all-to-all-start.3 = ((bf16[8,4,128,16]{2,3,1,0:T(8,128)(2,1)}), bf16[8,4,128,16]{2,3,1,0:T(8,128)(2,1)S(1)}, u32[]{:S(2)}, u32[]{:S(2)}) async-start(bf16[8,4,128,16]{2,3,1,0:T(8,128)(2,1)} %broadcast_in_dim.111), calls=%async_computation.4 | async-start | bytes 262144 | tf_op jit(solution)/shard_map/all_to_all | solution.py:51
  218.3 5.7 %all-to-all-done.3 = bf16[8,4,128,16]{2,3,1,0:T(8,128)(2,1)S(1)} async-done(((bf16[8,4,128,16]{2,3,1,0:T(8,128)(2,1)}), bf16[8,4,128,16]{2,3,1,0:T(8,128)(2,1)S(1)}, u32[]{:S(2)}, u32[]{:S(2)}) %all-to-all-start.3) | async-done | bytes 131104 | tf_op jit(solution)/shard_map/all_to_all | solution.py:51
  224.0 1.7 convolution_multiply_fusion
  225.8 32.5 %reduce-scatter.2.cloned.1.call-done = bf16[1,512,896]{2,1,0:T(8,128)(2,1)} async-done(((bf16[8,512,896]{2,1,0:T(8,128)(2,1)}), bf16[1,512,896]{2,1,0:T(8,128)(2,1)}) %reduce-scatter.2.cloned.1.call-update) | async-done | bytes 917520 | tf_op jit(solution)/shard_map/reduce_scatter | solution.py:222
  258.3 2.8 %fusion.14 = bf16[512,896]{1,0:T(8,128)(2,1)} fusion(f32[4,128,896]{2,1,0:T(8,128)} %convolution_multiply_fusion, bf16[1,512,896]{2,1,0:T(8,128)(2,1)} %reduce-scatter.2.cloned.1.call-done), kind=kLoop, calls=%fused_computation.20 | loop fusion | flops 1376256 | bytes 3670016 | tf_op jit(solution)/shard_map/convert_element_type | solution.py:228
  (81 shorter events, 1.2 us)
Async XLA Ops:
  6.5 2.9 %copy-start = (bf16[32,128,256]{2,1,0:T(8,128)(2,1)S(1)}, bf16[32,128,256]{2,1,0:T(8,128)(2,1)}, u32[]{:S(2)}) copy-start(bf16[32,128,256]{2,1,0:T(8,128)(2,1)} %param.31) | copy-start | bytes 6291460
  6.5 51.3 %copy-start.4 = (bf16[4,48,896]{2,1,0:T(8,128)(2,1)S(1)}, bf16[4,48,896]{2,1,0:T(8,128)(2,1)}, u32[]{:S(2)}) copy-start(bf16[4,48,896]{2,1,0:T(8,128)(2,1)} %param.21) | copy-start | bytes 1032196
  6.5 52.4 %copy-start.13 = (bf16[4,2,16,128]{3,2,1,0:T(8,128)(2,1)S(1)}, bf16[4,2,16,128]{3,2,1,0:T(8,128)(2,1)}, u32[]{:S(2)}) copy-start(bf16[4,2,16,128]{3,2,1,0:T(8,128)(2,1)} %param.23) | copy-start | bytes 98308
  6.5 52.5 %copy-start.11 = (bf16[4,16,512]{2,1,0:T(8,128)(2,1)S(1)}, bf16[4,16,512]{2,1,0:T(8,128)(2,1)}, u32[]{:S(2)}) copy-start(bf16[4,16,512]{2,1,0:T(8,128)(2,1)} %param.22) | copy-start | bytes 196612
  6.5 52.5 %copy-start.12 = (bf16[4,16,512]{2,1,0:T(8,128)(2,1)S(1)}, bf16[4,16,512]{2,1,0:T(8,128)(2,1)}, u32[]{:S(2)}) copy-start(bf16[4,16,512]{2,1,0:T(8,128)(2,1)} %param.24) | copy-start | bytes 196612
  6.5 52.6 %copy-start.9 = (bf16[4,16,896]{2,1,0:T(8,128)(2,1)S(1)}, bf16[4,16,896]{2,1,0:T(8,128)(2,1)}, u32[]{:S(2)}) copy-start(bf16[4,16,896]{2,1,0:T(8,128)(2,1)} %param.25) | copy-start | bytes 344068
  6.6 51.3 %all-gather.3.cloned.1.call-start = ((), (), s32[]{:S(2)}) async-start(), calls=%async_computation.5 | async-start | bytes 8257536 | tf_op jit(solution)/shard_map/all_gather | solution.py:85
  14.6 44.8 %all-to-all-start.2 = ((bf16[2,16,128,256]{3,2,0,1:T(8,128)(2,1)}), bf16[2,16,128,256]{3,2,0,1:T(8,128)(2,1)S(1)}, u32[]{:S(2)}, u32[]{:S(2)}) async-start(bf16[2,16,128,256]{3,2,0,1:T(8,128)(2,1)} %copy.73), calls=%async_computation.2 | async-start | bytes 4194304 | tf_op jit(solution)/shard_map/all_to_all | solution.py:172
  23.2 144.7 %all-gather.5.cloned.1.call-start = ((), (), s32[]{:S(2)}) async-start(), calls=%async_computation.6 | async-start | bytes 5849088 | tf_op jit(solution)/shard_map/all_gather | solution.py:97
  59.2 9.9 %copy-start.21 = (s32[32]{0:T(128)S(1)}, s32[32]{0:T(128)}, u32[]{:S(2)}) copy-start(s32[32]{0:T(128)} %param.29) | copy-start | bytes 388
  59.2 10.0 %copy-start.22 = (s32[32]{0:T(128)S(1)}, s32[32]{0:T(128)}, u32[]{:S(2)}) copy-start(s32[32]{0:T(128)} %param.28) | copy-start | bytes 388
  59.2 10.4 %copy-start.20 = (s32[4]{0:T(128)S(1)}, s32[4]{0:T(128)}, u32[]{:S(2)}) copy-start(s32[4]{0:T(128)} %param.26) | copy-start | bytes 52
  59.3 10.5 %copy-start.23 = (s32[4]{0:T(128)S(1)}, s32[4]{0:T(128)}, u32[]{:S(2)}) copy-start(s32[4]{0:T(128)} %param.27) | copy-start | bytes 52
  62.4 80.4 %all-to-all-start.1 = ((bf16[16,4,272,128]{3,2,1,0:T(8,128)(2,1)}), bf16[16,4,272,128]{3,2,1,0:T(8,128)(2,1)}, u32[]{:S(2)}, u32[]{:S(2)}) async-start(bf16[16,4,272,128]{3,2,1,0:T(8,128)(2,1)} %broadcast_in_dim.65), calls=%async_computation.1 | async-start | bytes 8912896 | tf_op jit(solution)/shard_map/all_to_all | solution.py:51
  69.2 82.7 %copy-start.14 = (f32[7168]{0:T(1024)S(1)}, f32[7168]{0:T(1024)}, u32[]{:S(2)}) copy-start(f32[7168]{0:T(1024)} %param.17) | copy-start | bytes 86020
  69.7 77.4 %copy-start.17 = (f32[64]{0:T(128)}, f32[64]{0:T(128)S(1)}, u32[]{:S(2)}) copy-start(f32[64]{0:T(128)S(1)} %multiply_power_fusion) | copy-start | bytes 772
  69.8 87.9 %copy-start.19 = (pred[4,128]{1,0:T(4,128)(4,1)}, pred[4,128]{1,0:T(4,128)(4,1)S(1)}, u32[]{:S(2)}) copy-start(pred[4,128]{1,0:T(4,128)(4,1)S(1)} %iota_compare_fusion.1) | copy-start | bytes 1540
  70.0 87.8 %copy-start.15 = (f32[4,128]{1,0:T(4,128)}, f32[4,128]{1,0:T(4,128)S(1)}, u32[]{:S(2)}) copy-start(f32[4,128]{1,0:T(4,128)S(1)} %add_convert_fusion.1) | copy-start | bytes 6148
  157.7 2.9 %copy-start.2 = (bf16[512,7168]{1,0:T(8,128)(2,1)}, bf16[512,7168]{1,0:T(8,128)(2,1)S(1)}, u32[]{:S(2)}) copy-start(bf16[512,7168]{1,0:T(8,128)(2,1)S(1)} %fusion.2) | copy-start | bytes 22020100
  172.7 14.5 %all-to-all-start = ((bf16[8,4,128,48]{2,3,1,0:T(8,128)(2,1)}), bf16[8,4,128,48]{2,3,1,0:T(8,128)(2,1)S(1)}, u32[]{:S(2)}, u32[]{:S(2)}) async-start(bf16[8,4,128,48]{2,3,1,0:T(8,128)(2,1)} %broadcast_in_dim.59), calls=%async_computation | async-start | bytes 786432 | tf_op jit(solution)/shard_map/all_to_all | solution.py:51
  179.5 7.8 %copy-start.5 = (bf16[4,8192]{1,0:T(4,128)(2,1)S(1)}, bf16[4,8192]{1,0:T(4,128)(2,1)}, u32[]{:S(2)}) copy-start(bf16[4,8192]{1,0:T(4,128)(2,1)} %get-tuple-element.17) | copy-start | bytes 196612
  179.5 78.8 %reduce-scatter.2.cloned.1.call-start = ((), (), s32[]{:S(2)}) async-start(), calls=%async_computation.7 | async-start | bytes 8257536 | tf_op jit(solution)/shard_map/reduce_scatter | solution.py:222
  185.7 1.6 copy-start.7
  185.9 4.6 %copy-start.8 = (pred[2,2048]{1,0:T(4,128)(4,1)S(1)}, pred[2,2048]{1,0:T(4,128)(4,1)}, u32[]{:S(2)}) copy-start(pred[2,2048]{1,0:T(4,128)(4,1)} %fusion.59) | copy-start | bytes 12292
  187.2 5.9 %copy-start.6 = (bf16[4,128,48]{1,2,0:T(8,128)(2,1)}, bf16[4,128,48]{1,2,0:T(8,128)(2,1)S(1)}, u32[]{:S(2)}) copy-start(bf16[4,128,48]{1,2,0:T(8,128)(2,1)S(1)} %reduce_sum.52) | copy-start | bytes 147460
  189.8 3.4 %copy-start.3 = (bf16[2,16,128,256]{3,2,1,0:T(8,128)(2,1)S(1)}, bf16[2,16,128,256]{3,2,1,0:T(8,128)(2,1)}, u32[]{:S(2)}) copy-start(bf16[2,16,128,256]{3,2,1,0:T(8,128)(2,1)} %copy.74) | copy-start | bytes 6291460
  195.5 2.2 copy-start.10
  195.5 3.2 %copy-start.16 = (f32[4,128]{1,0:T(4,128)S(1)}, f32[4,128]{1,0:T(4,128)}, u32[]{:S(2)}) copy-start(f32[4,128]{1,0:T(4,128)} %copy-done.15) | copy-start | bytes 6148
  195.5 3.2 %copy-start.18 = (f32[64]{0:T(128)S(1)}, f32[64]{0:T(128)}, u32[]{:S(2)}) copy-start(f32[64]{0:T(128)} %copy-done.17) | copy-start | bytes 772
  203.6 57.4 %copy-start.1 = (bf16[32,128,256]{2,1,0:T(8,128)(2,1)S(1)}, bf16[32,128,256]{2,1,0:T(8,128)(2,1)}, u32[]{:S(2)}) copy-start(bf16[32,128,256]{2,1,0:T(8,128)(2,1)} %param.31) | copy-start | bytes 6291460
  213.8 10.2 %all-to-all-start.3 = ((bf16[8,4,128,16]{2,3,1,0:T(8,128)(2,1)}), bf16[8,4,128,16]{2,3,1,0:T(8,128)(2,1)S(1)}, u32[]{:S(2)}, u32[]{:S(2)}) async-start(bf16[8,4,128,16]{2,3,1,0:T(8,128)(2,1)} %broadcast_in_dim.111), calls=%async_computation.4 | async-start | bytes 262144 | tf_op jit(solution)/shard_map/all_to_all | solution.py:51
Sparse Core Ops, SparseCore 0:
  9.1 48.7 all-gather.2
  60.0 103.7 all-gather.4
  213.0 45.1 reduce-scatter.1

commit v5 on v3

--- a/solution.py
+++ b/solution.py
@@ -82,10 +82,52 @@
     group_size = query_weight.shape[1] // (HEAD_SIZE * local_kv)
     page_rows = cache_page_pool.shape[1]
     tensor_count = lax.axis_size("tensor")
-    gathered = lax.all_gather(residual_input, "tensor", axis=1, tiled=True)
+    chip_count = tensor_count // 2
+    core = tensor_index % 2
+    chip = tensor_index // 2
+    swap = [(index, index ^ 1) for index in range(tensor_count)]
+    along = [
+        (2 * ((target // 2 - 1) % chip_count), target)
+        if target % 2 == 0
+        else (2 * ((target // 2 + 1) % chip_count) + 1, target)
+        for target in range(tensor_count)
+    ]
+    partner = lax.ppermute(residual_input, "tensor", swap)
+    pair = jnp.where(
+        core == 0,
+        jnp.concatenate([residual_input, partner], axis=1),
+        jnp.concatenate([partner, residual_input], axis=1),
+    )
+    beside = lax.ppermute(pair, "tensor", along)
+    relayed = lax.ppermute(
+        lax.dynamic_slice_in_dim(beside, core * piece_width, piece_width, 1), "tensor", along
+    )
+    held = jnp.concatenate([beside, relayed], axis=1)
+    mirrored = lax.ppermute(held, "tensor", swap)
+    pair_width = 2 * piece_width
+    minus_piece = jnp.where(core == 0, held[:, :pair_width], mirrored[:, :pair_width])
+    plus_piece = jnp.where(core == 0, mirrored[:, :pair_width], held[:, :pair_width])
+    opposite = jnp.where(
+        core == 0,
+        jnp.concatenate([held[:, pair_width:], mirrored[:, pair_width:]], axis=1),
+        jnp.concatenate([mirrored[:, pair_width:], held[:, pair_width:]], axis=1),
+    )
+    relative = jnp.stack([pair, plus_piece, opposite, minus_piece])
+    chip_order = (jnp.arange(chip_count, dtype=jnp.int32) - chip) % chip_count
+    gathered = jnp.take(relative, chip_order, axis=0)
     widened = gathered.astype(jnp.float32)
-    inverse = lax.rsqrt(jnp.mean(widened * widened, axis=1, keepdims=True) + EPSILON)
-    normed = (widened * inverse * input_norm_gain).astype(jnp.bfloat16)
+    inverse = lax.rsqrt(
+        jnp.sum(widened * widened, axis=(0, 2), keepdims=True) / (tensor_count * piece_width)
+        + EPSILON
+    )
+    normed_parts = (
+        widened * inverse * input_norm_gain.reshape(chip_count, 1, pair_width)
+    ).astype(jnp.bfloat16)
+    own_normed = (
+        residual_input.astype(jnp.float32)
+        * inverse[0]
+        * lax.dynamic_slice_in_dim(input_norm_gain, tensor_index * piece_width, piece_width, 0)
+    ).astype(jnp.bfloat16)
     adapter_parts = (
         adapter_down_maps,
         adapter_query_up,
@@ -113,9 +155,7 @@
         start += width
     down_picked, query_picked, key_value_picked, output_down_picked, oup_sel = picked_parts
     adapter_rank_size = query_picked.shape[1]
-    own_columns = lax.dynamic_slice_in_dim(
-        normed, tensor_index * piece_width, piece_width, 1
-    ).reshape(request_number, request_slot_rows, piece_width)
+    own_columns = own_normed.reshape(request_number, request_slot_rows, piece_width)
     partial_low = jnp.einsum(
         "rsd,rkd->rsk", own_columns, down_picked, preferred_element_type=jnp.float32
     )
@@ -125,14 +165,24 @@
         .sum(axis=0)
         .astype(jnp.bfloat16)
     )
-    query_rows = jnp.dot(normed, query_weight, preferred_element_type=jnp.float32).reshape(request_number, request_slot_rows, -1)
+    query_rows = jnp.einsum(
+        "csf,cfn->sn",
+        normed_parts,
+        query_weight.reshape(chip_count, pair_width, -1),
+        preferred_element_type=jnp.float32,
+    ).reshape(request_number, request_slot_rows, -1)
     query_rows = query_rows + ADAPTER_SCALE * jnp.einsum(
         "ibm,imf->ibf",
         reduced_input[..., :adapter_rank_size],
         query_picked,
         preferred_element_type=jnp.float32,
     )
-    keyval = jnp.dot(normed, key_value_weight, preferred_element_type=jnp.float32).reshape(
+    keyval = jnp.einsum(
+        "csf,cfn->sn",
+        normed_parts,
+        key_value_weight.reshape(chip_count, pair_width, -1),
+        preferred_element_type=jnp.float32,
+    ).reshape(
         request_number, request_slot_rows, local_kv, 2 * HEAD_SIZE
     )
     key_add = jnp.einsum(

time: 240 us -> 255 us (1.062)
  waiting for transfers between devices: 120 us -> 98.1 us
  other arithmetic: 22 us -> 41.5 us
  local copies, waits for them, and re-layouts: 26.6 us -> 43.7 us
  starting transfers between devices: 18.3 us -> 23.4 us
  matrix products: 38.3 us -> 33.4 us
    all_gather x1, waiting for transfers between devices: 47.2 us -> 0.01 us  [local(): lax.all_gather(joined.reshape(local_adapters, lane_rows, 128), 'req', axi...]
    ppermute x0 -> x4, waiting for transfers between devices: none -> 22.7 us  [the longest x1 20.5 us: local(): beside = lax.ppermute(pair, 'tensor', along)]
    another operation x1 -> x4, other arithmetic: 0.32 us -> 12 us  [the longest x2 6.03 us: local(): relative = jnp.stack([pair, plus_piece, opposite, minus_piece])]
    select_n x0 -> x4, other arithmetic: none -> 8.28 us  [the longest x2 6.38 us: local(): jnp.where(core == 0, jnp.concatenate([residual_input, partner], axis=1),...]
    gather x0 -> x1, local copies, waits for them, and re-layouts: none -> 7.19 us  [local(): gathered = jnp.take(relative, chip_order, axis=0)]
    ppermute x0 -> x4, starting transfers between devices: none -> 7.17 us  [the longest x1 3.12 us: local(): lax.ppermute(lax.dynamic_slice_in_dim(beside, core * piece_width, piece_w...]
    reshape x0 -> x1, local copies, waits for them, and re-layouts: none -> 5.96 us  [local(): key_value_weight.reshape(chip_count, pair_width, -1)]
    convert_element_type x1, other arithmetic: 5.77 us -> 0.29 us  [local(): own_normed = (residual_input.astype(jnp.float32) * inverse[0] * lax.dynam...]
  transfers between devices with their start and end apart: 6 -> 9, of which waited for: 5 -> 6; matrix products, arithmetic and copies ran while one was open for 21% -> 31% of each run, Pallas kernels for 0% -> 0%
where the time goes in v5:
time: 255 us; the launch traced here: 254 us
  waiting for transfers between devices  98.1 us (38%)
  local copies, waits for them, and re-layouts  43.7 us (17%)
  other arithmetic  41.5 us (16%)
  matrix products  33.4 us (13%)
  starting transfers between devices  23.4 us (9%)
  between operations  13.9 us (5%)
    all_to_all x1, waiting for transfers between devices, local(): lax.all_to_all(outgoing, 'req', split_axis=1, concat_axis=1, tiled=True)  32.6 us
    reduce_scatter x1, waiting for transfers between devices, local(): lax.psum_scatter(head_terms.astype(jnp.bfloat16), 'tensor', scatter_dimen...  30.2 us
    ppermute x1, waiting for transfers between devices, local(): beside = lax.ppermute(pair, 'tensor', along)  20.5 us
    all_to_all x2, waiting for transfers between devices, gather_by_exchange(): lax.all_to_all(spread, axis_name, split_axis=0, concat_axis=0, tiled=True)  12.5 us
    unnamed x65, local copies, waits for them, and re-layouts  9.92 us
    dot_general x1, matrix products, local(): jnp.einsum('sc,ctf->tsf', attended, output_weight.reshape(output_weight.s...  9.09 us
    all_to_all x2, starting transfers between devices, gather_by_exchange(): lax.all_to_all(spread, axis_name, split_axis=0, concat_axis=0, tiled=True)  8.47 us
    all_to_all x1, starting transfers between devices, local(): lax.all_to_all(outgoing, 'req', split_axis=1, concat_axis=1, tiled=True)  7.77 us
  transfers between devices with their start and end apart: 9, of which 6 were waited for; matrix products, arithmetic and copies ran while one was open for 31% of the time, Pallas kernels for 0%

profile of v5, /device:TPU:1, one launch (start us, length us, event | category | flops | bytes accessed | tf_op | source)
XLA Modules:
  0.0 254.0 jit_solution(12566833829800399434)
XLA Ops:
  6.5 1.0 copy.107
  7.6 0.9 copy.109
  8.5 0.9 copy.110
  9.4 1.1 copy.106
  10.7 0.8 bitcast_dynamic-update-slice_fusion
  11.6 0.9 copy.150
  12.6 1.5 collective-permute-start
  14.0 2.2 collective-permute-done
  16.3 3.2 %maximum_select_fusion.1 = bf16[512,1792]{1,0:T(8,128)(2,1)} fusion(bf16[512,896]{1,0:T(8,128)(2,1)} %collective-permute-done, bf16[512,896]{1,0:T(8,128)(2,1)S(1)} %copy-done.3, pred[]{:T(512)S(6)} %eq.6), kind=kLoop, calls=%fused_computation.25 | loop fusion | flops 8257536 | bytes 3670017 | tf_op jit(solution)/shard_map/jit(_where)/select_n | solution.py:96
  19.4 2.6 %collective-permute-start.1 = (bf16[512,1792]{1,0:T(8,128)(2,1)}, bf16[512,1792]{1,0:T(8,128)(2,1)}, u32[]{:S(2)}, u32[]{:S(2)}) collective-permute-start(bf16[512,1792]{1,0:T(8,128)(2,1)} %maximum_select_fusion.1), channel_id=1, source_target_pairs={{6,0},{3,1},{0,2},{5,3},{2,4},{7,5},{4,6},{1,7},{14,8},{11,9},{8,1... | collective-permute-start | bytes 5505032 | tf_op jit(solution)/shard_map/ppermute | solution.py:101
  22.0 20.5 %collective-permute-done.1 = bf16[512,1792]{1,0:T(8,128)(2,1)} collective-permute-done((bf16[512,1792]{1,0:T(8,128)(2,1)}, bf16[512,1792]{1,0:T(8,128)(2,1)}, u32[]{:S(2)}, u32[]{:S(2)}) %collective-permute-start.1) | collective-permute-done | bytes 1835040 | tf_op jit(solution)/shard_map/ppermute | solution.py:101
  42.5 2.2 constant_dynamic-slice_fusion
  44.7 3.1 %collective-permute-start.2 = (bf16[512,896]{1,0:T(8,128)(2,1)}, bf16[512,896]{1,0:T(8,128)(2,1)}, u32[]{:S(2)}, u32[]{:S(2)}) collective-permute-start(bf16[512,896]{1,0:T(8,128)(2,1)} %constant_dynamic-slice_fusion), channel_id=1, source_target_pairs={{6,0},{3,1},{0,2},{5,3},{2,4},{7,5},{4,6},{1,7},{14,8},{11,9},{8,1... | collective-permute-start | bytes 2752520 | tf_op jit(solution)/shard_map/ppermute | solution.py:102
  47.8 0.5 broadcast.418
  48.4 0.6 reduce.13
  49.3 0.6 pad_clamp_fusion
  49.9 2.0 gather_fusion.2
  51.9 3.1 %copy.77 = bf16[2,16,128,256]{3,2,0,1:T(8,128)(2,1)} copy(bf16[2,16,128,256]{3,2,1,0:T(8,128)(2,1)} %bitcast.196) | data formatting | bytes 4194304 | tf_op jit(solution)/shard_map/reshape | solution.py:215
  55.0 7.8 %all-to-all-start.1 = ((bf16[2,16,128,256]{3,2,0,1:T(8,128)(2,1)}), bf16[2,16,128,256]{3,2,0,1:T(8,128)(2,1)S(1)}, u32[]{:S(2)}, u32[]{:S(2)}) async-start(bf16[2,16,128,256]{3,2,0,1:T(8,128)(2,1)} %copy.77), calls=%async_computation.1 | async-start | bytes 4194304 | tf_op jit(solution)/shard_map/all_to_all | solution.py:218
  62.9 0.7 dynamic_slice.14
  63.5 3.6 %pad_maximum_fusion.1 = bf16[512,2688]{1,0:T(8,128)(2,1)} fusion(bf16[512,896]{1,0:T(8,128)(2,1)} %collective-permute-done.2, bf16[512,1792]{1,0:T(8,128)(2,1)} %collective-permute-done.1), kind=kLoop, calls=%fused_computation.23 | loop fusion | flops 5505024 | bytes 5505024 | tf_op jit(solution)/shard_map/concatenate | solution.py:105
  67.4 0.6 mul.219
  68.1 6.0 %copy.70 = bf16[4,1792,256]{1,2,0:T(8,128)(2,1)} copy(bf16[4,1792,256]{2,1,0:T(8,128)(2,1)} %bitcast.204) | data formatting | bytes 7340032 | tf_op jit(solution)/shard_map/reshape | solution.py:183
  74.1 0.6 compare_and_fusion
  74.7 0.6 pad_clamp_fusion.1
  76.0 0.8 broadcast_and_fusion
  76.7 1.0 multiply_cosine_fusion.1
  77.7 0.7 fusion.66
  78.5 3.2 %maximum_select_fusion = bf16[1,512,1792]{2,1,0:T(8,128)(2,1)} fusion(bf16[1,512,896]{2,1,0:T(8,128)(2,1)} %bitcast.1, bf16[1,512,896]{2,1,0:T(8,128)(2,1)S(1)} %bitcast.197, pred[]{:T(512)S(6)} %eq.6), kind=kLoop, calls=%fused_computation.24 | loop fusion | flops 8257536 | bytes 3670017 | tf_op jit(solution)/shard_map/jit(_where)/select_n | solution.py:96
  81.7 32.6 %all-to-all-done.1 = bf16[2,16,128,256]{3,2,0,1:T(8,128)(2,1)S(1)} async-done(((bf16[2,16,128,256]{3,2,0,1:T(8,128)(2,1)}), bf16[2,16,128,256]{3,2,0,1:T(8,128)(2,1)S(1)}, u32[]{:S(2)}, u32[]{:S(2)}) %all-to-all-start.1) | async-done | bytes 2097184 | tf_op jit(solution)/shard_map/all_to_all | solution.py:218
  114.3 1.7 copy.78
  115.9 1.3 slice_bitcast_fusion.4
  117.2 1.9 maximum_select_fusion.2
  119.1 2.4 select_bitcast_fusion.1
  121.7 3.6 %pad_maximum_fusion = bf16[4,512,1792]{2,1,0:T(8,128)(2,1)} fusion(bf16[1,512,1792]{2,1,0:T(8,128)(2,1)S(1)} %get-tuple-element.9, bf16[1,512,1792]{2,1,0:T(8,128)(2,1)S(1)} %maximum_select_fusion.2, bf16[1,512,1792]{2,1,0:T(8,128)(2,1)S(1)} %get-tuple-element.8, bf16[1,512,1792]{2,1,0:T(8,128)(2,1)S(1)} %copy-done.4), kind=kLoop, calls=%fused_computation.14 | loop fusion | flops 11010048 | bytes 14680064 | tf_op jit(solution)/shard_map/stack | solution.py:115
  125.3 7.2 %gather_fusion = bf16[4,512,1792]{2,1,0:T(8,128)(2,1)} fusion(bf16[4,512,1792]{2,1,0:T(8,128)(2,1)} %pad_maximum_fusion, s32[1024]{0:T(1024)} %get-tuple-element.25), kind=kCustom, calls=%fused_computation | custom fusion | bytes 14680080 | tf_op jit(solution)/shard_map/jit(_take)/gather | solution.py:117
  132.5 5.3 %fusion = f32[512]{0:T(512)S(1)} fusion(bf16[4,512,1792]{2,1,0:T(8,128)(2,1)} %gather_fusion, pred[4]{0:T(512)(128)(4,1)S(1)} %copy-done.15), kind=kLoop, calls=%fused_computation.5 | loop fusion | flops 14679552 | bytes 7342084 | tf_op jit(solution)/shard_map/reduce_sum | solution.py:120
  138.1 5.7 %fusion.2 = bf16[4,512,1792]{2,1,0:T(8,128)(2,1)} fusion(f32[4,1792]{1,0:T(4,128)S(1)} %copy-done.12, f32[512]{0:T(512)S(1)} %add_rsqrt_fusion, bf16[4,512,1792]{2,1,0:T(8,128)(2,1)S(1)} %copy-done.2, pred[4]{0:T(512)(128)(4,1)S(1)} %copy-done.15), kind=kLoop, calls=%fused_computation.7 | loop fusion | flops 18350080 | bytes 14710788 | tf_op jit(solution)/shard_map/convert.13
  143.8 7.2 %fusion.23 = f32[4,128,1,256]{3,1,0,2:T(8,128)} fusion(bf16[4,128,4,1792]{3,1,0,2:T(8,128)(2,1)} %bitcast.198, bf16[4,1792,256]{1,2,0:T(8,128)(2,1)} %copy.70), kind=kOutput, calls=%fused_computation.43 | convolution fusion | flops 1879048192 | bytes 11534336 | tf_op jit(solution)/shard_map/csf,cfn->sn/dot_general | solution.py:180
  150.9 7.1 %convolution_bitcast_fusion = f32[4,128,512]{2,1,0:T(8,128)} fusion(bf16[4,128,4,1792]{3,1,0,2:T(8,128)(2,1)S(1)} %bitcast.199, bf16[4,1792,512,1]{2,1,3,0:T(8,128)(2,1)} %bitcast.232), kind=kOutput, calls=%fused_computation.41 | convolution fusion | flops 3758096384 | bytes 15728640 | tf_op jit(solution)/shard_map/csf,cfn->sn/dot_general | solution.py:168
  158.0 4.6 %gather_fusion.1 = bf16[4,608,128]{2,1,0:T(8,128)(2,1)S(1)} fusion(bf16[64,608,128]{2,1,0:T(8,128)(2,1)} %all-gather.2.cloned.1.call-done, s32[1024]{0:T(1024)} %pad_clamp_fusion.1), kind=kCustom, calls=%fused_computation.1 | custom fusion | bytes 1245200 | tf_op jit(solution)/shard_map/jit(_take)/gather | solution.py:145
  163.1 0.5 convolution_convert_fusion
  163.6 0.8 broadcast_in_dim.106
  164.4 4.0 %all-to-all-start = ((bf16[8,4,128,48]{2,3,1,0:T(8,128)(2,1)}), bf16[8,4,128,48]{2,3,1,0:T(8,128)(2,1)S(1)}, u32[]{:S(2)}, u32[]{:S(2)}) async-start(bf16[8,4,128,48]{2,3,1,0:T(8,128)(2,1)} %broadcast_in_dim.106), calls=%async_computation | async-start | bytes 786432 | tf_op jit(solution)/shard_map/all_to_all | solution.py:51
  168.4 0.7 fusion.88
  169.1 0.6 copy.115
  169.7 6.4 %all-to-all-done = bf16[8,4,128,48]{2,3,1,0:T(8,128)(2,1)S(1)} async-done(((bf16[8,4,128,48]{2,3,1,0:T(8,128)(2,1)}), bf16[8,4,128,48]{2,3,1,0:T(8,128)(2,1)S(1)}, u32[]{:S(2)}, u32[]{:S(2)}) %all-to-all-start) | async-done | bytes 393248 | tf_op jit(solution)/shard_map/all_to_all | solution.py:51
  176.2 1.6 fusion.21
  178.1 0.6 fusion.87
  179.4 1.0 copy-done.6
  180.3 1.5 fusion.3
  181.8 2.3 fusion.26
  184.1 2.2 fusion.9
  186.6 1.2 fusion.59
  187.9 0.5 fusion.89
  188.8 1.5 fusion.22
  190.9 9.1 %convert_bitcast_fusion = bf16[8,512,896]{2,1,0:T(8,128)(2,1)} fusion(bf16[512,512,1]{1,0,2:T(8,128)(2,1)S(1)} %reshape.741, bf16[64,8,8,896]{3,2,1,0:T(8,128)(2,1)} %bitcast.233), kind=kOutput, calls=%fused_computation.15 | convolution fusion | flops 3761766400 | bytes 15204352 | tf_op jit(solution)/shard_map/sc,ctf->tsf/dot_general | solution.py:250
  200.0 0.8 copy-done.8
  201.0 0.7 broadcast_in_dim.112
  201.7 4.5 %all-to-all-start.2 = ((bf16[8,4,128,16]{2,3,1,0:T(8,128)(2,1)}), bf16[8,4,128,16]{2,3,1,0:T(8,128)(2,1)S(1)}, u32[]{:S(2)}, u32[]{:S(2)}) async-start(bf16[8,4,128,16]{2,3,1,0:T(8,128)(2,1)} %broadcast_in_dim.112), calls=%async_computation.3 | async-start | bytes 262144 | tf_op jit(solution)/shard_map/all_to_all | solution.py:51
  206.2 6.1 %all-to-all-done.2 = bf16[8,4,128,16]{2,3,1,0:T(8,128)(2,1)S(1)} async-done(((bf16[8,4,128,16]{2,3,1,0:T(8,128)(2,1)}), bf16[8,4,128,16]{2,3,1,0:T(8,128)(2,1)S(1)}, u32[]{:S(2)}, u32[]{:S(2)}) %all-to-all-start.2) | async-done | bytes 131104 | tf_op jit(solution)/shard_map/all_to_all | solution.py:51
  212.3 1.8 convolution_multiply_fusion
  214.1 30.2 %reduce-scatter.2.cloned.1.call-done = bf16[1,512,896]{2,1,0:T(8,128)(2,1)} async-done(((bf16[8,512,896]{2,1,0:T(8,128)(2,1)}), bf16[1,512,896]{2,1,0:T(8,128)(2,1)}) %reduce-scatter.2.cloned.1.call-update) | async-done | bytes 917520 | tf_op jit(solution)/shard_map/reduce_scatter | solution.py:268
  244.3 2.8 %fusion.16 = bf16[512,896]{1,0:T(8,128)(2,1)} fusion(f32[4,128,896]{2,1,0:T(8,128)} %convolution_multiply_fusion, bf16[1,512,896]{2,1,0:T(8,128)(2,1)} %reduce-scatter.2.cloned.1.call-done), kind=kLoop, calls=%fused_computation.28 | loop fusion | flops 1376256 | bytes 3670016 | tf_op jit(solution)/shard_map/convert_element_type | solution.py:274
  (99 shorter events, 5.2 us)
Async XLA Ops:
  6.5 43.3 %copy-start = (bf16[32,128,256]{2,1,0:T(8,128)(2,1)S(1)}, bf16[32,128,256]{2,1,0:T(8,128)(2,1)}, u32[]{:S(2)}) copy-start(bf16[32,128,256]{2,1,0:T(8,128)(2,1)} %param.31) | copy-start | bytes 6291460
  6.5 6.0 %copy-start.3 = (bf16[512,896]{1,0:T(8,128)(2,1)S(1)}, bf16[512,896]{1,0:T(8,128)(2,1)}, u32[]{:S(2)}) copy-start(bf16[512,896]{1,0:T(8,128)(2,1)} %param.16) | copy-start | bytes 2752516
  6.5 151.5 %all-gather.2.cloned.1.call-start = ((), (), s32[]{:S(2)}) async-start(), calls=%async_computation.4 | async-start | bytes 10584064 | tf_op jit(solution)/shard_map/all_gather | solution.py:142
  11.6 36.7 %copy-start.21 = (s32[1,32]{1,0:T(1,128)S(1)}, s32[1,32]{1,0:T(1,128)}, u32[]{:S(2)}) copy-start(s32[1,32]{1,0:T(1,128)} %param.30) | copy-start | bytes 388
  12.6 3.7 %collective-permute-start = (bf16[512,896]{1,0:T(8,128)(2,1)S(1)}, bf16[512,896]{1,0:T(8,128)(2,1)}, u32[]{:S(2)}, u32[]{:S(2)}) collective-permute-start(bf16[512,896]{1,0:T(8,128)(2,1)S(1)} %copy-done.3), channel_id=1, source_target_pairs={{0,1},{1,0},{2,3},{3,2},{4,5},{5,4},{6,7},{7,6},{8,9},{9,8},{10,11... | collective-permute-start | bytes 2752520 | tf_op jit(solution)/shard_map/ppermute | solution.py:95
  19.4 23.1 %collective-permute-start.1 = (bf16[512,1792]{1,0:T(8,128)(2,1)}, bf16[512,1792]{1,0:T(8,128)(2,1)}, u32[]{:S(2)}, u32[]{:S(2)}) collective-permute-start(bf16[512,1792]{1,0:T(8,128)(2,1)} %maximum_select_fusion.1), channel_id=1, source_target_pairs={{6,0},{3,1},{0,2},{5,3},{2,4},{7,5},{4,6},{1,7},{14,8},{11,9},{8,1... | collective-permute-start | bytes 5505032 | tf_op jit(solution)/shard_map/ppermute | solution.py:101
  44.7 18.8 %collective-permute-start.2 = (bf16[512,896]{1,0:T(8,128)(2,1)}, bf16[512,896]{1,0:T(8,128)(2,1)}, u32[]{:S(2)}, u32[]{:S(2)}) collective-permute-start(bf16[512,896]{1,0:T(8,128)(2,1)} %constant_dynamic-slice_fusion), channel_id=1, source_target_pairs={{6,0},{3,1},{0,2},{5,3},{2,4},{7,5},{4,6},{1,7},{14,8},{11,9},{8,1... | collective-permute-start | bytes 2752520 | tf_op jit(solution)/shard_map/ppermute | solution.py:102
  51.9 10.9 %copy-start.22 = (s32[32]{0:T(128)S(1)}, s32[32]{0:T(128)}, u32[]{:S(2)}) copy-start(s32[32]{0:T(128)} %param.29) | copy-start | bytes 388
  51.9 11.0 %copy-start.23 = (s32[32]{0:T(128)S(1)}, s32[32]{0:T(128)}, u32[]{:S(2)}) copy-start(s32[32]{0:T(128)} %param.28) | copy-start | bytes 388
  55.0 59.3 %all-to-all-start.1 = ((bf16[2,16,128,256]{3,2,0,1:T(8,128)(2,1)}), bf16[2,16,128,256]{3,2,0,1:T(8,128)(2,1)S(1)}, u32[]{:S(2)}, u32[]{:S(2)}) async-start(bf16[2,16,128,256]{3,2,0,1:T(8,128)(2,1)} %copy.77), calls=%async_computation.1 | async-start | bytes 4194304 | tf_op jit(solution)/shard_map/all_to_all | solution.py:218
  62.8 4.7 %copy-start.14 = (f32[7168]{0:T(1024)S(1)}, f32[7168]{0:T(1024)}, u32[]{:S(2)}) copy-start(f32[7168]{0:T(1024)} %param.17) | copy-start | bytes 86020
  67.1 48.8 %collective-permute-start.3 = (bf16[512,2688]{1,0:T(8,128)(2,1)}, bf16[512,2688]{1,0:T(8,128)(2,1)}, u32[]{:S(2)}, u32[]{:S(2)}) collective-permute-start(bf16[512,2688]{1,0:T(8,128)(2,1)} %pad_maximum_fusion.1), channel_id=1, source_target_pairs={{0,1},{1,0},{2,3},{3,2},{4,5},{5,4},{6,7},{7,6},{8,9},{9,8},{10,11... | collective-permute-start | bytes 8257544 | tf_op jit(solution)/shard_map/ppermute | solution.py:106
  68.1 6.6 %copy-start.20 = (s32[4]{0:T(128)S(1)}, s32[4]{0:T(128)}, u32[]{:S(2)}) copy-start(s32[4]{0:T(128)} %param.26) | copy-start | bytes 52
  68.1 7.2 %copy-start.24 = (s32[4]{0:T(128)S(1)}, s32[4]{0:T(128)}, u32[]{:S(2)}) copy-start(s32[4]{0:T(128)} %param.27) | copy-start | bytes 52
  75.4 0.6 copy-start.18
  75.4 1.3 copy-start.16
  119.1 2.6 %copy-start.4 = (bf16[1,512,1792]{2,1,0:T(8,128)(2,1)S(1)}, bf16[1,512,1792]{2,1,0:T(8,128)(2,1)}, u32[]{:S(2)}) copy-start(bf16[1,512,1792]{2,1,0:T(8,128)(2,1)} %maximum_select_fusion) | copy-start | bytes 5505028
  125.3 7.2 %copy-start.15 = (pred[4]{0:T(512)(128)(4,1)S(1)}, pred[4]{0:T(512)(128)(4,1)}, u32[]{:S(2)}) copy-start(pred[4]{0:T(512)(128)(4,1)} %compare_and_fusion) | copy-start | bytes 16
  132.5 5.6 %copy-start.2 = (bf16[4,512,1792]{2,1,0:T(8,128)(2,1)S(1)}, bf16[4,512,1792]{2,1,0:T(8,128)(2,1)}, u32[]{:S(2)}) copy-start(bf16[4,512,1792]{2,1,0:T(8,128)(2,1)} %gather_fusion) | copy-start | bytes 22020100
  132.5 5.6 %copy-start.12 = (f32[4,1792]{1,0:T(4,128)S(1)}, f32[4,1792]{1,0:T(4,128)}, u32[]{:S(2)}) copy-start(f32[4,1792]{1,0:T(4,128)} %mul.219) | copy-start | bytes 86020
  143.8 7.2 %copy-start.5 = (bf16[4,512,1792]{2,1,0:T(8,128)(2,1)S(1)}, bf16[4,512,1792]{2,1,0:T(8,128)(2,1)}, u32[]{:S(2)}) copy-start(bf16[4,512,1792]{2,1,0:T(8,128)(2,1)} %fusion.2) | copy-start | bytes 22020100
  164.4 11.7 %all-to-all-start = ((bf16[8,4,128,48]{2,3,1,0:T(8,128)(2,1)}), bf16[8,4,128,48]{2,3,1,0:T(8,128)(2,1)S(1)}, u32[]{:S(2)}, u32[]{:S(2)}) async-start(bf16[8,4,128,48]{2,3,1,0:T(8,128)(2,1)} %broadcast_in_dim.106), calls=%async_computation | async-start | bytes 786432 | tf_op jit(solution)/shard_map/all_to_all | solution.py:51
  168.4 76.0 %reduce-scatter.2.cloned.1.call-start = ((), (), s32[]{:S(2)}) async-start(), calls=%async_computation.5 | async-start | bytes 8257536 | tf_op jit(solution)/shard_map/reduce_scatter | solution.py:268
  176.2 2.6 %copy-start.9 = (bf16[4,128,48]{1,2,0:T(8,128)(2,1)}, bf16[4,128,48]{1,2,0:T(8,128)(2,1)S(1)}, u32[]{:S(2)}) copy-start(bf16[4,128,48]{1,2,0:T(8,128)(2,1)S(1)} %reduce_sum.52) | copy-start | bytes 147460
  178.7 1.6 copy-start.6
  184.1 2.3 copy-start.10
  184.1 2.3 copy-start.11
  184.1 2.2 copy-start.13
  184.1 2.5 copy-start.17
  184.1 3.8 %copy-start.7 = (pred[4,128,128]{1,2,0:T(8,128)(4,1)S(1)}, pred[4,128,128]{1,2,0:T(8,128)(4,1)}, u32[]{:S(2)}) copy-start(pred[4,128,128]{1,2,0:T(8,128)(4,1)} %broadcast_and_fusion) | copy-start | bytes 196612
  187.8 1.0 copy-start.19
  200.0 0.8 copy-start.8
  200.0 47.1 %copy-start.1 = (bf16[32,128,256]{2,1,0:T(8,128)(2,1)S(1)}, bf16[32,128,256]{2,1,0:T(8,128)(2,1)}, u32[]{:S(2)}) copy-start(bf16[32,128,256]{2,1,0:T(8,128)(2,1)} %param.31) | copy-start | bytes 6291460
  201.7 10.6 %all-to-all-start.2 = ((bf16[8,4,128,16]{2,3,1,0:T(8,128)(2,1)}), bf16[8,4,128,16]{2,3,1,0:T(8,128)(2,1)S(1)}, u32[]{:S(2)}, u32[]{:S(2)}) async-start(bf16[8,4,128,16]{2,3,1,0:T(8,128)(2,1)} %broadcast_in_dim.112), calls=%async_computation.3 | async-start | bytes 262144 | tf_op jit(solution)/shard_map/all_to_all | solution.py:51
Sparse Core Ops, SparseCore 0:
  12.7 103.5 all-gather.1
  200.1 44.1 reduce-scatter.1

commit v6 on v5

--- a/solution.py
+++ b/solution.py
@@ -142,6 +142,7 @@
     every_adapter = lax.all_gather(
         joined.reshape(local_adapters, lane_rows, 128), "req", axis=0, tiled=True
     )
+    every_adapter, cache_page_pool = lax.optimization_barrier((every_adapter, cache_page_pool))
     picked = jnp.take(every_adapter, request_adapter, axis=0, mode="clip").reshape(
         request_number, -1
     )

time: 255 us -> 248 us (0.973)
  waiting for transfers between devices: 98.1 us -> 87 us
  starting transfers between devices: 23.4 us -> 29.4 us
  other arithmetic: 41.5 us -> 38.6 us
    all_to_all x1, waiting for transfers between devices: 32.6 us -> 22.1 us  [local(): lax.all_to_all(outgoing, 'req', split_axis=1, concat_axis=1, tiled=True)]
    all_to_all x2, waiting for transfers between devices: 12.5 us -> 7.73 us  [gather_by_exchange(): lax.all_to_all(spread, axis_name, split_axis=0, concat_axis=0, tiled=True)]
    ppermute x1, starting transfers between devices: 0.01 us -> 3.55 us  [local(): mirrored = lax.ppermute(held, 'tensor', swap)]
    unnamed x65 -> x61, local copies, waits for them, and re-layouts: 9.92 us -> 10.7 us
  transfers between devices with their start and end apart: 9 -> 9, of which waited for: 6 -> 7; matrix products, arithmetic and copies ran while one was open for 31% -> 30% of each run, Pallas kernels for 0% -> 0%
where the time goes in v6:
time: 248 us; the launch traced here: 246 us
  waiting for transfers between devices  87 us (35%)
  local copies, waits for them, and re-layouts  43.2 us (17%)
  other arithmetic  38.6 us (16%)
  matrix products  34.4 us (14%)
  starting transfers between devices  29.4 us (12%)
  between operations  13.9 us (6%)
    reduce_scatter x1, waiting for transfers between devices, local(): lax.psum_scatter(head_terms.astype(jnp.bfloat16), 'tensor', scatter_dimen...  32 us
    all_to_all x1, waiting for transfers between devices, local(): lax.all_to_all(outgoing, 'req', split_axis=1, concat_axis=1, tiled=True)  22.1 us
    ppermute x1, waiting for transfers between devices, local(): beside = lax.ppermute(pair, 'tensor', along)  20.5 us
    unnamed x61, local copies, waits for them, and re-layouts  10.7 us
    all_to_all x2, starting transfers between devices, gather_by_exchange(): lax.all_to_all(spread, axis_name, split_axis=0, concat_axis=0, tiled=True)  10.4 us
    dot_general x1, matrix products, local(): jnp.einsum('sc,ctf->tsf', attended, output_weight.reshape(output_weight.s...  9.11 us
    all_to_all x1, starting transfers between devices, local(): lax.all_to_all(outgoing, 'req', split_axis=1, concat_axis=1, tiled=True)  7.94 us
    all_to_all x2, waiting for transfers between devices, gather_by_exchange(): lax.all_to_all(spread, axis_name, split_axis=0, concat_axis=0, tiled=True)  7.73 us
  transfers between devices with their start and end apart: 9, of which 7 were waited for; matrix products, arithmetic and copies ran while one was open for 30% of the time, Pallas kernels for 0%

profile of v6, /device:TPU:1, one launch (start us, length us, event | category | flops | bytes accessed | tf_op | source)
XLA Modules:
  0.0 246.5 jit_solution(1400931632566693605)
XLA Ops:
  6.5 1.0 copy.107
  7.6 0.9 copy.109
  8.5 0.9 copy.110
  9.4 1.1 copy.106
  10.7 0.8 bitcast_dynamic-update-slice_fusion
  11.7 0.9 copy.150
  12.6 1.5 collective-permute-start
  14.1 2.2 collective-permute-done
  16.3 3.3 %maximum_select_fusion.1 = bf16[512,1792]{1,0:T(8,128)(2,1)} fusion(bf16[512,896]{1,0:T(8,128)(2,1)} %collective-permute-done, bf16[512,896]{1,0:T(8,128)(2,1)S(1)} %copy-done.3, pred[]{:T(512)S(6)} %eq.6), kind=kLoop, calls=%fused_computation.25 | loop fusion | flops 8257536 | bytes 3670017 | tf_op jit(solution)/shard_map/jit(_where)/select_n | solution.py:96
  19.6 2.6 %collective-permute-start.1 = (bf16[512,1792]{1,0:T(8,128)(2,1)}, bf16[512,1792]{1,0:T(8,128)(2,1)}, u32[]{:S(2)}, u32[]{:S(2)}) collective-permute-start(bf16[512,1792]{1,0:T(8,128)(2,1)} %maximum_select_fusion.1), channel_id=1, source_target_pairs={{6,0},{3,1},{0,2},{5,3},{2,4},{7,5},{4,6},{1,7},{14,8},{11,9},{8,1... | collective-permute-start | bytes 5505032 | tf_op jit(solution)/shard_map/ppermute | solution.py:101
  22.2 20.5 %collective-permute-done.1 = bf16[512,1792]{1,0:T(8,128)(2,1)} collective-permute-done((bf16[512,1792]{1,0:T(8,128)(2,1)}, bf16[512,1792]{1,0:T(8,128)(2,1)}, u32[]{:S(2)}, u32[]{:S(2)}) %collective-permute-start.1) | collective-permute-done | bytes 1835040 | tf_op jit(solution)/shard_map/ppermute | solution.py:101
  42.7 2.2 constant_dynamic-slice_fusion
  44.8 3.1 %collective-permute-start.2 = (bf16[512,896]{1,0:T(8,128)(2,1)}, bf16[512,896]{1,0:T(8,128)(2,1)}, u32[]{:S(2)}, u32[]{:S(2)}) collective-permute-start(bf16[512,896]{1,0:T(8,128)(2,1)} %constant_dynamic-slice_fusion), channel_id=1, source_target_pairs={{6,0},{3,1},{0,2},{5,3},{2,4},{7,5},{4,6},{1,7},{14,8},{11,9},{8,1... | collective-permute-start | bytes 2752520 | tf_op jit(solution)/shard_map/ppermute | solution.py:102
  48.5 0.6 broadcast.418
  49.1 0.6 reduce.13
  50.0 6.1 %copy.70 = bf16[4,1792,256]{1,2,0:T(8,128)(2,1)} copy(bf16[4,1792,256]{2,1,0:T(8,128)(2,1)} %bitcast.204) | data formatting | bytes 7340032 | tf_op jit(solution)/shard_map/reshape | solution.py:184
  56.1 2.5 %collective-permute-done.2 = bf16[512,896]{1,0:T(8,128)(2,1)} collective-permute-done((bf16[512,896]{1,0:T(8,128)(2,1)}, bf16[512,896]{1,0:T(8,128)(2,1)}, u32[]{:S(2)}, u32[]{:S(2)}) %collective-permute-start.2) | collective-permute-done | bytes 917536 | tf_op jit(solution)/shard_map/ppermute | solution.py:102
  58.6 2.0 pad_maximum_fusion.1
  60.6 3.6 %collective-permute-start.3 = (bf16[512,2688]{1,0:T(8,128)(2,1)S(1)}, bf16[512,2688]{1,0:T(8,128)(2,1)S(1)}, u32[]{:S(2)}, u32[]{:S(2)}) collective-permute-start(bf16[512,2688]{1,0:T(8,128)(2,1)S(1)} %pad_maximum_fusion.1), channel_id=1, source_target_pairs={{0,1},{1,0},{2,3},{3,2},{4,5},{5,4},{6,7},{7,6},{8,9},{9,8},{10,11... | collective-permute-start | bytes 8257544 | tf_op jit(solution)/shard_map/ppermute | solution.py:106
  64.5 0.8 broadcast_and_fusion
  65.3 1.8 multiply_cosine_fusion.1
  67.2 2.0 maximum_select_fusion
  69.2 1.9 maximum_select_fusion.2
  71.2 1.8 select_bitcast_fusion.1
  73.0 3.7 %pad_maximum_fusion = bf16[4,512,1792]{2,1,0:T(8,128)(2,1)} fusion(bf16[1,512,1792]{2,1,0:T(8,128)(2,1)S(1)} %get-tuple-element.13, bf16[1,512,1792]{2,1,0:T(8,128)(2,1)S(1)} %maximum_select_fusion.2, bf16[1,512,1792]{2,1,0:T(8,128)(2,1)S(1)} %get-tuple-element.12, bf16[1,512,1792]{2,1,0:T(8,128)(2,1)S(1)} %maximum_select_fusion), kind=kLoop, calls=%fused_computation.14 | loop fusion | flops 11010048 | bytes 14680064 | tf_op jit(solution)/shard_map/stack | solution.py:115
  76.7 7.2 %gather_fusion = bf16[4,512,1792]{2,1,0:T(8,128)(2,1)} fusion(bf16[4,512,1792]{2,1,0:T(8,128)(2,1)} %pad_maximum_fusion, s32[1024]{0:T(1024)S(1)} %pad_clamp_fusion.2), kind=kCustom, calls=%fused_computation | custom fusion | bytes 14680080 | tf_op jit(solution)/shard_map/jit(_take)/gather | solution.py:117
  83.9 5.3 %fusion = f32[512]{0:T(512)S(1)} fusion(bf16[4,512,1792]{2,1,0:T(8,128)(2,1)} %gather_fusion, pred[4]{0:T(512)(128)(4,1)S(1)} %compare_and_fusion), kind=kLoop, calls=%fused_computation.5 | loop fusion | flops 14679552 | bytes 7342084 | tf_op jit(solution)/shard_map/reduce_sum | solution.py:120
  89.1 1.2 multiply_convert_fusion
  90.4 5.7 %fusion.2 = bf16[4,512,1792]{2,1,0:T(8,128)(2,1)} fusion(f32[4,1792]{1,0:T(4,128)S(1)} %mul.219, f32[512]{0:T(512)S(1)} %add_rsqrt_fusion, bf16[4,512,1792]{2,1,0:T(8,128)(2,1)S(1)} %copy-done.2, pred[4]{0:T(512)(128)(4,1)S(1)} %compare_and_fusion), kind=kLoop, calls=%fused_computation.7 | loop fusion | flops 18350080 | bytes 14710788 | tf_op jit(solution)/shard_map/convert.13
  96.0 7.2 %fusion.23 = f32[4,128,1,256]{3,1,0,2:T(8,128)} fusion(bf16[4,128,4,1792]{3,1,0,2:T(8,128)(2,1)} %bitcast.198, bf16[4,1792,256]{1,2,0:T(8,128)(2,1)} %copy.70), kind=kOutput, calls=%fused_computation.43 | convolution fusion | flops 1879048192 | bytes 11534336 | tf_op jit(solution)/shard_map/csf,cfn->sn/dot_general | solution.py:181
  103.2 7.1 %convolution_bitcast_fusion = f32[4,128,512]{2,1,0:T(8,128)} fusion(bf16[4,128,4,1792]{3,1,0,2:T(8,128)(2,1)S(1)} %bitcast.199, bf16[4,1792,512,1]{2,1,3,0:T(8,128)(2,1)} %bitcast.232), kind=kOutput, calls=%fused_computation.41 | convolution fusion | flops 3758096384 | bytes 15728640 | tf_op jit(solution)/shard_map/csf,cfn->sn/dot_general | solution.py:169
  110.3 5.3 %gather_fusion.1 = bf16[4,608,128]{2,1,0:T(8,128)(2,1)} fusion(bf16[64,608,128]{2,1,0:T(8,128)(2,1)} %all-gather.2.cloned.1.call-done, s32[1024]{0:T(1024)S(1)} %get-tuple-element.29), kind=kCustom, calls=%fused_computation.1 | custom fusion | bytes 1245200 | tf_op jit(solution)/shard_map/jit(_take)/gather | solution.py:146
  115.6 1.4 copy.149
  117.1 1.6 convolution_convert_fusion
  118.8 0.8 broadcast_in_dim.106
  119.6 3.4 %all-to-all-start = ((bf16[8,4,128,48]{2,3,1,0:T(8,128)(2,1)}), bf16[8,4,128,48]{2,3,1,0:T(8,128)(2,1)S(1)}, u32[]{:S(2)}, u32[]{:S(2)}) async-start(bf16[8,4,128,48]{2,3,1,0:T(8,128)(2,1)} %broadcast_in_dim.106), calls=%async_computation | async-start | bytes 786432 | tf_op jit(solution)/shard_map/all_to_all | solution.py:51
  123.0 0.7 fusion.88
  123.7 2.0 gather_fusion.2
  125.6 3.2 %copy.77 = bf16[2,16,128,256]{3,2,0,1:T(8,128)(2,1)} copy(bf16[2,16,128,256]{3,2,1,0:T(8,128)(2,1)} %bitcast.196) | data formatting | bytes 4194304 | tf_op jit(solution)/shard_map/reshape | solution.py:216
  128.9 1.8 all-to-all-done
  130.6 7.9 %all-to-all-start.1 = ((bf16[2,16,128,256]{3,2,0,1:T(8,128)(2,1)}), bf16[2,16,128,256]{3,2,0,1:T(8,128)(2,1)}, u32[]{:S(2)}, u32[]{:S(2)}) async-start(bf16[2,16,128,256]{3,2,0,1:T(8,128)(2,1)} %copy.77), calls=%async_computation.1 | async-start | bytes 4194304 | tf_op jit(solution)/shard_map/all_to_all | solution.py:219
  138.9 0.6 copy-done.13
  139.9 0.4 reshape.689
  140.3 0.6 fusion.87
  141.6 0.4 copy-done.14
  142.0 0.9 fusion.29
  142.9 1.2 fusion.59
  144.1 0.5 fusion.89
  144.9 0.8 copy-done.5
  145.6 22.1 %all-to-all-done.1 = bf16[2,16,128,256]{3,2,0,1:T(8,128)(2,1)} async-done(((bf16[2,16,128,256]{3,2,0,1:T(8,128)(2,1)}), bf16[2,16,128,256]{3,2,0,1:T(8,128)(2,1)}, u32[]{:S(2)}, u32[]{:S(2)}) %all-to-all-start.1) | async-done | bytes 2097184 | tf_op jit(solution)/shard_map/all_to_all | solution.py:219
  167.7 1.8 copy.78
  169.5 1.5 fusion.3
  171.0 2.3 fusion.26
  173.3 2.2 fusion.9
  175.6 1.1 bitcast_multiply_fusion
  176.8 1.9 fusion.22
  179.2 9.1 %convert_bitcast_fusion = bf16[8,512,896]{2,1,0:T(8,128)(2,1)} fusion(bf16[512,512,1]{1,0,2:T(8,128)(2,1)S(1)} %reshape.741, bf16[64,8,8,896]{3,2,1,0:T(8,128)(2,1)} %bitcast.233), kind=kOutput, calls=%fused_computation.15 | convolution fusion | flops 3761766400 | bytes 15204352 | tf_op jit(solution)/shard_map/sc,ctf->tsf/dot_general | solution.py:251
  188.4 0.8 copy-done.12
  189.3 0.7 broadcast_in_dim.112
  190.0 7.0 %all-to-all-start.2 = ((bf16[8,4,128,16]{2,3,1,0:T(8,128)(2,1)}), bf16[8,4,128,16]{2,3,1,0:T(8,128)(2,1)S(1)}, u32[]{:S(2)}, u32[]{:S(2)}) async-start(bf16[8,4,128,16]{2,3,1,0:T(8,128)(2,1)} %broadcast_in_dim.112), calls=%async_computation.3 | async-start | bytes 262144 | tf_op jit(solution)/shard_map/all_to_all | solution.py:51
  197.1 6.0 %all-to-all-done.2 = bf16[8,4,128,16]{2,3,1,0:T(8,128)(2,1)S(1)} async-done(((bf16[8,4,128,16]{2,3,1,0:T(8,128)(2,1)}), bf16[8,4,128,16]{2,3,1,0:T(8,128)(2,1)S(1)}, u32[]{:S(2)}, u32[]{:S(2)}) %all-to-all-start.2) | async-done | bytes 131104 | tf_op jit(solution)/shard_map/all_to_all | solution.py:51
  203.1 1.7 convolution_multiply_fusion
  204.8 32.0 %reduce-scatter.2.cloned.1.call-done = bf16[1,512,896]{2,1,0:T(8,128)(2,1)} async-done(((bf16[8,512,896]{2,1,0:T(8,128)(2,1)}), bf16[1,512,896]{2,1,0:T(8,128)(2,1)}) %reduce-scatter.2.cloned.1.call-update) | async-done | bytes 917520 | tf_op jit(solution)/shard_map/reduce_scatter | solution.py:269
  236.8 2.8 %fusion.16 = bf16[512,896]{1,0:T(8,128)(2,1)} fusion(f32[4,128,896]{2,1,0:T(8,128)} %convolution_multiply_fusion, bf16[1,512,896]{2,1,0:T(8,128)(2,1)} %reduce-scatter.2.cloned.1.call-done), kind=kLoop, calls=%fused_computation.28 | loop fusion | flops 1376256 | bytes 3670016 | tf_op jit(solution)/shard_map/convert_element_type | solution.py:275
  (95 shorter events, 4.2 us)
Async XLA Ops:
  6.5 117.1 %copy-start = (bf16[32,128,256]{2,1,0:T(8,128)(2,1)S(1)}, bf16[32,128,256]{2,1,0:T(8,128)(2,1)}, u32[]{:S(2)}) copy-start(bf16[32,128,256]{2,1,0:T(8,128)(2,1)} %param.31) | copy-start | bytes 6291460
  6.5 6.1 %copy-start.3 = (bf16[512,896]{1,0:T(8,128)(2,1)S(1)}, bf16[512,896]{1,0:T(8,128)(2,1)}, u32[]{:S(2)}) copy-start(bf16[512,896]{1,0:T(8,128)(2,1)} %param.16) | copy-start | bytes 2752516
  6.5 103.8 %all-gather.2.cloned.1.call-start = ((), (), s32[]{:S(2)}) async-start(), calls=%async_computation.4 | async-start | bytes 10584064 | tf_op jit(solution)/shard_map/all_gather | solution.py:142
  11.6 36.4 %copy-start.19 = (s32[32]{0:T(128)S(1)}, s32[32]{0:T(128)}, u32[]{:S(2)}) copy-start(s32[32]{0:T(128)} %param.29) | copy-start | bytes 388
  11.6 36.4 %copy-start.20 = (s32[32]{0:T(128)S(1)}, s32[32]{0:T(128)}, u32[]{:S(2)}) copy-start(s32[32]{0:T(128)} %param.28) | copy-start | bytes 388
  11.6 36.8 %copy-start.15 = (f32[7168]{0:T(1024)S(1)}, f32[7168]{0:T(1024)}, u32[]{:S(2)}) copy-start(f32[7168]{0:T(1024)} %param.17) | copy-start | bytes 86020
  11.6 37.5 %copy-start.21 = (s32[1,32]{1,0:T(1,128)S(1)}, s32[1,32]{1,0:T(1,128)}, u32[]{:S(2)}) copy-start(s32[1,32]{1,0:T(1,128)} %param.30) | copy-start | bytes 388
  12.6 3.7 %collective-permute-start = (bf16[512,896]{1,0:T(8,128)(2,1)S(1)}, bf16[512,896]{1,0:T(8,128)(2,1)}, u32[]{:S(2)}, u32[]{:S(2)}) collective-permute-start(bf16[512,896]{1,0:T(8,128)(2,1)S(1)} %copy-done.3), channel_id=1, source_target_pairs={{0,1},{1,0},{2,3},{3,2},{4,5},{5,4},{6,7},{7,6},{8,9},{9,8},{10,11... | collective-permute-start | bytes 2752520 | tf_op jit(solution)/shard_map/ppermute | solution.py:95
  19.6 23.1 %collective-permute-start.1 = (bf16[512,1792]{1,0:T(8,128)(2,1)}, bf16[512,1792]{1,0:T(8,128)(2,1)}, u32[]{:S(2)}, u32[]{:S(2)}) collective-permute-start(bf16[512,1792]{1,0:T(8,128)(2,1)} %maximum_select_fusion.1), channel_id=1, source_target_pairs={{6,0},{3,1},{0,2},{5,3},{2,4},{7,5},{4,6},{1,7},{14,8},{11,9},{8,1... | collective-permute-start | bytes 5505032 | tf_op jit(solution)/shard_map/ppermute | solution.py:101
  44.8 13.8 %collective-permute-start.2 = (bf16[512,896]{1,0:T(8,128)(2,1)}, bf16[512,896]{1,0:T(8,128)(2,1)}, u32[]{:S(2)}, u32[]{:S(2)}) collective-permute-start(bf16[512,896]{1,0:T(8,128)(2,1)} %constant_dynamic-slice_fusion), channel_id=1, source_target_pairs={{6,0},{3,1},{0,2},{5,3},{2,4},{7,5},{4,6},{1,7},{14,8},{11,9},{8,1... | collective-permute-start | bytes 2752520 | tf_op jit(solution)/shard_map/ppermute | solution.py:102
  56.1 8.1 %copy-start.18 = (s32[4]{0:T(128)S(1)}, s32[4]{0:T(128)}, u32[]{:S(2)}) copy-start(s32[4]{0:T(128)} %param.26) | copy-start | bytes 52
  56.1 8.2 %copy-start.22 = (s32[4]{0:T(128)S(1)}, s32[4]{0:T(128)}, u32[]{:S(2)}) copy-start(s32[4]{0:T(128)} %param.27) | copy-start | bytes 52
  60.6 8.5 %collective-permute-start.3 = (bf16[512,2688]{1,0:T(8,128)(2,1)S(1)}, bf16[512,2688]{1,0:T(8,128)(2,1)S(1)}, u32[]{:S(2)}, u32[]{:S(2)}) collective-permute-start(bf16[512,2688]{1,0:T(8,128)(2,1)S(1)} %pad_maximum_fusion.1), channel_id=1, source_target_pairs={{0,1},{1,0},{2,3},{3,2},{4,5},{5,4},{6,7},{7,6},{8,9},{9,8},{10,11... | collective-permute-start | bytes 8257544 | tf_op jit(solution)/shard_map/ppermute | solution.py:106
  64.3 6.8 %copy-start.16 = (pred[4,128]{1,0:T(4,128)(4,1)}, pred[4,128]{1,0:T(4,128)(4,1)S(1)}, u32[]{:S(2)}) copy-start(pred[4,128]{1,0:T(4,128)(4,1)S(1)} %iota_compare_fusion.1) | copy-start | bytes 1540
  83.9 6.5 %copy-start.2 = (bf16[4,512,1792]{2,1,0:T(8,128)(2,1)S(1)}, bf16[4,512,1792]{2,1,0:T(8,128)(2,1)}, u32[]{:S(2)}) copy-start(bf16[4,512,1792]{2,1,0:T(8,128)(2,1)} %gather_fusion) | copy-start | bytes 22020100
  96.0 7.2 %copy-start.4 = (bf16[4,512,1792]{2,1,0:T(8,128)(2,1)S(1)}, bf16[4,512,1792]{2,1,0:T(8,128)(2,1)}, u32[]{:S(2)}) copy-start(bf16[4,512,1792]{2,1,0:T(8,128)(2,1)} %fusion.2) | copy-start | bytes 22020100
  119.6 11.0 %all-to-all-start = ((bf16[8,4,128,48]{2,3,1,0:T(8,128)(2,1)}), bf16[8,4,128,48]{2,3,1,0:T(8,128)(2,1)S(1)}, u32[]{:S(2)}, u32[]{:S(2)}) async-start(bf16[8,4,128,48]{2,3,1,0:T(8,128)(2,1)} %broadcast_in_dim.106), calls=%async_computation | async-start | bytes 786432 | tf_op jit(solution)/shard_map/all_to_all | solution.py:51
  125.6 13.9 %copy-start.9 = (f32[4,128,512]{2,1,0:T(8,128)S(1)}, f32[4,128,512]{2,1,0:T(8,128)}, u32[]{:S(2)}) copy-start(f32[4,128,512]{2,1,0:T(8,128)} %convolution_bitcast_fusion) | copy-start | bytes 3145732
  130.6 37.1 %all-to-all-start.1 = ((bf16[2,16,128,256]{3,2,0,1:T(8,128)(2,1)}), bf16[2,16,128,256]{3,2,0,1:T(8,128)(2,1)}, u32[]{:S(2)}, u32[]{:S(2)}) async-start(bf16[2,16,128,256]{3,2,0,1:T(8,128)(2,1)} %copy.77), calls=%async_computation.1 | async-start | bytes 4194304 | tf_op jit(solution)/shard_map/all_to_all | solution.py:219
  138.6 98.3 %reduce-scatter.2.cloned.1.call-start = ((), (), s32[]{:S(2)}) async-start(), calls=%async_computation.5 | async-start | bytes 8257536 | tf_op jit(solution)/shard_map/reduce_scatter | solution.py:269
  138.9 0.6 copy-start.13
  139.9 1.0 copy-start.7
  139.9 1.0 copy-start.8
  140.9 1.1 copy-start.14
  140.9 3.2 %copy-start.10 = (pred[4,128,128]{1,2,0:T(8,128)(4,1)S(1)}, pred[4,128,128]{1,2,0:T(8,128)(4,1)}, u32[]{:S(2)}) copy-start(pred[4,128,128]{1,2,0:T(8,128)(4,1)} %broadcast_and_fusion) | copy-start | bytes 196612
  144.7 1.0 copy-start.5
  175.5 1.3 copy-start.6
  175.5 1.3 copy-start.11
  175.5 1.3 copy-start.17
  188.3 0.8 copy-start.12
  188.3 51.3 %copy-start.1 = (bf16[32,128,256]{2,1,0:T(8,128)(2,1)S(1)}, bf16[32,128,256]{2,1,0:T(8,128)(2,1)}, u32[]{:S(2)}) copy-start(bf16[32,128,256]{2,1,0:T(8,128)(2,1)} %param.31) | copy-start | bytes 6291460
  190.0 13.1 %all-to-all-start.2 = ((bf16[8,4,128,16]{2,3,1,0:T(8,128)(2,1)}), bf16[8,4,128,16]{2,3,1,0:T(8,128)(2,1)S(1)}, u32[]{:S(2)}, u32[]{:S(2)}) async-start(bf16[8,4,128,16]{2,3,1,0:T(8,128)(2,1)} %broadcast_in_dim.112), calls=%async_computation.3 | async-start | bytes 262144 | tf_op jit(solution)/shard_map/all_to_all | solution.py:51
Sparse Core Ops, SparseCore 0:
  12.7 81.0 all-gather.1
  188.5 48.3 reduce-scatter.1

commit v7 on v5

--- a/solution.py
+++ b/solution.py
@@ -49,6 +49,17 @@
 def gather_by_exchange(piece, axis_name, count):
     spread = jnp.broadcast_to(piece[None], (count,) + piece.shape)
     return lax.all_to_all(spread, axis_name, split_axis=0, concat_axis=0, tiled=True)
+
+
+def sum_over_tensor(partial, count):
+    total = partial.astype(jnp.bfloat16).astype(jnp.float32)
+    step = 1
+    while step < count:
+        pairs = [(index, index ^ step) for index in range(count)]
+        sent = total.astype(jnp.bfloat16)
+        total = sent.astype(jnp.float32) + lax.ppermute(sent, "tensor", pairs).astype(jnp.float32)
+        step *= 2
+    return total
 
 
 def local(
@@ -142,6 +153,12 @@
     every_adapter = lax.all_gather(
         joined.reshape(local_adapters, lane_rows, 128), "req", axis=0, tiled=True
     )
+    slot_order = page_slot_table[0].reshape(holders, cached_count).T.reshape(-1)
+    outgoing = cache_page_pool[slot_order].reshape(
+        cached_count, holders, page_rows, cache_page_pool.shape[2]
+    )
+    every_adapter, outgoing = lax.optimization_barrier((every_adapter, outgoing))
+    arrived = lax.all_to_all(outgoing, "req", split_axis=1, concat_axis=1, tiled=True)
     picked = jnp.take(every_adapter, request_adapter, axis=0, mode="clip").reshape(
         request_number, -1
     )
@@ -159,12 +176,7 @@
     partial_low = jnp.einsum(
         "rsd,rkd->rsk", own_columns, down_picked, preferred_element_type=jnp.float32
     )
-    reduced_input = (
-        gather_by_exchange(partial_low.astype(jnp.bfloat16), "tensor", tensor_count)
-        .astype(jnp.float32)
-        .sum(axis=0)
-        .astype(jnp.bfloat16)
-    )
+    reduced_input = sum_over_tensor(partial_low, tensor_count).astype(jnp.bfloat16)
     query_rows = jnp.einsum(
         "csf,cfn->sn",
         normed_parts,
@@ -211,11 +223,6 @@
     own_mask = causal & (slot_index[None, None, :] < prompt_length[:, None, None])
     own_part = partial_softmax(query_rot, key_rot, value_new, own_mask)
     asked_queries = query_rot[1::2]
-    slot_order = page_slot_table[0].reshape(holders, cached_count).T.reshape(-1)
-    outgoing = cache_page_pool[slot_order].reshape(
-        cached_count, holders, page_rows, cache_page_pool.shape[2]
-    )
-    arrived = lax.all_to_all(outgoing, "req", split_axis=1, concat_axis=1, tiled=True)
     my_base = lax.dynamic_slice_in_dim(first_page_device, req_index * cached_count, cached_count, 0)
     page_of = (jnp.arange(holders, dtype=jnp.int32)[None, :] - my_base[:, None]) % holders
     key_pos = (
@@ -259,12 +266,7 @@
         output_down_picked,
         preferred_element_type=jnp.float32,
     )
-    reduced_output = (
-        gather_by_exchange(low_part.astype(jnp.bfloat16), "tensor", tensor_count)
-        .astype(jnp.float32)
-        .sum(axis=0)
-        .astype(jnp.bfloat16)
-    )
+    reduced_output = sum_over_tensor(low_part, tensor_count).astype(jnp.bfloat16)
     head_total = lax.psum_scatter(
         head_terms.astype(jnp.bfloat16), "tensor", scatter_dimension=0, tiled=False
     ).astype(jnp.float32)

time: 255 us -> 238 us (0.933)
  waiting for transfers between devices: 98.1 us -> 85.4 us
  local copies, waits for them, and re-layouts: 43.7 us -> 39 us
  other arithmetic: 41.5 us -> 37.4 us
  matrix products: 33.4 us -> 36.3 us
    all_to_all x2 -> x0, waiting for transfers between devices: 12.5 us -> none  [gather_by_exchange(): lax.all_to_all(spread, axis_name, split_axis=0, concat_axis=0, tiled=True)]
    all_to_all x1, waiting for transfers between devices: 32.6 us -> 21.7 us  [local(): lax.all_to_all(outgoing, 'req', split_axis=1, concat_axis=1, tiled=True)]
    all_to_all x2 -> x0, starting transfers between devices: 8.47 us -> none  [gather_by_exchange(): lax.all_to_all(spread, axis_name, split_axis=0, concat_axis=0, tiled=True)]
    ppermute x0 -> x6, starting transfers between devices: none -> 7.97 us  [sum_over_tensor(): lax.ppermute(sent, 'tensor', pairs).astype(jnp.float32)]
    ppermute x0 -> x6, waiting for transfers between devices: none -> 6.77 us  [sum_over_tensor(): lax.ppermute(sent, 'tensor', pairs).astype(jnp.float32)]
    reduce_scatter x1, waiting for transfers between devices: 30.2 us -> 33.7 us  [local(): lax.psum_scatter(head_terms.astype(jnp.bfloat16), 'tensor', scatter_dimen...]
    reshape x1 -> x0, local copies, waits for them, and re-layouts: 3.13 us -> none  [local(): cache_page_pool[slot_order]]
    dot_general x1, matrix products: 7.13 us -> 10.1 us  [local(): jnp.einsum('csf,cfn->sn', normed_parts, query_weight.reshape(chip_count,...]
  transfers between devices with their start and end apart: 9 -> 13, of which waited for: 6 -> 9; matrix products, arithmetic and copies ran while one was open for 31% -> 32% of each run, Pallas kernels for 0% -> 0%
where the time goes in v7:
time: 238 us; the launch traced here: 237 us
  waiting for transfers between devices  85.4 us (36%)
  local copies, waits for them, and re-layouts  39 us (16%)
  other arithmetic  37.4 us (16%)
  matrix products  36.3 us (15%)
  starting transfers between devices  25.3 us (11%)
  between operations  13.9 us (6%)
    reduce_scatter x1, waiting for transfers between devices, local(): lax.psum_scatter(head_terms.astype(jnp.bfloat16), 'tensor', scatter_dimen...  33.7 us
    all_to_all x1, waiting for transfers between devices, local(): lax.all_to_all(outgoing, 'req', split_axis=1, concat_axis=1, tiled=True)  21.7 us
    ppermute x1, waiting for transfers between devices, local(): beside = lax.ppermute(pair, 'tensor', along)  20.5 us
    dot_general x1, matrix products, local(): jnp.einsum('csf,cfn->sn', normed_parts, query_weight.reshape(chip_count,...  10.1 us
    dot_general x1, matrix products, local(): jnp.einsum('sc,ctf->tsf', attended, output_weight.reshape(output_weight.s...  9.14 us
    unnamed x65, local copies, waits for them, and re-layouts  9.12 us
    ppermute x6, starting transfers between devices, sum_over_tensor(): lax.ppermute(sent, 'tensor', pairs).astype(jnp.float32)  7.97 us
    all_to_all x1, starting transfers between devices, local(): lax.all_to_all(outgoing, 'req', split_axis=1, concat_axis=1, tiled=True)  7.81 us
  transfers between devices with their start and end apart: 13, of which 9 were waited for; matrix products, arithmetic and copies ran while one was open for 32% of the time, Pallas kernels for 0%

profile of v7, /device:TPU:1, one launch (start us, length us, event | category | flops | bytes accessed | tf_op | source)
XLA Modules:
  0.0 237.3 jit_solution(12745697755306017173)
XLA Ops:
  6.5 1.0 copy.107
  7.6 0.9 copy.109
  8.5 0.9 copy.110
  9.4 1.1 copy.106
  10.7 0.8 bitcast_dynamic-update-slice_fusion
  11.7 0.9 copy.150
  12.6 1.5 collective-permute-start
  14.1 2.2 collective-permute-done
  16.3 3.2 %maximum_select_fusion.1 = bf16[512,1792]{1,0:T(8,128)(2,1)} fusion(bf16[512,896]{1,0:T(8,128)(2,1)} %collective-permute-done, bf16[512,896]{1,0:T(8,128)(2,1)S(1)} %copy-done.4, pred[]{:T(512)S(6)} %eq.6), kind=kLoop, calls=%fused_computation.25 | loop fusion | flops 8257536 | bytes 3670017 | tf_op jit(solution)/shard_map/jit(_where)/select_n | solution.py:107
  19.5 2.6 %collective-permute-start.1 = (bf16[512,1792]{1,0:T(8,128)(2,1)}, bf16[512,1792]{1,0:T(8,128)(2,1)}, u32[]{:S(2)}, u32[]{:S(2)}) collective-permute-start(bf16[512,1792]{1,0:T(8,128)(2,1)} %maximum_select_fusion.1), channel_id=1, source_target_pairs={{6,0},{3,1},{0,2},{5,3},{2,4},{7,5},{4,6},{1,7},{14,8},{11,9},{8,1... | collective-permute-start | bytes 5505032 | tf_op jit(solution)/shard_map/ppermute | solution.py:112
  22.1 20.5 %collective-permute-done.1 = bf16[512,1792]{1,0:T(8,128)(2,1)} collective-permute-done((bf16[512,1792]{1,0:T(8,128)(2,1)}, bf16[512,1792]{1,0:T(8,128)(2,1)}, u32[]{:S(2)}, u32[]{:S(2)}) %collective-permute-start.1) | collective-permute-done | bytes 1835040 | tf_op jit(solution)/shard_map/ppermute | solution.py:112
  42.5 2.2 constant_dynamic-slice_fusion
  44.7 3.1 %collective-permute-start.2 = (bf16[512,896]{1,0:T(8,128)(2,1)}, bf16[512,896]{1,0:T(8,128)(2,1)}, u32[]{:S(2)}, u32[]{:S(2)}) collective-permute-start(bf16[512,896]{1,0:T(8,128)(2,1)} %constant_dynamic-slice_fusion), channel_id=1, source_target_pairs={{6,0},{3,1},{0,2},{5,3},{2,4},{7,5},{4,6},{1,7},{14,8},{11,9},{8,1... | collective-permute-start | bytes 2752520 | tf_op jit(solution)/shard_map/ppermute | solution.py:113
  47.9 0.6 dynamic_slice.14
  48.9 0.6 mul.219
  49.5 0.6 broadcast.416
  50.1 0.7 reduce.11
  51.1 6.2 %copy.71 = bf16[4,1792,256]{1,2,0:T(8,128)(2,1)} copy(bf16[4,1792,256]{2,1,0:T(8,128)(2,1)} %bitcast.203) | data formatting | bytes 7340032 | tf_op jit(solution)/shard_map/reshape | solution.py:195
  57.3 0.6 pad_clamp_fusion
  57.9 2.1 gather_fusion.1
  59.9 2.0 pad_maximum_fusion.1
  62.0 2.1 collective-permute-start.3
  64.4 0.8 broadcast_and_fusion
  65.2 1.0 multiply_cosine_fusion.1
  66.3 1.9 maximum_select_fusion
  68.2 0.6 collective-permute-done.3
  68.8 1.9 maximum_select_fusion.2
  70.8 1.8 select_bitcast_fusion.1
  72.6 3.6 %pad_maximum_fusion = bf16[4,512,1792]{2,1,0:T(8,128)(2,1)} fusion(bf16[1,512,1792]{2,1,0:T(8,128)(2,1)S(1)} %get-tuple-element.13, bf16[1,512,1792]{2,1,0:T(8,128)(2,1)S(1)} %maximum_select_fusion.2, bf16[1,512,1792]{2,1,0:T(8,128)(2,1)S(1)} %get-tuple-element.12, bf16[1,512,1792]{2,1,0:T(8,128)(2,1)S(1)} %maximum_select_fusion), kind=kLoop, calls=%fused_computation.14 | loop fusion | flops 11010048 | bytes 14680064 | tf_op jit(solution)/shard_map/stack | solution.py:126
  76.2 7.2 %gather_fusion = bf16[4,512,1792]{2,1,0:T(8,128)(2,1)} fusion(bf16[4,512,1792]{2,1,0:T(8,128)(2,1)} %pad_maximum_fusion, s32[1024]{0:T(1024)S(1)} %pad_clamp_fusion.2), kind=kCustom, calls=%fused_computation | custom fusion | bytes 14680080 | tf_op jit(solution)/shard_map/jit(_take)/gather | solution.py:128
  83.4 5.3 %fusion = f32[512]{0:T(512)S(1)} fusion(bf16[4,512,1792]{2,1,0:T(8,128)(2,1)} %gather_fusion, pred[4]{0:T(512)(128)(4,1)S(1)} %compare_and_fusion), kind=kLoop, calls=%fused_computation.5 | loop fusion | flops 14679552 | bytes 7342084 | tf_op jit(solution)/shard_map/reduce_sum | solution.py:131
  89.0 5.7 %fusion.2 = bf16[4,512,1792]{2,1,0:T(8,128)(2,1)} fusion(f32[4,1792]{1,0:T(4,128)S(1)} %copy-done.13, f32[512]{0:T(512)S(1)} %add_rsqrt_fusion, bf16[4,512,1792]{2,1,0:T(8,128)(2,1)S(1)} %copy-done.2, pred[4]{0:T(512)(128)(4,1)S(1)} %compare_and_fusion), kind=kLoop, calls=%fused_computation.7 | loop fusion | flops 18350080 | bytes 14710788 | tf_op jit(solution)/shard_map/convert.11
  94.7 10.1 %convolution_bitcast_fusion = f32[4,128,512]{2,1,0:T(8,128)} fusion(bf16[4,128,4,1792]{3,1,0,2:T(8,128)(2,1)} %bitcast.197, bf16[4,1792,512,1]{2,1,3,0:T(8,128)(2,1)} %bitcast.231), kind=kOutput, calls=%fused_computation.41 | convolution fusion | flops 3758096384 | bytes 15728640 | tf_op jit(solution)/shard_map/csf,cfn->sn/dot_general | solution.py:180
  104.8 4.6 %gather_fusion.2 = bf16[4,608,128]{2,1,0:T(8,128)(2,1)S(1)} fusion(bf16[64,608,128]{2,1,0:T(8,128)(2,1)} %all-gather.2.cloned.1.call-done, s32[1024]{0:T(1024)} %get-tuple-element.28), kind=kCustom, calls=%fused_computation.2 | custom fusion | bytes 1245200 | tf_op jit(solution)/shard_map/jit(_take)/gather | solution.py:162
  109.9 0.5 convolution_convert_fusion
  110.7 7.2 %fusion.23 = f32[4,128,1,256]{3,1,0,2:T(8,128)} fusion(bf16[4,128,4,1792]{3,1,0,2:T(8,128)(2,1)} %bitcast.198, bf16[4,1792,256]{1,2,0:T(8,128)(2,1)} %copy.71), kind=kOutput, calls=%fused_computation.43 | convolution fusion | flops 1879048192 | bytes 11534336 | tf_op jit(solution)/shard_map/csf,cfn->sn/dot_general | solution.py:192
  118.0 0.7 fusion.88
  118.7 2.3 collective-permute-done.5
  121.0 0.7 collective-permute-start.6
  121.7 1.5 copy.77
  123.2 7.8 %all-to-all-start = ((bf16[2,16,128,256]{3,2,0,1:T(8,128)(2,1)}), bf16[2,16,128,256]{3,2,0,1:T(8,128)(2,1)}, u32[]{:S(2)}, u32[]{:S(2)}) async-start(bf16[2,16,128,256]{3,2,0,1:T(8,128)(2,1)} %copy.77), calls=%async_computation | async-start | bytes 4194304 | tf_op jit(solution)/shard_map/all_to_all | solution.py:161
  132.1 0.6 fusion.87
  133.8 1.0 fusion.29
  134.7 1.2 fusion.59
  135.9 0.5 fusion.89
  136.7 0.8 copy-done.5
  137.5 21.7 %all-to-all-done = bf16[2,16,128,256]{3,2,0,1:T(8,128)(2,1)} async-done(((bf16[2,16,128,256]{3,2,0,1:T(8,128)(2,1)}), bf16[2,16,128,256]{3,2,0,1:T(8,128)(2,1)}, u32[]{:S(2)}, u32[]{:S(2)}) %all-to-all-start) | async-done | bytes 2097184 | tf_op jit(solution)/shard_map/all_to_all | solution.py:161
  159.2 1.8 copy.78
  161.0 1.5 fusion.3
  162.5 2.3 fusion.26
  164.7 2.2 fusion.9
  167.1 1.1 bitcast_multiply_fusion
  168.2 1.9 fusion.22
  170.7 9.1 %convert_bitcast_fusion = bf16[8,512,896]{2,1,0:T(8,128)(2,1)} fusion(bf16[512,512,1]{1,0,2:T(8,128)(2,1)S(1)} %reshape.739, bf16[64,8,8,896]{3,2,1,0:T(8,128)(2,1)} %bitcast.232), kind=kOutput, calls=%fused_computation.15 | convolution fusion | flops 3761766400 | bytes 15204352 | tf_op jit(solution)/shard_map/sc,ctf->tsf/dot_general | solution.py:257
  179.8 0.8 copy-done.10
  180.8 3.7 %collective-permute-start.7 = (bf16[4,128,16]{1,2,0:T(8,128)(2,1)S(1)}, bf16[4,128,16]{1,2,0:T(8,128)(2,1)S(1)}, u32[]{:S(2)}, u32[]{:S(2)}) collective-permute-start(bf16[4,128,16]{1,2,0:T(8,128)(2,1)S(1)} %convolution_convert_fusion.1), channel_id=1, source_target_pairs={{0,1},{1,0},{2,3},{3,2},{4,5},{5,4},{6,7},{7,6},{8,9},{9,8},{10,11... | collective-permute-start | bytes 49160 | tf_op jit(solution)/shard_map/ppermute | solution.py:60
  184.5 0.8 collective-permute-done.7
  185.4 0.5 collective-permute-start.8
  185.9 2.2 collective-permute-done.8
  188.1 2.6 %collective-permute-start.9 = (bf16[4,128,16]{1,2,0:T(8,128)(2,1)S(1)}, bf16[4,128,16]{1,2,0:T(8,128)(2,1)S(1)}, u32[]{:S(2)}, u32[]{:S(2)}) collective-permute-start(bf16[4,128,16]{1,2,0:T(8,128)(2,1)S(1)} %add_convert_fusion.5), channel_id=1, source_target_pairs={{0,4},{1,5},{2,6},{3,7},{4,0},{5,1},{6,2},{7,3},{8,12},{9,13},{10,... | collective-permute-start | bytes 49160 | tf_op jit(solution)/shard_map/ppermute | solution.py:60
  190.8 1.5 collective-permute-done.9
  192.3 1.8 convolution_multiply_fusion
  194.0 33.7 %reduce-scatter.2.cloned.1.call-done = bf16[1,512,896]{2,1,0:T(8,128)(2,1)} async-done(((bf16[8,512,896]{2,1,0:T(8,128)(2,1)}), bf16[1,512,896]{2,1,0:T(8,128)(2,1)}) %reduce-scatter.2.cloned.1.call-update) | async-done | bytes 917520 | tf_op jit(solution)/shard_map/reduce_scatter | solution.py:270
  227.7 2.8 %fusion.16 = bf16[512,896]{1,0:T(8,128)(2,1)} fusion(f32[4,128,896]{2,1,0:T(8,128)} %convolution_multiply_fusion, bf16[1,512,896]{2,1,0:T(8,128)(2,1)} %reduce-scatter.2.cloned.1.call-done), kind=kLoop, calls=%fused_computation.28 | loop fusion | flops 1376256 | bytes 3670016 | tf_op jit(solution)/shard_map/convert_element_type | solution.py:276
  (108 shorter events, 6.0 us)
Async XLA Ops:
  6.5 51.3 %copy-start = (bf16[32,128,256]{2,1,0:T(8,128)(2,1)S(1)}, bf16[32,128,256]{2,1,0:T(8,128)(2,1)}, u32[]{:S(2)}) copy-start(bf16[32,128,256]{2,1,0:T(8,128)(2,1)} %param.31) | copy-start | bytes 6291460
  6.5 6.0 %copy-start.4 = (bf16[512,896]{1,0:T(8,128)(2,1)S(1)}, bf16[512,896]{1,0:T(8,128)(2,1)}, u32[]{:S(2)}) copy-start(bf16[512,896]{1,0:T(8,128)(2,1)} %param.16) | copy-start | bytes 2752516
  6.5 98.3 %all-gather.2.cloned.1.call-start = ((), (), s32[]{:S(2)}) async-start(), calls=%async_computation.2 | async-start | bytes 10584064 | tf_op jit(solution)/shard_map/all_gather | solution.py:153
  11.6 36.2 %copy-start.21 = (s32[32]{0:T(128)S(1)}, s32[32]{0:T(128)}, u32[]{:S(2)}) copy-start(s32[32]{0:T(128)} %param.29) | copy-start | bytes 388
  11.6 36.3 %copy-start.22 = (s32[32]{0:T(128)S(1)}, s32[32]{0:T(128)}, u32[]{:S(2)}) copy-start(s32[32]{0:T(128)} %param.28) | copy-start | bytes 388
  11.6 37.2 %copy-start.14 = (f32[7168]{0:T(1024)S(1)}, f32[7168]{0:T(1024)}, u32[]{:S(2)}) copy-start(f32[7168]{0:T(1024)} %param.17) | copy-start | bytes 86020
  11.6 38.5 %copy-start.23 = (s32[1,32]{1,0:T(1,128)S(1)}, s32[1,32]{1,0:T(1,128)}, u32[]{:S(2)}) copy-start(s32[1,32]{1,0:T(1,128)} %param.30) | copy-start | bytes 388
  12.6 3.7 %collective-permute-start = (bf16[512,896]{1,0:T(8,128)(2,1)S(1)}, bf16[512,896]{1,0:T(8,128)(2,1)}, u32[]{:S(2)}, u32[]{:S(2)}) collective-permute-start(bf16[512,896]{1,0:T(8,128)(2,1)S(1)} %copy-done.4), channel_id=1, source_target_pairs={{0,1},{1,0},{2,3},{3,2},{4,5},{5,4},{6,7},{7,6},{8,9},{9,8},{10,11... | collective-permute-start | bytes 2752520 | tf_op jit(solution)/shard_map/ppermute | solution.py:106
  19.5 23.1 %collective-permute-start.1 = (bf16[512,1792]{1,0:T(8,128)(2,1)}, bf16[512,1792]{1,0:T(8,128)(2,1)}, u32[]{:S(2)}, u32[]{:S(2)}) collective-permute-start(bf16[512,1792]{1,0:T(8,128)(2,1)} %maximum_select_fusion.1), channel_id=1, source_target_pairs={{6,0},{3,1},{0,2},{5,3},{2,4},{7,5},{4,6},{1,7},{14,8},{11,9},{8,1... | collective-permute-start | bytes 5505032 | tf_op jit(solution)/shard_map/ppermute | solution.py:112
  44.7 15.2 %collective-permute-start.2 = (bf16[512,896]{1,0:T(8,128)(2,1)}, bf16[512,896]{1,0:T(8,128)(2,1)}, u32[]{:S(2)}, u32[]{:S(2)}) collective-permute-start(bf16[512,896]{1,0:T(8,128)(2,1)} %constant_dynamic-slice_fusion), channel_id=1, source_target_pairs={{6,0},{3,1},{0,2},{5,3},{2,4},{7,5},{4,6},{1,7},{14,8},{11,9},{8,1... | collective-permute-start | bytes 2752520 | tf_op jit(solution)/shard_map/ppermute | solution.py:113
  51.1 6.2 %copy-start.20 = (s32[4]{0:T(128)S(1)}, s32[4]{0:T(128)}, u32[]{:S(2)}) copy-start(s32[4]{0:T(128)} %param.26) | copy-start | bytes 52
  59.9 4.2 %copy-start.24 = (s32[4]{0:T(128)S(1)}, s32[4]{0:T(128)}, u32[]{:S(2)}) copy-start(s32[4]{0:T(128)} %param.27) | copy-start | bytes 52
  59.9 6.3 %copy-start.19 = (s32[2]{0:T(128)S(1)}, s32[2]{0:T(128)}, u32[]{:S(2)}) copy-start(s32[2]{0:T(128)} %dynamic_slice.14) | copy-start | bytes 28
  62.0 6.8 %collective-permute-start.3 = (bf16[512,2688]{1,0:T(8,128)(2,1)S(1)}, bf16[512,2688]{1,0:T(8,128)(2,1)S(1)}, u32[]{:S(2)}, u32[]{:S(2)}) collective-permute-start(bf16[512,2688]{1,0:T(8,128)(2,1)S(1)} %pad_maximum_fusion.1), channel_id=1, source_target_pairs={{0,1},{1,0},{2,3},{3,2},{4,5},{5,4},{6,7},{7,6},{8,9},{9,8},{10,11... | collective-permute-start | bytes 8257544 | tf_op jit(solution)/shard_map/ppermute | solution.py:117
  64.1 1.1 copy-start.15
  64.2 6.5 %copy-start.17 = (pred[4,128]{1,0:T(4,128)(4,1)}, pred[4,128]{1,0:T(4,128)(4,1)S(1)}, u32[]{:S(2)}) copy-start(pred[4,128]{1,0:T(4,128)(4,1)S(1)} %iota_compare_fusion.1) | copy-start | bytes 1540
  83.4 5.6 %copy-start.2 = (bf16[4,512,1792]{2,1,0:T(8,128)(2,1)S(1)}, bf16[4,512,1792]{2,1,0:T(8,128)(2,1)}, u32[]{:S(2)}) copy-start(bf16[4,512,1792]{2,1,0:T(8,128)(2,1)} %gather_fusion) | copy-start | bytes 22020100
  83.4 5.6 %copy-start.13 = (f32[4,1792]{1,0:T(4,128)S(1)}, f32[4,1792]{1,0:T(4,128)}, u32[]{:S(2)}) copy-start(f32[4,1792]{1,0:T(4,128)} %mul.219) | copy-start | bytes 86020
  110.4 11.3 %copy-start.3 = (bf16[32,128,256]{2,1,0:T(8,128)(2,1)S(1)}, bf16[32,128,256]{2,1,0:T(8,128)(2,1)}, u32[]{:S(2)}) copy-start(bf16[32,128,256]{2,1,0:T(8,128)(2,1)} %gather_fusion.1) | copy-start | bytes 6291460
  110.4 7.5 %collective-permute-start.4 = (bf16[4,128,48]{1,2,0:T(8,128)(2,1)S(1)}, bf16[4,128,48]{1,2,0:T(8,128)(2,1)S(1)}, u32[]{:S(2)}, u32[]{:S(2)}) collective-permute-start(bf16[4,128,48]{1,2,0:T(8,128)(2,1)S(1)} %convolution_convert_fusion), channel_id=1, source_target_pairs={{0,1},{1,0},{2,3},{3,2},{4,5},{5,4},{6,7},{7,6},{8,9},{9,8},{10,11... | collective-permute-start | bytes 147464 | tf_op jit(solution)/shard_map/ppermute | solution.py:60
  117.9 3.0 %collective-permute-start.5 = (bf16[4,128,48]{1,2,0:T(8,128)(2,1)S(1)}, bf16[4,128,48]{1,2,0:T(8,128)(2,1)S(1)}, u32[]{:S(2)}, u32[]{:S(2)}) collective-permute-start(bf16[4,128,48]{1,2,0:T(8,128)(2,1)S(1)} %add_convert_fusion.3), channel_id=1, source_target_pairs={{0,2},{1,3},{2,0},{3,1},{4,6},{5,7},{6,4},{7,5},{8,10},{9,11},{10,... | collective-permute-start | bytes 147464 | tf_op jit(solution)/shard_map/ppermute | solution.py:60
  121.0 10.4 %collective-permute-start.6 = (bf16[4,128,48]{1,2,0:T(8,128)(2,1)S(1)}, bf16[4,128,48]{1,2,0:T(8,128)(2,1)S(1)}, u32[]{:S(2)}, u32[]{:S(2)}) collective-permute-start(bf16[4,128,48]{1,2,0:T(8,128)(2,1)S(1)} %add_convert_fusion.2), channel_id=1, source_target_pairs={{0,4},{1,5},{2,6},{3,7},{4,0},{5,1},{6,2},{7,3},{8,12},{9,13},{10,... | collective-permute-start | bytes 147464 | tf_op jit(solution)/shard_map/ppermute | solution.py:60
  123.2 8.1 %copy-start.7 = (f32[4,128,512]{2,1,0:T(8,128)S(1)}, f32[4,128,512]{2,1,0:T(8,128)}, u32[]{:S(2)}) copy-start(f32[4,128,512]{2,1,0:T(8,128)} %convolution_bitcast_fusion) | copy-start | bytes 3145732
  123.2 35.9 %all-to-all-start = ((bf16[2,16,128,256]{3,2,0,1:T(8,128)(2,1)}), bf16[2,16,128,256]{3,2,0,1:T(8,128)(2,1)}, u32[]{:S(2)}, u32[]{:S(2)}) async-start(bf16[2,16,128,256]{3,2,0,1:T(8,128)(2,1)} %copy.77), calls=%async_computation | async-start | bytes 4194304 | tf_op jit(solution)/shard_map/all_to_all | solution.py:161
  131.1 96.6 %reduce-scatter.2.cloned.1.call-start = ((), (), s32[]{:S(2)}) async-start(), calls=%async_computation.3 | async-start | bytes 8257536 | tf_op jit(solution)/shard_map/reduce_scatter | solution.py:270
  131.4 1.4 copy-start.11
  132.7 1.0 copy-start.12
  132.7 2.0 copy-start.16
  132.7 3.2 %copy-start.8 = (pred[4,128,128]{1,2,0:T(8,128)(4,1)S(1)}, pred[4,128,128]{1,2,0:T(8,128)(4,1)}, u32[]{:S(2)}) copy-start(pred[4,128,128]{1,2,0:T(8,128)(4,1)} %broadcast_and_fusion) | copy-start | bytes 196612
  136.5 1.0 copy-start.5
  166.9 1.3 copy-start.6
  166.9 1.3 copy-start.9
  166.9 1.3 copy-start.18
  179.8 0.8 copy-start.10
  179.8 50.7 %copy-start.1 = (bf16[32,128,256]{2,1,0:T(8,128)(2,1)S(1)}, bf16[32,128,256]{2,1,0:T(8,128)(2,1)}, u32[]{:S(2)}) copy-start(bf16[32,128,256]{2,1,0:T(8,128)(2,1)} %param.31) | copy-start | bytes 6291460
  180.8 4.6 %collective-permute-start.7 = (bf16[4,128,16]{1,2,0:T(8,128)(2,1)S(1)}, bf16[4,128,16]{1,2,0:T(8,128)(2,1)S(1)}, u32[]{:S(2)}, u32[]{:S(2)}) collective-permute-start(bf16[4,128,16]{1,2,0:T(8,128)(2,1)S(1)} %convolution_convert_fusion.1), channel_id=1, source_target_pairs={{0,1},{1,0},{2,3},{3,2},{4,5},{5,4},{6,7},{7,6},{8,9},{9,8},{10,11... | collective-permute-start | bytes 49160 | tf_op jit(solution)/shard_map/ppermute | solution.py:60
  185.4 2.7 %collective-permute-start.8 = (bf16[4,128,16]{1,2,0:T(8,128)(2,1)S(1)}, bf16[4,128,16]{1,2,0:T(8,128)(2,1)S(1)}, u32[]{:S(2)}, u32[]{:S(2)}) collective-permute-start(bf16[4,128,16]{1,2,0:T(8,128)(2,1)S(1)} %add_convert_fusion.6), channel_id=1, source_target_pairs={{0,2},{1,3},{2,0},{3,1},{4,6},{5,7},{6,4},{7,5},{8,10},{9,11},{10,... | collective-permute-start | bytes 49160 | tf_op jit(solution)/shard_map/ppermute | solution.py:60
  188.1 4.2 %collective-permute-start.9 = (bf16[4,128,16]{1,2,0:T(8,128)(2,1)S(1)}, bf16[4,128,16]{1,2,0:T(8,128)(2,1)S(1)}, u32[]{:S(2)}, u32[]{:S(2)}) collective-permute-start(bf16[4,128,16]{1,2,0:T(8,128)(2,1)S(1)} %add_convert_fusion.5), channel_id=1, source_target_pairs={{0,4},{1,5},{2,6},{3,7},{4,0},{5,1},{6,2},{7,3},{8,12},{9,13},{10,... | collective-permute-start | bytes 49160 | tf_op jit(solution)/shard_map/ppermute | solution.py:60
Sparse Core Ops, SparseCore 0:
  12.7 81.0 all-gather.1
  179.9 47.6 reduce-scatter.1

commit v8 on v7

--- a/solution.py
+++ b/solution.py
@@ -157,8 +157,8 @@
     outgoing = cache_page_pool[slot_order].reshape(
         cached_count, holders, page_rows, cache_page_pool.shape[2]
     )
-    every_adapter, outgoing = lax.optimization_barrier((every_adapter, outgoing))
     arrived = lax.all_to_all(outgoing, "req", split_axis=1, concat_axis=1, tiled=True)
+    every_adapter, arrived = lax.optimization_barrier((every_adapter, arrived))
     picked = jnp.take(every_adapter, request_adapter, axis=0, mode="clip").reshape(
         request_number, -1
     )

time: 238 us -> 220 us (0.924)
  waiting for transfers between devices: 85.4 us -> 68.7 us
    all_to_all x1, waiting for transfers between devices: 21.7 us -> 0.56 us  [local(): lax.all_to_all(outgoing, 'req', split_axis=1, concat_axis=1, tiled=True)]
    ppermute x6, starting transfers between devices: 7.97 us -> 11.3 us  [sum_over_tensor(): lax.ppermute(sent, 'tensor', pairs).astype(jnp.float32)]
    reshape x0 -> x1, local copies, waits for them, and re-layouts: none -> 3.32 us  [local(): cache_page_pool[slot_order]]
    reduce_scatter x1, waiting for transfers between devices: 33.7 us -> 36.3 us  [local(): lax.psum_scatter(head_terms.astype(jnp.bfloat16), 'tensor', scatter_dimen...]
    all_gather x1, waiting for transfers between devices: 0.01 us -> 2.55 us  [local(): lax.all_gather(joined.reshape(local_adapters, lane_rows, 128), 'req', axi...]
    unnamed x65 -> x45, local copies, waits for them, and re-layouts: 9.12 us -> 7.98 us
  transfers between devices with their start and end apart: 13 -> 13, of which waited for: 9 -> 11; matrix products, arithmetic and copies ran while one was open for 32% -> 33% of each run, Pallas kernels for 0% -> 0%
where the time goes in v8:
time: 220 us; the launch traced here: 219 us
  waiting for transfers between devices  68.7 us (31%)
  local copies, waits for them, and re-layouts  37.2 us (17%)
  other arithmetic  36.9 us (17%)
  matrix products  36.1 us (16%)
  starting transfers between devices  26.4 us (12%)
  between operations  13.9 us (6%)
    reduce_scatter x1, waiting for transfers between devices, local(): lax.psum_scatter(head_terms.astype(jnp.bfloat16), 'tensor', scatter_dimen...  36.3 us
    ppermute x1, waiting for transfers between devices, local(): beside = lax.ppermute(pair, 'tensor', along)  20.5 us
    ppermute x6, starting transfers between devices, sum_over_tensor(): lax.ppermute(sent, 'tensor', pairs).astype(jnp.float32)  11.3 us
    dot_general x1, matrix products, local(): jnp.einsum('csf,cfn->sn', normed_parts, query_weight.reshape(chip_count,...  10.1 us
    dot_general x1, matrix products, local(): jnp.einsum('sc,ctf->tsf', attended, output_weight.reshape(output_weight.s...  9.11 us
    unnamed x45, local copies, waits for them, and re-layouts  7.98 us
    all_to_all x1, starting transfers between devices, local(): lax.all_to_all(outgoing, 'req', split_axis=1, concat_axis=1, tiled=True)  7.62 us
    dot_general x1, matrix products, local(): jnp.einsum('csf,cfn->sn', normed_parts, key_value_weight.reshape(chip_cou...  7.01 us
  transfers between devices with their start and end apart: 13, of which 11 were waited for; matrix products, arithmetic and copies ran while one was open for 33% of the time, Pallas kernels for 0%

profile of v8, /device:TPU:1, one launch (start us, length us, event | category | flops | bytes accessed | tf_op | source)
XLA Modules:
  0.0 219.2 jit_solution(1973719904022847794)
XLA Ops:
  6.5 1.0 copy.107
  7.6 0.9 copy.109
  8.5 0.9 copy.110
  9.4 1.1 copy.106
  10.7 0.8 bitcast_dynamic-update-slice_fusion
  11.6 0.9 copy.150
  12.6 1.5 collective-permute-start
  14.0 2.2 %collective-permute-done = bf16[512,896]{1,0:T(8,128)(2,1)} collective-permute-done((bf16[512,896]{1,0:T(8,128)(2,1)S(1)}, bf16[512,896]{1,0:T(8,128)(2,1)}, u32[]{:S(2)}, u32[]{:S(2)}) %collective-permute-start) | collective-permute-done | bytes 917536 | tf_op jit(solution)/shard_map/ppermute | solution.py:106
  16.3 3.1 %maximum_select_fusion.1 = bf16[512,1792]{1,0:T(8,128)(2,1)} fusion(bf16[512,896]{1,0:T(8,128)(2,1)} %collective-permute-done, bf16[512,896]{1,0:T(8,128)(2,1)S(1)} %copy-done.3, pred[]{:T(512)S(6)} %eq.6), kind=kLoop, calls=%fused_computation.25 | loop fusion | flops 8257536 | bytes 3670017 | tf_op jit(solution)/shard_map/jit(_where)/select_n | solution.py:107
  19.4 2.6 %collective-permute-start.1 = (bf16[512,1792]{1,0:T(8,128)(2,1)}, bf16[512,1792]{1,0:T(8,128)(2,1)}, u32[]{:S(2)}, u32[]{:S(2)}) collective-permute-start(bf16[512,1792]{1,0:T(8,128)(2,1)} %maximum_select_fusion.1), channel_id=1, source_target_pairs={{6,0},{3,1},{0,2},{5,3},{2,4},{7,5},{4,6},{1,7},{14,8},{11,9},{8,1... | collective-permute-start | bytes 5505032 | tf_op jit(solution)/shard_map/ppermute | solution.py:112
  22.0 20.5 %collective-permute-done.1 = bf16[512,1792]{1,0:T(8,128)(2,1)} collective-permute-done((bf16[512,1792]{1,0:T(8,128)(2,1)}, bf16[512,1792]{1,0:T(8,128)(2,1)}, u32[]{:S(2)}, u32[]{:S(2)}) %collective-permute-start.1) | collective-permute-done | bytes 1835040 | tf_op jit(solution)/shard_map/ppermute | solution.py:112
  42.5 2.2 constant_dynamic-slice_fusion
  44.6 3.1 %collective-permute-start.2 = (bf16[512,896]{1,0:T(8,128)(2,1)}, bf16[512,896]{1,0:T(8,128)(2,1)}, u32[]{:S(2)}, u32[]{:S(2)}) collective-permute-start(bf16[512,896]{1,0:T(8,128)(2,1)} %constant_dynamic-slice_fusion), channel_id=1, source_target_pairs={{6,0},{3,1},{0,2},{5,3},{2,4},{7,5},{4,6},{1,7},{14,8},{11,9},{8,1... | collective-permute-start | bytes 2752520 | tf_op jit(solution)/shard_map/ppermute | solution.py:113
  47.7 0.5 broadcast.416
  48.3 0.7 reduce.11
  49.2 2.1 gather_fusion.1
  51.3 3.3 %copy.68 = bf16[2,16,128,256]{3,2,0,1:T(8,128)(2,1)} copy(bf16[2,16,128,256]{3,2,1,0:T(8,128)(2,1)} %bitcast.195) | data formatting | bytes 4194304 | tf_op jit(solution)/shard_map/reshape | solution.py:157
  54.6 7.6 %all-to-all-start = ((bf16[2,16,128,256]{3,2,0,1:T(8,128)(2,1)}), bf16[2,16,128,256]{3,2,0,1:T(8,128)(2,1)S(1)}, u32[]{:S(2)}, u32[]{:S(2)}) async-start(bf16[2,16,128,256]{3,2,0,1:T(8,128)(2,1)} %copy.68), calls=%async_computation | async-start | bytes 4194304 | tf_op jit(solution)/shard_map/all_to_all | solution.py:160
  62.9 5.9 %copy.72 = bf16[4,1792,256]{1,2,0:T(8,128)(2,1)} copy(bf16[4,1792,256]{2,1,0:T(8,128)(2,1)} %bitcast.203) | data formatting | bytes 7340032 | tf_op jit(solution)/shard_map/reshape | solution.py:195
  68.9 2.0 pad_maximum_fusion.1
  71.7 1.8 multiply_cosine_fusion.1
  73.6 1.9 maximum_select_fusion
  75.5 0.7 collective-permute-done.3
  76.3 2.0 maximum_select_fusion.2
  78.3 1.7 select_bitcast_fusion.1
  80.1 3.7 %pad_maximum_fusion = bf16[4,512,1792]{2,1,0:T(8,128)(2,1)} fusion(bf16[1,512,1792]{2,1,0:T(8,128)(2,1)S(1)} %get-tuple-element.13, bf16[1,512,1792]{2,1,0:T(8,128)(2,1)S(1)} %maximum_select_fusion.2, bf16[1,512,1792]{2,1,0:T(8,128)(2,1)S(1)} %get-tuple-element.12, bf16[1,512,1792]{2,1,0:T(8,128)(2,1)S(1)} %maximum_select_fusion), kind=kLoop, calls=%fused_computation.14 | loop fusion | flops 11010048 | bytes 14680064 | tf_op jit(solution)/shard_map/stack | solution.py:126
  83.7 7.0 %gather_fusion = bf16[4,512,1792]{2,1,0:T(8,128)(2,1)} fusion(bf16[4,512,1792]{2,1,0:T(8,128)(2,1)} %pad_maximum_fusion, s32[1024]{0:T(1024)S(1)} %pad_clamp_fusion.2), kind=kCustom, calls=%fused_computation | custom fusion | bytes 14680080 | tf_op jit(solution)/shard_map/jit(_take)/gather | solution.py:128
  90.7 5.5 %fusion = f32[512]{0:T(512)S(1)} fusion(bf16[4,512,1792]{2,1,0:T(8,128)(2,1)} %gather_fusion, pred[4]{0:T(512)(128)(4,1)S(1)} %compare_and_fusion), kind=kLoop, calls=%fused_computation.5 | loop fusion | flops 14679552 | bytes 7342084 | tf_op jit(solution)/shard_map/reduce_sum | solution.py:131
  96.2 1.2 multiply_convert_fusion
  97.4 5.7 %fusion.2 = bf16[4,512,1792]{2,1,0:T(8,128)(2,1)} fusion(f32[4,1792]{1,0:T(4,128)S(1)} %mul.219, f32[512]{0:T(512)S(1)} %add_rsqrt_fusion, bf16[4,512,1792]{2,1,0:T(8,128)(2,1)S(1)} %copy-done.2, pred[4]{0:T(512)(128)(4,1)S(1)} %compare_and_fusion), kind=kLoop, calls=%fused_computation.7 | loop fusion | flops 18350080 | bytes 14710788 | tf_op jit(solution)/shard_map/convert.11
  103.1 10.1 %convolution_bitcast_fusion = f32[4,128,512]{2,1,0:T(8,128)} fusion(bf16[4,128,4,1792]{3,1,0,2:T(8,128)(2,1)} %bitcast.197, bf16[4,1792,512,1]{2,1,3,0:T(8,128)(2,1)} %bitcast.231), kind=kOutput, calls=%fused_computation.41 | convolution fusion | flops 3758096384 | bytes 15728640 | tf_op jit(solution)/shard_map/csf,cfn->sn/dot_general | solution.py:180
  113.2 0.6 all-to-all-done
  113.8 2.6 %all-gather.2.cloned.1.call-done = bf16[64,608,128]{2,1,0:T(8,128)(2,1)} async-done(((bf16[4,608,128]{2,1,0:T(8,128)(2,1)}), bf16[64,608,128]{2,1,0:T(8,128)(2,1)}) %all-gather.2.cloned.1.call-update) | async-done | bytes 9961488 | tf_op jit(solution)/shard_map/all_gather | solution.py:153
  116.3 4.5 %gather_fusion.2 = bf16[4,608,128]{2,1,0:T(8,128)(2,1)S(1)} fusion(bf16[64,608,128]{2,1,0:T(8,128)(2,1)} %all-gather.2.cloned.1.call-done, s32[1024]{0:T(1024)S(1)} %get-tuple-element.28), kind=kCustom, calls=%fused_computation.2 | custom fusion | bytes 1245200 | tf_op jit(solution)/shard_map/jit(_take)/gather | solution.py:162
  120.8 0.3 copy.149
  121.3 1.6 convolution_convert_fusion
  122.9 0.9 collective-permute-start.4
  123.8 7.0 %fusion.23 = f32[4,128,1,256]{3,1,0,2:T(8,128)} fusion(bf16[4,128,4,1792]{3,1,0,2:T(8,128)(2,1)} %bitcast.198, bf16[4,1792,256]{1,2,0:T(8,128)(2,1)} %copy.72), kind=kOutput, calls=%fused_computation.43 | convolution fusion | flops 1879048192 | bytes 11534336 | tf_op jit(solution)/shard_map/csf,cfn->sn/dot_general | solution.py:192
  130.9 1.5 collective-permute-start.5
  132.4 2.0 collective-permute-done.5
  134.5 2.8 %collective-permute-start.6 = (bf16[4,128,48]{1,2,0:T(8,128)(2,1)S(1)}, bf16[4,128,48]{1,2,0:T(8,128)(2,1)S(1)}, u32[]{:S(2)}, u32[]{:S(2)}) collective-permute-start(bf16[4,128,48]{1,2,0:T(8,128)(2,1)S(1)} %add_convert_fusion.2), channel_id=1, source_target_pairs={{0,4},{1,5},{2,6},{3,7},{4,0},{5,1},{6,2},{7,3},{8,12},{9,13},{10,... | collective-permute-start | bytes 147464 | tf_op jit(solution)/shard_map/ppermute | solution.py:60
  137.3 1.5 copy.78
  139.0 0.3 fusion.21
  139.4 0.4 reshape.689
  139.8 0.6 fusion.87
  140.4 0.3 subtract_convert_fusion
  141.0 1.0 copy-done.4
  142.0 1.5 fusion.3
  143.4 2.3 %fusion.26 = f32[2,1,1,128,4,128]{3,5,4,1,0,2:T(8,128)S(1)} fusion(f32[2,128,4,2048]{3,1,2,0:T(8,128)S(1)} %get-tuple-element.25, f32[2,128,4]{1,2,0:T(4,128)S(1)} %get-tuple-element.24, pred[2,2048]{1,0:T(4,128)(4,1)S(1)} %fusion.66, bf16[2,2048,1,256]{3,1,0,2:T(8,128)(2,1)S(1)} %bitcast.202), kind=kOutput, calls=%fused_computation.44 | convolution fusion | flops 547356672 | bytes 9973760 | tf_op jit(solution)/shard_map/bvsgk,bkvd->bvsgd/dot_general | solution.py:40
  145.7 2.2 %fusion.9 = f32[2,128,4]{1,2,0:T(4,128)S(1)} fusion(f32[2,128,4,2048]{3,1,2,0:T(8,128)S(1)} %get-tuple-element.25, f32[2,128,4]{1,2,0:T(4,128)S(1)} %get-tuple-element.24, pred[2,2048]{1,0:T(4,128)(4,1)S(1)} %fusion.66), kind=kLoop, calls=%fused_computation.17 | loop fusion | flops 10484736 | bytes 8400896 | tf_op jit(solution)/shard_map/reduce_sum | solution.py:39
  148.2 1.2 fusion.59
  149.5 0.5 fusion.89
  150.4 1.5 fusion.22
  151.9 0.3 copy.82
  152.4 9.1 %convert_bitcast_fusion = bf16[8,512,896]{2,1,0:T(8,128)(2,1)} fusion(bf16[512,512,1]{1,0,2:T(8,128)(2,1)S(1)} %reshape.739, bf16[64,8,8,896]{3,2,1,0:T(8,128)(2,1)} %bitcast.232), kind=kOutput, calls=%fused_computation.15 | convolution fusion | flops 3761766400 | bytes 15204352 | tf_op jit(solution)/shard_map/sc,ctf->tsf/dot_general | solution.py:257
  161.8 2.1 collective-permute-start.7
  163.9 0.8 collective-permute-done.7
  164.7 1.3 collective-permute-start.8
  166.0 1.4 collective-permute-done.8
  167.4 2.8 %collective-permute-start.9 = (bf16[4,128,16]{1,2,0:T(8,128)(2,1)S(1)}, bf16[4,128,16]{1,2,0:T(8,128)(2,1)S(1)}, u32[]{:S(2)}, u32[]{:S(2)}) collective-permute-start(bf16[4,128,16]{1,2,0:T(8,128)(2,1)S(1)} %add_convert_fusion.5), channel_id=1, source_target_pairs={{0,4},{1,5},{2,6},{3,7},{4,0},{5,1},{6,2},{7,3},{8,12},{9,13},{10,... | collective-permute-start | bytes 49160 | tf_op jit(solution)/shard_map/ppermute | solution.py:60
  170.2 1.4 collective-permute-done.9
  171.6 1.7 convolution_multiply_fusion
  173.3 36.3 %reduce-scatter.2.cloned.1.call-done = bf16[1,512,896]{2,1,0:T(8,128)(2,1)} async-done(((bf16[8,512,896]{2,1,0:T(8,128)(2,1)}), bf16[1,512,896]{2,1,0:T(8,128)(2,1)}) %reduce-scatter.2.cloned.1.call-update) | async-done | bytes 917520 | tf_op jit(solution)/shard_map/reduce_scatter | solution.py:270
  209.6 2.8 %fusion.16 = bf16[512,896]{1,0:T(8,128)(2,1)} fusion(f32[4,128,896]{2,1,0:T(8,128)} %convolution_multiply_fusion, bf16[1,512,896]{2,1,0:T(8,128)(2,1)} %reduce-scatter.2.cloned.1.call-done), kind=kLoop, calls=%fused_computation.28 | loop fusion | flops 1376256 | bytes 3670016 | tf_op jit(solution)/shard_map/convert_element_type | solution.py:276
  (88 shorter events, 4.0 us)
Async XLA Ops:
  6.5 42.7 %copy-start = (bf16[32,128,256]{2,1,0:T(8,128)(2,1)S(1)}, bf16[32,128,256]{2,1,0:T(8,128)(2,1)}, u32[]{:S(2)}) copy-start(bf16[32,128,256]{2,1,0:T(8,128)(2,1)} %param.31) | copy-start | bytes 6291460
  6.5 6.0 %copy-start.3 = (bf16[512,896]{1,0:T(8,128)(2,1)S(1)}, bf16[512,896]{1,0:T(8,128)(2,1)}, u32[]{:S(2)}) copy-start(bf16[512,896]{1,0:T(8,128)(2,1)} %param.16) | copy-start | bytes 2752516
  6.5 109.8 %all-gather.2.cloned.1.call-start = ((), (), s32[]{:S(2)}) async-start(), calls=%async_computation.2 | async-start | bytes 10584064 | tf_op jit(solution)/shard_map/all_gather | solution.py:153
  11.6 36.7 %copy-start.11 = (s32[1,32]{1,0:T(1,128)S(1)}, s32[1,32]{1,0:T(1,128)}, u32[]{:S(2)}) copy-start(s32[1,32]{1,0:T(1,128)} %param.30) | copy-start | bytes 388
  11.6 37.6 %copy-start.10 = (s32[4]{0:T(128)S(1)}, s32[4]{0:T(128)}, u32[]{:S(2)}) copy-start(s32[4]{0:T(128)} %param.26) | copy-start | bytes 52
  12.6 3.7 %collective-permute-start = (bf16[512,896]{1,0:T(8,128)(2,1)S(1)}, bf16[512,896]{1,0:T(8,128)(2,1)}, u32[]{:S(2)}, u32[]{:S(2)}) collective-permute-start(bf16[512,896]{1,0:T(8,128)(2,1)S(1)} %copy-done.3), channel_id=1, source_target_pairs={{0,1},{1,0},{2,3},{3,2},{4,5},{5,4},{6,7},{7,6},{8,9},{9,8},{10,11... | collective-permute-start | bytes 2752520 | tf_op jit(solution)/shard_map/ppermute | solution.py:106
  19.4 23.1 %collective-permute-start.1 = (bf16[512,1792]{1,0:T(8,128)(2,1)}, bf16[512,1792]{1,0:T(8,128)(2,1)}, u32[]{:S(2)}, u32[]{:S(2)}) collective-permute-start(bf16[512,1792]{1,0:T(8,128)(2,1)} %maximum_select_fusion.1), channel_id=1, source_target_pairs={{6,0},{3,1},{0,2},{5,3},{2,4},{7,5},{4,6},{1,7},{14,8},{11,9},{8,1... | collective-permute-start | bytes 5505032 | tf_op jit(solution)/shard_map/ppermute | solution.py:112
  44.6 24.3 %collective-permute-start.2 = (bf16[512,896]{1,0:T(8,128)(2,1)}, bf16[512,896]{1,0:T(8,128)(2,1)}, u32[]{:S(2)}, u32[]{:S(2)}) collective-permute-start(bf16[512,896]{1,0:T(8,128)(2,1)} %constant_dynamic-slice_fusion), channel_id=1, source_target_pairs={{6,0},{3,1},{0,2},{5,3},{2,4},{7,5},{4,6},{1,7},{14,8},{11,9},{8,1... | collective-permute-start | bytes 2752520 | tf_op jit(solution)/shard_map/ppermute | solution.py:113
  51.3 11.0 %copy-start.12 = (s32[32]{0:T(128)S(1)}, s32[32]{0:T(128)}, u32[]{:S(2)}) copy-start(s32[32]{0:T(128)} %param.29) | copy-start | bytes 388
  51.3 11.1 %copy-start.13 = (s32[32]{0:T(128)S(1)}, s32[32]{0:T(128)}, u32[]{:S(2)}) copy-start(s32[32]{0:T(128)} %param.28) | copy-start | bytes 388
  51.3 11.5 %copy-start.9 = (f32[7168]{0:T(1024)S(1)}, f32[7168]{0:T(1024)}, u32[]{:S(2)}) copy-start(f32[7168]{0:T(1024)} %param.17) | copy-start | bytes 86020
  54.6 59.1 %all-to-all-start = ((bf16[2,16,128,256]{3,2,0,1:T(8,128)(2,1)}), bf16[2,16,128,256]{3,2,0,1:T(8,128)(2,1)S(1)}, u32[]{:S(2)}, u32[]{:S(2)}) async-start(bf16[2,16,128,256]{3,2,0,1:T(8,128)(2,1)} %copy.68), calls=%async_computation | async-start | bytes 4194304 | tf_op jit(solution)/shard_map/all_to_all | solution.py:160
  62.3 147.3 %reduce-scatter.2.cloned.1.call-start = ((), (), s32[]{:S(2)}) async-start(), calls=%async_computation.3 | async-start | bytes 8257536 | tf_op jit(solution)/shard_map/reduce_scatter | solution.py:270
  68.9 2.4 %copy-start.14 = (s32[4]{0:T(128)S(1)}, s32[4]{0:T(128)}, u32[]{:S(2)}) copy-start(s32[4]{0:T(128)} %param.27) | copy-start | bytes 52
  70.9 5.4 %collective-permute-start.3 = (bf16[512,2688]{1,0:T(8,128)(2,1)S(1)}, bf16[512,2688]{1,0:T(8,128)(2,1)S(1)}, u32[]{:S(2)}, u32[]{:S(2)}) collective-permute-start(bf16[512,2688]{1,0:T(8,128)(2,1)S(1)} %pad_maximum_fusion.1), channel_id=1, source_target_pairs={{0,1},{1,0},{2,3},{3,2},{4,5},{5,4},{6,7},{7,6},{8,9},{9,8},{10,11... | collective-permute-start | bytes 8257544 | tf_op jit(solution)/shard_map/ppermute | solution.py:117
  90.7 6.7 %copy-start.2 = (bf16[4,512,1792]{2,1,0:T(8,128)(2,1)S(1)}, bf16[4,512,1792]{2,1,0:T(8,128)(2,1)}, u32[]{:S(2)}) copy-start(bf16[4,512,1792]{2,1,0:T(8,128)(2,1)} %gather_fusion) | copy-start | bytes 22020100
  122.9 7.9 %collective-permute-start.4 = (bf16[4,128,48]{1,2,0:T(8,128)(2,1)S(1)}, bf16[4,128,48]{1,2,0:T(8,128)(2,1)S(1)}, u32[]{:S(2)}, u32[]{:S(2)}) collective-permute-start(bf16[4,128,48]{1,2,0:T(8,128)(2,1)S(1)} %convolution_convert_fusion), channel_id=1, source_target_pairs={{0,1},{1,0},{2,3},{3,2},{4,5},{5,4},{6,7},{7,6},{8,9},{9,8},{10,11... | collective-permute-start | bytes 147464 | tf_op jit(solution)/shard_map/ppermute | solution.py:60
  130.8 8.2 %copy-start.7 = (f32[4,128,512]{2,1,0:T(8,128)S(1)}, f32[4,128,512]{2,1,0:T(8,128)}, u32[]{:S(2)}) copy-start(f32[4,128,512]{2,1,0:T(8,128)} %convolution_bitcast_fusion) | copy-start | bytes 3145732
  130.9 3.6 %collective-permute-start.5 = (bf16[4,128,48]{1,2,0:T(8,128)(2,1)S(1)}, bf16[4,128,48]{1,2,0:T(8,128)(2,1)S(1)}, u32[]{:S(2)}, u32[]{:S(2)}) collective-permute-start(bf16[4,128,48]{1,2,0:T(8,128)(2,1)S(1)} %add_convert_fusion.3), channel_id=1, source_target_pairs={{0,2},{1,3},{2,0},{3,1},{4,6},{5,7},{6,4},{7,5},{8,10},{9,11},{10,... | collective-permute-start | bytes 147464 | tf_op jit(solution)/shard_map/ppermute | solution.py:60
  134.5 4.5 %collective-permute-start.6 = (bf16[4,128,48]{1,2,0:T(8,128)(2,1)S(1)}, bf16[4,128,48]{1,2,0:T(8,128)(2,1)S(1)}, u32[]{:S(2)}, u32[]{:S(2)}) collective-permute-start(bf16[4,128,48]{1,2,0:T(8,128)(2,1)S(1)} %add_convert_fusion.2), channel_id=1, source_target_pairs={{0,4},{1,5},{2,6},{3,7},{4,0},{5,1},{6,2},{7,3},{8,12},{9,13},{10,... | collective-permute-start | bytes 147464 | tf_op jit(solution)/shard_map/ppermute | solution.py:60
  139.4 1.0 copy-start.5
  139.4 1.0 copy-start.6
  140.4 1.6 copy-start.4
  145.7 2.2 %copy-start.8 = (f32[4,128,1,256]{3,1,0,2:T(8,128)S(1)}, f32[4,128,1,256]{3,1,0,2:T(8,128)}, u32[]{:S(2)}) copy-start(f32[4,128,1,256]{3,1,0,2:T(8,128)} %fusion.23) | copy-start | bytes 1572868
  161.6 50.8 %copy-start.1 = (bf16[32,128,256]{2,1,0:T(8,128)(2,1)S(1)}, bf16[32,128,256]{2,1,0:T(8,128)(2,1)}, u32[]{:S(2)}) copy-start(bf16[32,128,256]{2,1,0:T(8,128)(2,1)} %param.31) | copy-start | bytes 6291460
  161.8 2.9 %collective-permute-start.7 = (bf16[4,128,16]{1,2,0:T(8,128)(2,1)S(1)}, bf16[4,128,16]{1,2,0:T(8,128)(2,1)S(1)}, u32[]{:S(2)}, u32[]{:S(2)}) collective-permute-start(bf16[4,128,16]{1,2,0:T(8,128)(2,1)S(1)} %convolution_convert_fusion.1), channel_id=1, source_target_pairs={{0,1},{1,0},{2,3},{3,2},{4,5},{5,4},{6,7},{7,6},{8,9},{9,8},{10,11... | collective-permute-start | bytes 49160 | tf_op jit(solution)/shard_map/ppermute | solution.py:60
  164.7 2.7 %collective-permute-start.8 = (bf16[4,128,16]{1,2,0:T(8,128)(2,1)S(1)}, bf16[4,128,16]{1,2,0:T(8,128)(2,1)S(1)}, u32[]{:S(2)}, u32[]{:S(2)}) collective-permute-start(bf16[4,128,16]{1,2,0:T(8,128)(2,1)S(1)} %add_convert_fusion.6), channel_id=1, source_target_pairs={{0,2},{1,3},{2,0},{3,1},{4,6},{5,7},{6,4},{7,5},{8,10},{9,11},{10,... | collective-permute-start | bytes 49160 | tf_op jit(solution)/shard_map/ppermute | solution.py:60
  167.4 4.2 %collective-permute-start.9 = (bf16[4,128,16]{1,2,0:T(8,128)(2,1)S(1)}, bf16[4,128,16]{1,2,0:T(8,128)(2,1)S(1)}, u32[]{:S(2)}, u32[]{:S(2)}) collective-permute-start(bf16[4,128,16]{1,2,0:T(8,128)(2,1)S(1)} %add_convert_fusion.5), channel_id=1, source_target_pairs={{0,4},{1,5},{2,6},{3,7},{4,0},{5,1},{6,2},{7,3},{8,12},{9,13},{10,... | collective-permute-start | bytes 49160 | tf_op jit(solution)/shard_map/ppermute | solution.py:60
Sparse Core Ops, SparseCore 0:
  12.7 103.5 all-gather.1
  161.7 47.8 reduce-scatter.1

commit v9 on v8

--- a/solution.py
+++ b/solution.py
@@ -104,41 +104,42 @@
         for target in range(tensor_count)
     ]
     partner = lax.ppermute(residual_input, "tensor", swap)
-    pair = jnp.where(
-        core == 0,
-        jnp.concatenate([residual_input, partner], axis=1),
-        jnp.concatenate([partner, residual_input], axis=1),
-    )
+    pair = jnp.concatenate([residual_input, partner], axis=1)
     beside = lax.ppermute(pair, "tensor", along)
-    relayed = lax.ppermute(
-        lax.dynamic_slice_in_dim(beside, core * piece_width, piece_width, 1), "tensor", along
-    )
+    relayed = lax.ppermute(beside[:, :piece_width], "tensor", along)
     held = jnp.concatenate([beside, relayed], axis=1)
     mirrored = lax.ppermute(held, "tensor", swap)
     pair_width = 2 * piece_width
-    minus_piece = jnp.where(core == 0, held[:, :pair_width], mirrored[:, :pair_width])
-    plus_piece = jnp.where(core == 0, mirrored[:, :pair_width], held[:, :pair_width])
-    opposite = jnp.where(
-        core == 0,
-        jnp.concatenate([held[:, pair_width:], mirrored[:, pair_width:]], axis=1),
-        jnp.concatenate([mirrored[:, pair_width:], held[:, pair_width:]], axis=1),
-    )
-    relative = jnp.stack([pair, plus_piece, opposite, minus_piece])
-    chip_order = (jnp.arange(chip_count, dtype=jnp.int32) - chip) % chip_count
-    gathered = jnp.take(relative, chip_order, axis=0)
-    widened = gathered.astype(jnp.float32)
-    inverse = lax.rsqrt(
-        jnp.sum(widened * widened, axis=(0, 2), keepdims=True) / (tensor_count * piece_width)
-        + EPSILON
-    )
-    normed_parts = (
-        widened * inverse * input_norm_gain.reshape(chip_count, 1, pair_width)
-    ).astype(jnp.bfloat16)
-    own_normed = (
-        residual_input.astype(jnp.float32)
-        * inverse[0]
-        * lax.dynamic_slice_in_dim(input_norm_gain, tensor_index * piece_width, piece_width, 0)
-    ).astype(jnp.bfloat16)
+    widened = jnp.concatenate(
+        [pair, held[:, :pair_width], mirrored[:, :pair_width], relayed, mirrored[:, pair_width:]],
+        axis=1,
+    ).astype(jnp.float32)
+    near = (chip - 1 + 2 * core) % chip_count
+    far = (chip + 1 - 2 * core) % chip_count
+    across = (chip + 2) % chip_count
+    block_ids = jnp.stack(
+        [
+            tensor_index,
+            tensor_index ^ 1,
+            2 * near + core,
+            2 * near + 1 - core,
+            2 * far + 1 - core,
+            2 * far + core,
+            2 * across + core,
+            2 * across + 1 - core,
+        ]
+    )
+    inverse = lax.rsqrt(jnp.mean(widened * widened, axis=1, keepdims=True) + EPSILON)
+    local_gain = jnp.take(
+        input_norm_gain.reshape(tensor_count, piece_width), block_ids, axis=0, mode="clip"
+    ).reshape(-1)
+    normed = (widened * inverse * local_gain).astype(jnp.bfloat16)
+
+    def local_rows(weight):
+        return jnp.take(
+            weight.reshape(tensor_count, piece_width, weight.shape[1]), block_ids, axis=0, mode="clip"
+        ).reshape(weight.shape)
+
     adapter_parts = (
         adapter_down_maps,
         adapter_query_up,
@@ -172,29 +173,19 @@
         start += width
     down_picked, query_picked, key_value_picked, output_down_picked, oup_sel = picked_parts
     adapter_rank_size = query_picked.shape[1]
-    own_columns = own_normed.reshape(request_number, request_slot_rows, piece_width)
+    own_columns = normed[:, :piece_width].reshape(request_number, request_slot_rows, piece_width)
     partial_low = jnp.einsum(
         "rsd,rkd->rsk", own_columns, down_picked, preferred_element_type=jnp.float32
     )
     reduced_input = sum_over_tensor(partial_low, tensor_count).astype(jnp.bfloat16)
-    query_rows = jnp.einsum(
-        "csf,cfn->sn",
-        normed_parts,
-        query_weight.reshape(chip_count, pair_width, -1),
-        preferred_element_type=jnp.float32,
-    ).reshape(request_number, request_slot_rows, -1)
+    query_rows = jnp.dot(normed, local_rows(query_weight), preferred_element_type=jnp.float32).reshape(request_number, request_slot_rows, -1)
     query_rows = query_rows + ADAPTER_SCALE * jnp.einsum(
         "ibm,imf->ibf",
         reduced_input[..., :adapter_rank_size],
         query_picked,
         preferred_element_type=jnp.float32,
     )
-    keyval = jnp.einsum(
-        "csf,cfn->sn",
-        normed_parts,
-        key_value_weight.reshape(chip_count, pair_width, -1),
-        preferred_element_type=jnp.float32,
-    ).reshape(
+    keyval = jnp.dot(normed, local_rows(key_value_weight), preferred_element_type=jnp.float32).reshape(
         request_number, request_slot_rows, local_kv, 2 * HEAD_SIZE
     )
     key_add = jnp.einsum(

time: 220 us -> 229 us (1.041)
  local copies, waits for them, and re-layouts: 37.2 us -> 60.3 us
  other arithmetic: 36.9 us -> 31.2 us
  matrix products: 36.1 us -> 31.6 us
  waiting for transfers between devices: 68.7 us -> 66 us
    unnamed x45 -> x70, local copies, waits for them, and re-layouts: 7.98 us -> 24.3 us
    convert_element_type x1 -> x2, other arithmetic: 1.22 us -> 13 us  [the longest x1 10.4 us: local(): widened = jnp.concatenate([pair, held[:, :pair_width], mirrored[:, :pair_...]
    another operation x4 -> x1, other arithmetic: 11.4 us -> 0.31 us
    slice x0 -> x5, local copies, waits for them, and re-layouts: none -> 7.51 us  [the longest x1 3.05 us: local(): mirrored[:, :pair_width]]
    select_n x4 -> x0, other arithmetic: 6.97 us -> none  [the longest x2 4.98 us: local(): jnp.where(core == 0, jnp.concatenate([residual_input, partner], axis=1),...]
    reshape x1, local copies, waits for them, and re-layouts: 5.95 us -> 0.01 us  [local(): input_norm_gain.reshape(tensor_count, piece_width)]
    dot_general x2, matrix products: 17.1 us -> 11.2 us  [the longest x1 7.19 us: local(): jnp.dot(normed, local_rows(key_value_weight), preferred_element_type=jnp....]
    gather x1 -> x3, local copies, waits for them, and re-layouts: 7 us -> 12.4 us  [the longest x2 11.9 us: local_rows(): jnp.take(weight.reshape(tensor_count, piece_width, weight.shape[1]), bloc...]
  transfers between devices with their start and end apart: 13 -> 13, of which waited for: 11 -> 8; matrix products, arithmetic and copies ran while one was open for 33% -> 34% of each run, Pallas kernels for 0% -> 0%
where the time goes in v9:
time: 229 us; the launch traced here: 228 us
  waiting for transfers between devices  66 us (29%)
  local copies, waits for them, and re-layouts  60.3 us (26%)
  matrix products  31.6 us (14%)
  other arithmetic  31.2 us (14%)
  starting transfers between devices  25.1 us (11%)
  between operations  14 us (6%)
    reduce_scatter x1, waiting for transfers between devices, local(): lax.psum_scatter(head_terms.astype(jnp.bfloat16), 'tensor', scatter_dimen...  37.5 us
    unnamed x70, local copies, waits for them, and re-layouts  24.3 us
    ppermute x1, waiting for transfers between devices, local(): beside = lax.ppermute(pair, 'tensor', along)  19.1 us
    gather x2, local copies, waits for them, and re-layouts, local_rows(): jnp.take(weight.reshape(tensor_count, piece_width, weight.shape[1]), bloc...  11.9 us
    ppermute x6, starting transfers between devices, sum_over_tensor(): lax.ppermute(sent, 'tensor', pairs).astype(jnp.float32)  10.5 us
    convert_element_type x1, other arithmetic, local(): widened = jnp.concatenate([pair, held[:, :pair_width], mirrored[:, :pair_...  10.4 us
    dot_general x1, matrix products, local(): jnp.einsum('sc,ctf->tsf', attended, output_weight.reshape(output_weight.s...  10.3 us
    all_to_all x1, starting transfers between devices, local(): lax.all_to_all(outgoing, 'req', split_axis=1, concat_axis=1, tiled=True)  7.4 us
  transfers between devices with their start and end apart: 13, of which 8 were waited for; matrix products, arithmetic and copies ran while one was open for 34% of the time, Pallas kernels for 0%

profile of v9, /device:TPU:1, one launch (start us, length us, event | category | flops | bytes accessed | tf_op | source)
XLA Modules:
  0.0 228.1 jit_solution(7012488068427495980)
XLA Ops:
  6.5 1.3 copy.96
  7.9 0.9 copy.97
  8.8 0.9 copy.99
  9.7 0.9 copy.100
  10.7 0.8 constant_dynamic-update-slice_fusion.14
  11.6 0.9 copy.140
  12.6 1.5 collective-permute-start
  14.0 2.3 %collective-permute-done = bf16[512,896]{1,0:T(8,128)(2,1)S(1)} collective-permute-done((bf16[512,896]{1,0:T(8,128)(2,1)}, bf16[512,896]{1,0:T(8,128)(2,1)S(1)}, u32[]{:S(2)}, u32[]{:S(2)}) %collective-permute-start) | collective-permute-done | bytes 917536 | tf_op jit(solution)/shard_map/ppermute | solution.py:106
  16.3 1.0 copy-done.3
  17.4 2.6 %pad_maximum_fusion.1 = bf16[512,1792]{1,0:T(8,128)(2,1)} fusion(bf16[512,896]{1,0:T(8,128)(2,1)S(1)} %collective-permute-done, bf16[512,896]{1,0:T(8,128)(2,1)} %param.16), kind=kLoop, calls=%fused_computation.24 | loop fusion | flops 3670016 | bytes 3670016 | tf_op jit(solution)/shard_map/concatenate | solution.py:107
  19.9 2.6 %collective-permute-start.1 = (bf16[512,1792]{1,0:T(8,128)(2,1)}, bf16[512,1792]{1,0:T(8,128)(2,1)}, u32[]{:S(2)}, u32[]{:S(2)}) collective-permute-start(bf16[512,1792]{1,0:T(8,128)(2,1)} %pad_maximum_fusion.1), channel_id=1, source_target_pairs={{6,0},{3,1},{0,2},{5,3},{2,4},{7,5},{4,6},{1,7},{14,8},{11,9},{8,1... | collective-permute-start | bytes 5505032 | tf_op jit(solution)/shard_map/ppermute | solution.py:108
  23.0 0.7 reduce.11
  24.0 19.1 %collective-permute-done.1 = bf16[512,1792]{1,0:T(8,128)(2,1)} collective-permute-done((bf16[512,1792]{1,0:T(8,128)(2,1)}, bf16[512,1792]{1,0:T(8,128)(2,1)}, u32[]{:S(2)}, u32[]{:S(2)}) %collective-permute-start.1) | collective-permute-done | bytes 1835040 | tf_op jit(solution)/shard_map/ppermute | solution.py:108
  43.0 2.2 slice.102
  45.2 3.1 %collective-permute-start.2 = (bf16[512,896]{1,0:T(8,128)(2,1)}, bf16[512,896]{1,0:T(8,128)(2,1)}, u32[]{:S(2)}, u32[]{:S(2)}) collective-permute-start(bf16[512,896]{1,0:T(8,128)(2,1)} %slice.102), channel_id=1, source_target_pairs={{6,0},{3,1},{0,2},{5,3},{2,4},{7,5},{4,6},{1,7},{14,8},{11,9},{8,1... | collective-permute-start | bytes 2752520 | tf_op jit(solution)/shard_map/ppermute | solution.py:109
  48.3 2.0 gather_fusion.2
  50.4 3.6 %copy.61 = bf16[2,16,128,256]{3,2,0,1:T(8,128)(2,1)} copy(bf16[2,16,128,256]{3,2,1,0:T(8,128)(2,1)} %bitcast.185) | data formatting | bytes 4194304 | tf_op jit(solution)/shard_map/reshape | solution.py:158
  54.0 7.4 %all-to-all-start = ((bf16[2,16,128,256]{3,2,0,1:T(8,128)(2,1)}), bf16[2,16,128,256]{3,2,0,1:T(8,128)(2,1)S(1)}, u32[]{:S(2)}, u32[]{:S(2)}) async-start(bf16[2,16,128,256]{3,2,0,1:T(8,128)(2,1)} %copy.61), calls=%async_computation | async-start | bytes 4194304 | tf_op jit(solution)/shard_map/all_to_all | solution.py:161
  61.7 1.1 constant_dynamic-update-slice_fusion.11
  62.7 1.1 constant_dynamic-update-slice_fusion.5
  63.8 3.6 %pad_maximum_fusion = bf16[512,2688]{1,0:T(8,128)(2,1)} fusion(bf16[512,896]{1,0:T(8,128)(2,1)} %collective-permute-done.2, bf16[512,1792]{1,0:T(8,128)(2,1)} %collective-permute-done.1), kind=kLoop, calls=%fused_computation.20 | loop fusion | flops 5505024 | bytes 5505024 | tf_op jit(solution)/shard_map/concatenate | solution.py:110
  67.6 4.7 %gather_fusion.4 = bf16[8,896,256]{2,1,0:T(8,128)(2,1)} fusion(bf16[8,896,256]{2,1,0:T(8,128)(2,1)} %bitcast.197, s32[1024]{0:T(1024)S(1)} %pad_clamp_fusion.2), kind=kCustom, calls=%fused_computation.4 | custom fusion | bytes 7340064 | tf_op jit(solution)/shard_map/jit(_take)/gather | solution.py:139
  72.3 0.6 gather_fusion
  73.1 7.2 %gather_fusion.1 = bf16[8,896,512]{2,1,0:T(8,128)(2,1)} fusion(bf16[8,896,512]{2,1,0:T(8,128)(2,1)} %bitcast.188, s32[1024]{0:T(1024)S(1)} %pad_clamp_fusion.2), kind=kCustom, calls=%fused_computation.1 | custom fusion | bytes 14680096 | tf_op jit(solution)/shard_map/jit(_take)/gather | solution.py:139
  80.8 1.8 multiply_cosine_fusion.1
  82.7 1.1 constant_dynamic-update-slice_fusion.4
  83.9 1.0 constant_dynamic-update-slice_fusion.10
  84.9 2.9 %constant_dynamic-update-slice_fusion.3 = bf16[4,128,7168]{2,1,0:T(8,128)(2,1)} fusion(bf16[4,128,7168]{2,1,0:T(8,128)(2,1)} %constant_dynamic-update-slice_fusion.4, bf16[4,128,1792]{2,1,0:T(8,128)(2,1)} %bitcast.2), kind=kLoop, calls=%fused_computation.100 | loop fusion | bytes 3670016
  87.8 2.9 %constant_dynamic-update-slice_fusion.9 = bf16[512,7168]{1,0:T(8,128)(2,1)} fusion(bf16[512,7168]{1,0:T(8,128)(2,1)} %constant_dynamic-update-slice_fusion.10, bf16[512,1792]{1,0:T(8,128)(2,1)} %collective-permute-done.1), kind=kLoop, calls=%fused_computation.106 | loop fusion | bytes 3670016
  90.7 3.0 %fusion.81 = (bf16[512,1792]{1,0:T(8,128)(2,1)S(1)}, bf16[512,7168]{1,0:T(8,128)(2,1)}) fusion(bf16[512,2688]{1,0:T(8,128)(2,1)} %collective-permute-done.3, bf16[512,7168]{1,0:T(8,128)(2,1)} %constant_dynamic-update-slice_fusion.9), kind=kLoop, calls=%fused_computation.154 | loop fusion | bytes 5505024 | tf_op jit(solution)/shard_map/slice | solution.py:114
  93.8 2.2 constant_dynamic-update-slice_fusion.7
  96.0 2.3 %fusion.80 = (bf16[512,896]{1,0:T(8,128)(2,1)S(1)}, bf16[512,7168]{1,0:T(8,128)(2,1)}) fusion(bf16[512,2688]{1,0:T(8,128)(2,1)} %collective-permute-done.3, bf16[512,7168]{1,0:T(8,128)(2,1)} %constant_dynamic-update-slice_fusion.7), kind=kLoop, calls=%fused_computation.153 | loop fusion | bytes 2752512 | tf_op jit(solution)/shard_map/slice | solution.py:114
  98.3 10.4 %convert_element_type.149 = f32[512,7168]{1,0:T(8,128)} convert(bf16[512,7168]{1,0:T(8,128)(2,1)} %get-tuple-element.13) | non-fusion elementwise | flops 3670016 | bytes 22020096 | tf_op jit(solution)/shard_map/convert_element_type | solution.py:116
  108.7 1.4 constant_dynamic-update-slice_fusion.2
  110.1 2.3 constant_dynamic-update-slice_fusion.1
  112.3 1.0 constant_dynamic-update-slice_fusion
  113.4 1.5 multiply_reduce_fusion
  114.9 2.6 %fusion.14 = bf16[512,896]{1,0:T(8,128)(2,1)} fusion(f32[512,7168]{1,0:T(8,128)} %convert_element_type.149, f32[896]{0:T(1024)S(1)} %slice-done.6, f32[512]{0:T(512)S(1)} %get-tuple-element.27), kind=kLoop, calls=%fused_computation.23 | loop fusion | flops 1376256 | bytes 2758144 | tf_op jit(solution)/shard_map/convert_element_type | solution.py:136
  117.5 4.5 %gather_fusion.3 = bf16[4,608,128]{2,1,0:T(8,128)(2,1)S(1)} fusion(bf16[64,608,128]{2,1,0:T(8,128)(2,1)} %all-gather.2.cloned.1.call-done, s32[1024]{0:T(1024)S(1)} %get-tuple-element.32), kind=kCustom, calls=%fused_computation.3 | custom fusion | bytes 1245200 | tf_op jit(solution)/shard_map/jit(_take)/gather | solution.py:163
  122.5 1.8 convolution_convert_fusion
  124.3 1.1 collective-permute-start.4
  125.4 7.2 %fusion.25 = f32[4,128,1,256]{3,1,0,2:T(8,128)} fusion(bf16[7168,256,1]{1,0,2:T(8,128)(2,1)} %bitcast.198, bf16[4,128,7168]{2,1,0:T(8,128)(2,1)} %constant_dynamic-update-slice_fusion, f32[7168]{0:T(1024)S(1)} %copy-done.10, f32[4,128]{1,0:T(4,128)S(1)} %get-tuple-element.26), kind=kOutput, calls=%fused_computation.38 | convolution fusion | flops 1893728256 | bytes 11565056 | tf_op jit(solution)/shard_map/dot_general | solution.py:188
  132.6 1.0 collective-permute-start.5
  133.7 1.9 collective-permute-done.5
  135.7 2.9 %collective-permute-start.6 = (bf16[4,128,48]{1,2,0:T(8,128)(2,1)S(1)}, bf16[4,128,48]{1,2,0:T(8,128)(2,1)S(1)}, u32[]{:S(2)}, u32[]{:S(2)}) collective-permute-start(bf16[4,128,48]{1,2,0:T(8,128)(2,1)S(1)} %add_convert_fusion.2), channel_id=1, source_target_pairs={{0,4},{1,5},{2,6},{3,7},{4,0},{5,1},{6,2},{7,3},{8,12},{9,13},{10,... | collective-permute-start | bytes 147464 | tf_op jit(solution)/shard_map/ppermute | solution.py:60
  138.6 1.5 copy.70
  140.6 4.0 %fusion.20 = f32[4,128,512]{2,1,0:T(8,128)S(1)} fusion(f32[4,128,512]{2,1,0:T(8,128)S(1)} %convolution_multiply_fusion.3, bf16[7168,512,1]{1,0,2:T(8,128)(2,1)S(1)} %bitcast.191, bf16[4,128,7168]{2,1,0:T(8,128)(2,1)S(1)} %bitcast.219, f32[7168]{0:T(1024)S(1)} %copy-done.10, f32[4,128]{1,0:T(4,128)S(1)} %get-tuple-element.26), kind=kOutput, calls=%fused_computation.35 | convolution fusion | flops 3773038592 | bytes 16807936 | tf_op jit(solution)/shard_map/dot_general | solution.py:181
  145.1 0.6 fusion.82
  146.6 1.5 fusion
  148.1 2.4 %fusion.6 = f32[2,128,4]{1,2,0:T(4,128)S(1)} fusion(f32[2,128,4,2048]{3,1,2,0:T(8,128)S(1)} %get-tuple-element.29, f32[2,128,4]{1,2,0:T(4,128)S(1)} %get-tuple-element.28, pred[2,2048]{1,0:T(4,128)(4,1)S(1)} %fusion.61), kind=kLoop, calls=%fused_computation.14 | loop fusion | flops 10484736 | bytes 8400896 | tf_op jit(solution)/shard_map/reduce_sum | solution.py:39
  150.5 2.3 fusion.22
  153.1 1.2 fusion.54
  155.3 1.5 fusion.21
  157.1 1.0 reshape.703
  158.1 10.3 %convert_bitcast_fusion = bf16[8,512,896]{2,1,0:T(8,128)(2,1)} fusion(bf16[512,512,1]{1,0,2:T(8,128)(2,1)} %reshape.703, bf16[64,8,8,896]{3,2,1,0:T(8,128)(2,1)} %bitcast.229), kind=kOutput, calls=%fused_computation.13 | convolution fusion | flops 3761766400 | bytes 15204352 | tf_op jit(solution)/shard_map/sc,ctf->tsf/dot_general | solution.py:248
  168.6 2.9 %collective-permute-start.7 = (bf16[4,128,16]{1,2,0:T(8,128)(2,1)S(1)}, bf16[4,128,16]{1,2,0:T(8,128)(2,1)S(1)}, u32[]{:S(2)}, u32[]{:S(2)}) collective-permute-start(bf16[4,128,16]{1,2,0:T(8,128)(2,1)S(1)} %convolution_convert_fusion.1), channel_id=1, source_target_pairs={{0,1},{1,0},{2,3},{3,2},{4,5},{5,4},{6,7},{7,6},{8,9},{9,8},{10,11... | collective-permute-start | bytes 49160 | tf_op jit(solution)/shard_map/ppermute | solution.py:60
  171.5 0.8 collective-permute-done.7
  172.3 0.6 collective-permute-start.8
  172.9 2.1 collective-permute-done.8
  175.0 2.0 collective-permute-start.9
  177.1 2.1 collective-permute-done.9
  179.2 1.8 convolution_multiply_fusion
  180.9 37.5 %reduce-scatter.2.cloned.1.call-done = bf16[1,512,896]{2,1,0:T(8,128)(2,1)} async-done(((bf16[8,512,896]{2,1,0:T(8,128)(2,1)}), bf16[1,512,896]{2,1,0:T(8,128)(2,1)}) %reduce-scatter.2.cloned.1.call-update) | async-done | bytes 917520 | tf_op jit(solution)/shard_map/reduce_scatter | solution.py:261
  218.5 2.8 %fusion.15 = bf16[512,896]{1,0:T(8,128)(2,1)} fusion(f32[4,128,896]{2,1,0:T(8,128)} %convolution_multiply_fusion, bf16[1,512,896]{2,1,0:T(8,128)(2,1)} %reduce-scatter.2.cloned.1.call-done), kind=kLoop, calls=%fused_computation.26 | loop fusion | flops 1376256 | bytes 3670016 | tf_op jit(solution)/shard_map/convert_element_type | solution.py:267
  (116 shorter events, 6.4 us)
Async XLA Ops:
  6.5 41.8 %copy-start = (bf16[32,128,256]{2,1,0:T(8,128)(2,1)S(1)}, bf16[32,128,256]{2,1,0:T(8,128)(2,1)}, u32[]{:S(2)}) copy-start(bf16[32,128,256]{2,1,0:T(8,128)(2,1)} %param.31) | copy-start | bytes 6291460
  6.5 16.5 %copy-start.13 = (s32[1,32]{1,0:T(1,128)S(1)}, s32[1,32]{1,0:T(1,128)}, u32[]{:S(2)}) copy-start(s32[1,32]{1,0:T(1,128)} %param.30) | copy-start | bytes 388
  6.5 41.8 %copy-start.12 = (s32[4]{0:T(128)S(1)}, s32[4]{0:T(128)}, u32[]{:S(2)}) copy-start(s32[4]{0:T(128)} %param.26) | copy-start | bytes 52
  6.5 111.0 %all-gather.2.cloned.1.call-start = ((), (), s32[]{:S(2)}) async-start(), calls=%async_computation.2 | async-start | bytes 10584064 | tf_op jit(solution)/shard_map/all_gather | solution.py:154
  12.6 3.8 %collective-permute-start = (bf16[512,896]{1,0:T(8,128)(2,1)}, bf16[512,896]{1,0:T(8,128)(2,1)S(1)}, u32[]{:S(2)}, u32[]{:S(2)}) collective-permute-start(bf16[512,896]{1,0:T(8,128)(2,1)} %param.16), channel_id=1, source_target_pairs={{0,1},{1,0},{2,3},{3,2},{4,5},{5,4},{6,7},{7,6},{8,9},{9,8},{10,11... | collective-permute-start | bytes 2752520 | tf_op jit(solution)/shard_map/ppermute | solution.py:106
  16.3 1.0 copy-start.3
  19.9 41.7 %copy-start.2 = (bf16[512,896]{1,0:T(8,128)(2,1)S(1)}, bf16[512,896]{1,0:T(8,128)(2,1)}, u32[]{:S(2)}) copy-start(bf16[512,896]{1,0:T(8,128)(2,1)} %param.16) | copy-start | bytes 2752516
  19.9 23.1 %collective-permute-start.1 = (bf16[512,1792]{1,0:T(8,128)(2,1)}, bf16[512,1792]{1,0:T(8,128)(2,1)}, u32[]{:S(2)}, u32[]{:S(2)}) collective-permute-start(bf16[512,1792]{1,0:T(8,128)(2,1)} %pad_maximum_fusion.1), channel_id=1, source_target_pairs={{6,0},{3,1},{0,2},{5,3},{2,4},{7,5},{4,6},{1,7},{14,8},{11,9},{8,1... | collective-permute-start | bytes 5505032 | tf_op jit(solution)/shard_map/ppermute | solution.py:108
  45.2 18.6 %collective-permute-start.2 = (bf16[512,896]{1,0:T(8,128)(2,1)}, bf16[512,896]{1,0:T(8,128)(2,1)}, u32[]{:S(2)}, u32[]{:S(2)}) collective-permute-start(bf16[512,896]{1,0:T(8,128)(2,1)} %slice.102), channel_id=1, source_target_pairs={{6,0},{3,1},{0,2},{5,3},{2,4},{7,5},{4,6},{1,7},{14,8},{11,9},{8,1... | collective-permute-start | bytes 2752520 | tf_op jit(solution)/shard_map/ppermute | solution.py:109
  54.0 13.4 %copy-start.14 = (s32[32]{0:T(128)S(1)}, s32[32]{0:T(128)}, u32[]{:S(2)}) copy-start(s32[32]{0:T(128)} %param.28) | copy-start | bytes 388
  54.0 13.6 %copy-start.11 = (f32[7168]{0:T(1024)S(1)}, f32[7168]{0:T(1024)}, u32[]{:S(2)}) copy-start(f32[7168]{0:T(1024)} %param.17) | copy-start | bytes 86020
  54.0 63.6 %all-to-all-start = ((bf16[2,16,128,256]{3,2,0,1:T(8,128)(2,1)}), bf16[2,16,128,256]{3,2,0,1:T(8,128)(2,1)S(1)}, u32[]{:S(2)}, u32[]{:S(2)}) async-start(bf16[2,16,128,256]{3,2,0,1:T(8,128)(2,1)} %copy.61), calls=%async_computation | async-start | bytes 4194304 | tf_op jit(solution)/shard_map/all_to_all | solution.py:161
  61.4 157.1 %reduce-scatter.2.cloned.1.call-start = ((), (), s32[]{:S(2)}) async-start(), calls=%async_computation.3 | async-start | bytes 8257536 | tf_op jit(solution)/shard_map/reduce_scatter | solution.py:261
  67.4 23.3 %collective-permute-start.3 = (bf16[512,2688]{1,0:T(8,128)(2,1)}, bf16[512,2688]{1,0:T(8,128)(2,1)}, u32[]{:S(2)}, u32[]{:S(2)}) collective-permute-start(bf16[512,2688]{1,0:T(8,128)(2,1)} %pad_maximum_fusion), channel_id=1, source_target_pairs={{0,1},{1,0},{2,3},{3,2},{4,5},{5,4},{6,7},{7,6},{8,9},{9,8},{10,11... | collective-permute-start | bytes 8257544 | tf_op jit(solution)/shard_map/ppermute | solution.py:111
  72.8 7.5 %copy-start.9 = (f32[7168]{0:T(1024)}, f32[7168]{0:T(1024)S(1)}, u32[]{:S(2)}) copy-start(f32[7168]{0:T(1024)S(1)} %mul.232) | copy-start | bytes 86020
  73.1 7.2 %copy-start.15 = (s32[32]{0:T(128)S(1)}, s32[32]{0:T(128)}, u32[]{:S(2)}) copy-start(s32[32]{0:T(128)} %param.29) | copy-start | bytes 388
  73.1 7.3 %copy-start.16 = (s32[4]{0:T(128)S(1)}, s32[4]{0:T(128)}, u32[]{:S(2)}) copy-start(s32[4]{0:T(128)} %param.27) | copy-start | bytes 52
  73.1 9.6 %copy-start.4 = (bf16[512,896]{1,0:T(8,128)(2,1)S(1)}, bf16[512,896]{1,0:T(8,128)(2,1)}, u32[]{:S(2)}) copy-start(bf16[512,896]{1,0:T(8,128)(2,1)} %copy-done.3) | copy-start | bytes 2752516
  98.3 15.1 %slice-start = ((s8[7340032]{0:T(1024)(128)(4,1)}), s8[4194304]{0:T(1024)(128)(4,1)S(1)}, s32[]{:S(2)}) async-start(s8[7340032]{0:T(1024)(128)(4,1)} %bitcast.183), calls=%async_computation.4 | async-start | bytes 8388608
  98.3 15.1 %slice-start.1 = ((s8[7340032]{0:T(1024)(128)(4,1)}), s8[3145728]{0:T(1024)(128)(4,1)S(1)}, s32[]{:S(2)}) async-start(s8[7340032]{0:T(1024)(128)(4,1)} %bitcast.183), calls=%async_computation.5 | async-start | bytes 6291456
  108.7 6.2 %slice-start.6 = ((f32[7168]{0:T(1024)}), f32[896]{0:T(1024)S(1)}, s32[]{:S(2)}) async-start(f32[7168]{0:T(1024)} %copy-done.9), calls=%async_computation.10 | async-start | bytes 8192 | tf_op jit(solution)/shard_map/slice | solution.py:176
  113.4 12.0 %copy-start.10 = (f32[7168]{0:T(1024)S(1)}, f32[7168]{0:T(1024)}, u32[]{:S(2)}) copy-start(f32[7168]{0:T(1024)} %copy-done.9) | copy-start | bytes 86020
  122.5 18.0 %slice-start.2 = ((s8[7340032]{0:T(1024)(128)(4,1)}), s8[4194304]{0:T(1024)(128)(4,1)S(1)}, s32[]{:S(2)}) async-start(s8[7340032]{0:T(1024)(128)(4,1)} %bitcast.189), calls=%async_computation.6 | async-start | bytes 8388608
  122.5 18.0 %slice-start.4 = ((s8[7340032]{0:T(1024)(128)(4,1)}), s8[4194304]{0:T(1024)(128)(4,1)S(1)}, s32[]{:S(2)}) async-start(s8[7340032]{0:T(1024)(128)(4,1)} %bitcast.218), calls=%async_computation.8 | async-start | bytes 8388608
  124.3 8.3 %collective-permute-start.4 = (bf16[4,128,48]{1,2,0:T(8,128)(2,1)S(1)}, bf16[4,128,48]{1,2,0:T(8,128)(2,1)S(1)}, u32[]{:S(2)}, u32[]{:S(2)}) collective-permute-start(bf16[4,128,48]{1,2,0:T(8,128)(2,1)S(1)} %convolution_convert_fusion), channel_id=1, source_target_pairs={{0,1},{1,0},{2,3},{3,2},{4,5},{5,4},{6,7},{7,6},{8,9},{9,8},{10,11... | collective-permute-start | bytes 147464 | tf_op jit(solution)/shard_map/ppermute | solution.py:60
  125.4 15.2 %slice-start.3 = ((s8[7340032]{0:T(1024)(128)(4,1)}), s8[3145728]{0:T(1024)(128)(4,1)S(1)}, s32[]{:S(2)}) async-start(s8[7340032]{0:T(1024)(128)(4,1)} %bitcast.189), calls=%async_computation.7 | async-start | bytes 6291456
  125.4 15.2 %slice-start.5 = ((s8[7340032]{0:T(1024)(128)(4,1)}), s8[3145728]{0:T(1024)(128)(4,1)S(1)}, s32[]{:S(2)}) async-start(s8[7340032]{0:T(1024)(128)(4,1)} %bitcast.218), calls=%async_computation.9 | async-start | bytes 6291456
  132.6 3.0 %collective-permute-start.5 = (bf16[4,128,48]{1,2,0:T(8,128)(2,1)S(1)}, bf16[4,128,48]{1,2,0:T(8,128)(2,1)S(1)}, u32[]{:S(2)}, u32[]{:S(2)}) collective-permute-start(bf16[4,128,48]{1,2,0:T(8,128)(2,1)S(1)} %add_convert_fusion.3), channel_id=1, source_target_pairs={{0,2},{1,3},{2,0},{3,1},{4,6},{5,7},{6,4},{7,5},{8,10},{9,11},{10,... | collective-permute-start | bytes 147464 | tf_op jit(solution)/shard_map/ppermute | solution.py:60
  135.7 4.5 %collective-permute-start.6 = (bf16[4,128,48]{1,2,0:T(8,128)(2,1)S(1)}, bf16[4,128,48]{1,2,0:T(8,128)(2,1)S(1)}, u32[]{:S(2)}, u32[]{:S(2)}) collective-permute-start(bf16[4,128,48]{1,2,0:T(8,128)(2,1)S(1)} %add_convert_fusion.2), channel_id=1, source_target_pairs={{0,4},{1,5},{2,6},{3,7},{4,0},{5,1},{6,2},{7,3},{8,12},{9,13},{10,... | collective-permute-start | bytes 147464 | tf_op jit(solution)/shard_map/ppermute | solution.py:60
  140.6 5.1 %copy-start.6 = (f32[4,128,64]{2,1,0:T(8,128)S(1)}, f32[4,128,64]{2,1,0:T(8,128)}, u32[]{:S(2)}) copy-start(f32[4,128,64]{2,1,0:T(8,128)} %get-tuple-element.24) | copy-start | bytes 393220
  140.6 5.1 %copy-start.7 = (f32[4,128,64]{2,1,0:T(8,128)S(1)}, f32[4,128,64]{2,1,0:T(8,128)}, u32[]{:S(2)}) copy-start(f32[4,128,64]{2,1,0:T(8,128)} %get-tuple-element.25) | copy-start | bytes 393220
  145.0 1.6 copy-start.5
  150.5 2.3 %copy-start.8 = (f32[4,128,1,256]{3,1,0,2:T(8,128)S(1)}, f32[4,128,1,256]{3,1,0,2:T(8,128)}, u32[]{:S(2)}) copy-start(f32[4,128,1,256]{3,1,0,2:T(8,128)} %fusion.25) | copy-start | bytes 1572868
  158.1 63.2 %copy-start.1 = (bf16[32,128,256]{2,1,0:T(8,128)(2,1)S(1)}, bf16[32,128,256]{2,1,0:T(8,128)(2,1)}, u32[]{:S(2)}) copy-start(bf16[32,128,256]{2,1,0:T(8,128)(2,1)} %param.31) | copy-start | bytes 6291460
  168.6 3.7 %collective-permute-start.7 = (bf16[4,128,16]{1,2,0:T(8,128)(2,1)S(1)}, bf16[4,128,16]{1,2,0:T(8,128)(2,1)S(1)}, u32[]{:S(2)}, u32[]{:S(2)}) collective-permute-start(bf16[4,128,16]{1,2,0:T(8,128)(2,1)S(1)} %convolution_convert_fusion.1), channel_id=1, source_target_pairs={{0,1},{1,0},{2,3},{3,2},{4,5},{5,4},{6,7},{7,6},{8,9},{9,8},{10,11... | collective-permute-start | bytes 49160 | tf_op jit(solution)/shard_map/ppermute | solution.py:60
  172.3 2.7 %collective-permute-start.8 = (bf16[4,128,16]{1,2,0:T(8,128)(2,1)S(1)}, bf16[4,128,16]{1,2,0:T(8,128)(2,1)S(1)}, u32[]{:S(2)}, u32[]{:S(2)}) collective-permute-start(bf16[4,128,16]{1,2,0:T(8,128)(2,1)S(1)} %add_convert_fusion.6), channel_id=1, source_target_pairs={{0,2},{1,3},{2,0},{3,1},{4,6},{5,7},{6,4},{7,5},{8,10},{9,11},{10,... | collective-permute-start | bytes 49160 | tf_op jit(solution)/shard_map/ppermute | solution.py:60
  175.0 4.2 %collective-permute-start.9 = (bf16[4,128,16]{1,2,0:T(8,128)(2,1)S(1)}, bf16[4,128,16]{1,2,0:T(8,128)(2,1)S(1)}, u32[]{:S(2)}, u32[]{:S(2)}) collective-permute-start(bf16[4,128,16]{1,2,0:T(8,128)(2,1)S(1)} %add_convert_fusion.5), channel_id=1, source_target_pairs={{0,4},{1,5},{2,6},{3,7},{4,0},{5,1},{6,2},{7,3},{8,12},{9,13},{10,... | collective-permute-start | bytes 49160 | tf_op jit(solution)/shard_map/ppermute | solution.py:60
Sparse Core Ops, SparseCore 0:
  12.7 103.5 all-gather.1
  168.5 49.9 reduce-scatter.1

commit v10 on v8

--- a/solution.py
+++ b/solution.py
@@ -267,8 +267,18 @@
         preferred_element_type=jnp.float32,
     )
     reduced_output = sum_over_tensor(low_part, tensor_count).astype(jnp.bfloat16)
+    by_chip = head_terms.astype(jnp.bfloat16).reshape(
+        (chip_count, 2) + head_terms.shape[1:]
+    )
+    kept = lax.dynamic_index_in_dim(by_chip, core, 1, keepdims=False)
+    given = lax.dynamic_index_in_dim(by_chip, 1 - core, 1, keepdims=False)
+    chip_total = (
+        kept.astype(jnp.float32)
+        + lax.ppermute(given, "tensor", swap).astype(jnp.float32)
+    ).astype(jnp.bfloat16)
+    same_core = [list(range(side, tensor_count, 2)) for side in range(2)]
     head_total = lax.psum_scatter(
-        head_terms.astype(jnp.bfloat16), "tensor", scatter_dimension=0, tiled=False
+        chip_total, "tensor", scatter_dimension=0, axis_index_groups=same_core, tiled=False
     ).astype(jnp.float32)
     adapter_output = jnp.einsum(
         "ibm,imf->ibf", reduced_output, oup_sel, preferred_element_type=jnp.float32

time: 220 us -> 231 us (1.050)
  other arithmetic: 36.9 us -> 44.7 us
  local copies, waits for them, and re-layouts: 37.2 us -> 42.6 us
    ppermute x0 -> x1, waiting for transfers between devices: none -> 6.38 us  [local(): lax.ppermute(given, 'tensor', swap).astype(jnp.float32)]
    convert_element_type x0 -> x1, other arithmetic: none -> 5.96 us  [local(): chip_total = (kept.astype(jnp.float32) + lax.ppermute(given, 'tensor', sw...]
    reduce_scatter x1, waiting for transfers between devices: 36.3 us -> 32 us  [local(): lax.psum_scatter(chip_total, 'tensor', scatter_dimension=0, axis_index_gr...]
    squeeze x0 -> x1, local copies, waits for them, and re-layouts: none -> 2.42 us  [local(): given = lax.dynamic_index_in_dim(by_chip, 1 - core, 1, keepdims=False)]
    unnamed x45 -> x47, local copies, waits for them, and re-layouts: 7.98 us -> 9.74 us
  transfers between devices with their start and end apart: 13 -> 14, of which waited for: 11 -> 10; matrix products, arithmetic and copies ran while one was open for 33% -> 33% of each run, Pallas kernels for 0% -> 0%
where the time goes in v10:
time: 231 us; the launch traced here: 230 us
  waiting for transfers between devices  68 us (29%)
  other arithmetic  44.7 us (19%)
  local copies, waits for them, and re-layouts  42.6 us (18%)
  matrix products  34.3 us (15%)
  starting transfers between devices  26.5 us (11%)
  between operations  13.9 us (6%)
    reduce_scatter x1, waiting for transfers between devices, local(): lax.psum_scatter(chip_total, 'tensor', scatter_dimension=0, axis_index_gr...  32 us
    ppermute x1, waiting for transfers between devices, local(): beside = lax.ppermute(pair, 'tensor', along)  20.5 us
    dot_general x1, matrix products, local(): jnp.einsum('csf,cfn->sn', normed_parts, query_weight.reshape(chip_count,...  10.1 us
    unnamed x47, local copies, waits for them, and re-layouts  9.74 us
    ppermute x6, starting transfers between devices, sum_over_tensor(): lax.ppermute(sent, 'tensor', pairs).astype(jnp.float32)  9.69 us
    all_to_all x1, starting transfers between devices, local(): lax.all_to_all(outgoing, 'req', split_axis=1, concat_axis=1, tiled=True)  7.59 us
    dot_general x1, matrix products, local(): jnp.einsum('sc,ctf->tsf', attended, output_weight.reshape(output_weight.s...  7.28 us
    dot_general x1, matrix products, local(): jnp.einsum('csf,cfn->sn', normed_parts, key_value_weight.reshape(chip_cou...  7.01 us
  transfers between devices with their start and end apart: 14, of which 10 were waited for; matrix products, arithmetic and copies ran while one was open for 33% of the time, Pallas kernels for 0%

profile of v10, /device:TPU:1, one launch (start us, length us, event | category | flops | bytes accessed | tf_op | source)
XLA Modules:
  0.0 230.0 jit_solution(3996382124019430044)
XLA Ops:
  6.5 1.0 copy.112
  7.6 0.9 copy.114
  8.5 0.9 copy.115
  9.4 1.1 copy.111
  10.7 0.8 bitcast_dynamic-update-slice_fusion
  11.6 0.9 copy.155
  12.6 1.5 collective-permute-start
  14.0 2.2 collective-permute-done
  16.3 3.1 %maximum_select_fusion.1 = bf16[512,1792]{1,0:T(8,128)(2,1)} fusion(bf16[512,896]{1,0:T(8,128)(2,1)} %collective-permute-done, bf16[512,896]{1,0:T(8,128)(2,1)S(1)} %copy-done.3, pred[]{:T(512)S(6)} %eq.6), kind=kLoop, calls=%fused_computation.28 | loop fusion | flops 8257536 | bytes 3670017 | tf_op jit(solution)/shard_map/jit(_where)/select_n | solution.py:107
  19.4 2.6 %collective-permute-start.1 = (bf16[512,1792]{1,0:T(8,128)(2,1)}, bf16[512,1792]{1,0:T(8,128)(2,1)}, u32[]{:S(2)}, u32[]{:S(2)}) collective-permute-start(bf16[512,1792]{1,0:T(8,128)(2,1)} %maximum_select_fusion.1), channel_id=1, source_target_pairs={{6,0},{3,1},{0,2},{5,3},{2,4},{7,5},{4,6},{1,7},{14,8},{11,9},{8,1... | collective-permute-start | bytes 5505032 | tf_op jit(solution)/shard_map/ppermute | solution.py:112
  22.0 20.5 %collective-permute-done.1 = bf16[512,1792]{1,0:T(8,128)(2,1)} collective-permute-done((bf16[512,1792]{1,0:T(8,128)(2,1)}, bf16[512,1792]{1,0:T(8,128)(2,1)}, u32[]{:S(2)}, u32[]{:S(2)}) %collective-permute-start.1) | collective-permute-done | bytes 1835040 | tf_op jit(solution)/shard_map/ppermute | solution.py:112
  42.4 2.2 constant_dynamic-slice_fusion
  44.6 3.1 %collective-permute-start.2 = (bf16[512,896]{1,0:T(8,128)(2,1)}, bf16[512,896]{1,0:T(8,128)(2,1)}, u32[]{:S(2)}, u32[]{:S(2)}) collective-permute-start(bf16[512,896]{1,0:T(8,128)(2,1)} %constant_dynamic-slice_fusion), channel_id=1, source_target_pairs={{6,0},{3,1},{0,2},{5,3},{2,4},{7,5},{4,6},{1,7},{14,8},{11,9},{8,1... | collective-permute-start | bytes 2752520 | tf_op jit(solution)/shard_map/ppermute | solution.py:113
  47.7 0.5 broadcast.416
  48.2 0.6 reduce.11
  49.1 2.1 gather_fusion.1
  51.2 3.4 %copy.71 = bf16[2,16,128,256]{3,2,0,1:T(8,128)(2,1)} copy(bf16[2,16,128,256]{3,2,1,0:T(8,128)(2,1)} %bitcast.203) | data formatting | bytes 4194304 | tf_op jit(solution)/shard_map/reshape | solution.py:157
  54.6 7.6 %all-to-all-start = ((bf16[2,16,128,256]{3,2,0,1:T(8,128)(2,1)}), bf16[2,16,128,256]{3,2,0,1:T(8,128)(2,1)S(1)}, u32[]{:S(2)}, u32[]{:S(2)}) async-start(bf16[2,16,128,256]{3,2,0,1:T(8,128)(2,1)} %copy.71), calls=%async_computation | async-start | bytes 4194304 | tf_op jit(solution)/shard_map/all_to_all | solution.py:160
  62.4 3.5 %pad_maximum_fusion.1 = bf16[512,2688]{1,0:T(8,128)(2,1)} fusion(bf16[512,896]{1,0:T(8,128)(2,1)} %collective-permute-done.2, bf16[512,1792]{1,0:T(8,128)(2,1)} %collective-permute-done.1), kind=kLoop, calls=%fused_computation.26 | loop fusion | flops 5505024 | bytes 5505024 | tf_op jit(solution)/shard_map/concatenate | solution.py:116
  66.3 5.9 %copy.75 = bf16[4,1792,256]{1,2,0:T(8,128)(2,1)} copy(bf16[4,1792,256]{2,1,0:T(8,128)(2,1)} %bitcast.213) | data formatting | bytes 7340032 | tf_op jit(solution)/shard_map/reshape | solution.py:195
  72.8 1.8 multiply_cosine_fusion.1
  74.7 1.9 maximum_select_fusion
  76.6 1.3 slice_bitcast_fusion.4
  77.9 1.9 maximum_select_fusion.2
  79.8 2.4 %select_bitcast_fusion.1 = (bf16[1,512,1792]{2,1,0:T(8,128)(2,1)S(1)}, bf16[1,512,1792]{2,1,0:T(8,128)(2,1)S(1)}) fusion(bf16[512,1792]{1,0:T(8,128)(2,1)} %collective-permute-done.1, pred[]{:T(512)S(6)} %eq.6, bf16[512,2688]{1,0:T(8,128)(2,1)} %collective-permute-done.3), kind=kLoop, calls=%fused_computation.34 | loop fusion | flops 1835008 | bytes 7340033 | tf_op jit(solution)/shard_map/stack | solution.py:126
  82.2 3.7 %pad_maximum_fusion = bf16[4,512,1792]{2,1,0:T(8,128)(2,1)} fusion(bf16[1,512,1792]{2,1,0:T(8,128)(2,1)S(1)} %get-tuple-element.13, bf16[1,512,1792]{2,1,0:T(8,128)(2,1)S(1)} %maximum_select_fusion.2, bf16[1,512,1792]{2,1,0:T(8,128)(2,1)S(1)} %get-tuple-element.12, bf16[1,512,1792]{2,1,0:T(8,128)(2,1)S(1)} %maximum_select_fusion), kind=kLoop, calls=%fused_computation.14 | loop fusion | flops 11010048 | bytes 14680064 | tf_op jit(solution)/shard_map/stack | solution.py:126
  85.9 7.0 %gather_fusion = bf16[4,512,1792]{2,1,0:T(8,128)(2,1)} fusion(bf16[4,512,1792]{2,1,0:T(8,128)(2,1)} %pad_maximum_fusion, s32[1024]{0:T(1024)S(1)} %get-tuple-element.29), kind=kCustom, calls=%fused_computation | custom fusion | bytes 14680080 | tf_op jit(solution)/shard_map/jit(_take)/gather | solution.py:128
  92.8 5.3 %fusion = f32[512]{0:T(512)S(1)} fusion(bf16[4,512,1792]{2,1,0:T(8,128)(2,1)} %gather_fusion, pred[4]{0:T(512)(128)(4,1)S(1)} %compare_and_fusion), kind=kLoop, calls=%fused_computation.5 | loop fusion | flops 14679552 | bytes 7342084 | tf_op jit(solution)/shard_map/reduce_sum | solution.py:131
  98.1 1.2 multiply_convert_fusion
  99.4 5.7 %fusion.2 = bf16[4,512,1792]{2,1,0:T(8,128)(2,1)} fusion(f32[4,1792]{1,0:T(4,128)S(1)} %mul.219, f32[512]{0:T(512)S(1)} %add_rsqrt_fusion, bf16[4,512,1792]{2,1,0:T(8,128)(2,1)S(1)} %copy-done.2, pred[4]{0:T(512)(128)(4,1)S(1)} %compare_and_fusion), kind=kLoop, calls=%fused_computation.7 | loop fusion | flops 18350080 | bytes 14710788 | tf_op jit(solution)/shard_map/convert.12
  105.0 10.1 %convolution_bitcast_fusion = f32[4,128,512]{2,1,0:T(8,128)} fusion(bf16[4,128,4,1792]{3,1,0,2:T(8,128)(2,1)} %bitcast.205, bf16[4,1792,512,1]{2,1,3,0:T(8,128)(2,1)} %bitcast.241), kind=kOutput, calls=%fused_computation.44 | convolution fusion | flops 3758096384 | bytes 15728640 | tf_op jit(solution)/shard_map/csf,cfn->sn/dot_general | solution.py:180
  115.1 1.2 all-gather.2.cloned.1.call-done
  116.3 4.5 %gather_fusion.2 = bf16[4,608,128]{2,1,0:T(8,128)(2,1)S(1)} fusion(bf16[64,608,128]{2,1,0:T(8,128)(2,1)} %all-gather.2.cloned.1.call-done, s32[1024]{0:T(1024)S(1)} %pad_clamp_fusion), kind=kCustom, calls=%fused_computation.2 | custom fusion | bytes 1245200 | tf_op jit(solution)/shard_map/jit(_take)/gather | solution.py:162
  121.2 1.6 convolution_convert_fusion
  122.9 0.9 collective-permute-start.4
  123.8 7.0 %fusion.25 = f32[4,128,1,256]{3,1,0,2:T(8,128)} fusion(bf16[4,128,4,1792]{3,1,0,2:T(8,128)(2,1)} %bitcast.206, bf16[4,1792,256]{1,2,0:T(8,128)(2,1)} %copy.75), kind=kOutput, calls=%fused_computation.46 | convolution fusion | flops 1879048192 | bytes 11534336 | tf_op jit(solution)/shard_map/csf,cfn->sn/dot_general | solution.py:192
  130.8 1.3 collective-permute-start.5
  132.2 2.0 collective-permute-done.5
  134.2 3.0 %collective-permute-start.6 = (bf16[4,128,48]{1,2,0:T(8,128)(2,1)S(1)}, bf16[4,128,48]{1,2,0:T(8,128)(2,1)S(1)}, u32[]{:S(2)}, u32[]{:S(2)}) collective-permute-start(bf16[4,128,48]{1,2,0:T(8,128)(2,1)S(1)} %add_convert_fusion.2), channel_id=1, source_target_pairs={{0,4},{1,5},{2,6},{3,7},{4,0},{5,1},{6,2},{7,3},{8,12},{9,13},{10,... | collective-permute-start | bytes 147464 | tf_op jit(solution)/shard_map/ppermute | solution.py:60
  137.3 1.6 copy.81
  139.4 0.4 reshape.694
  139.7 0.6 fusion.89
  141.0 1.0 copy-done.5
  142.0 1.5 fusion.3
  143.4 2.3 fusion.28
  145.7 2.2 fusion.11
  148.1 1.2 fusion.61
  149.4 0.5 fusion.91
  150.3 1.5 fusion.24
  152.4 7.3 %fusion.8 = bf16[512,8,896]{2,0,1:T(8,128)(2,1)S(1)} fusion(bf16[512,512,1]{1,0,2:T(8,128)(2,1)S(1)} %reshape.746, bf16[64,8,8,896]{3,2,1,0:T(8,128)(2,1)} %bitcast.242), kind=kOutput, calls=%fused_computation.18 | convolution fusion | flops 3761766400 | bytes 15204352 | tf_op jit(solution)/shard_map/sc,ctf->tsf/dot_general | solution.py:257
  159.7 2.4 %dynamic-slice_bitcast_fusion = bf16[4,512,896]{2,1,0:T(8,128)(2,1)} fusion(bf16[4,2,512,896]{3,2,1,0:T(8,128)(2,1)S(1)} %bitcast.207, s32[]{:T(128)S(6)} %select_n.173), kind=kLoop, calls=%fused_computation.25 | loop fusion | bytes 7340036 | tf_op jit(solution)/shard_map/jit(dynamic_index_in_dim)/squeeze | solution.py:274
  162.1 1.8 copy-done.4
  163.9 2.0 collective-permute-start.7
  165.9 6.4 %collective-permute-done.7 = bf16[4,512,896]{2,1,0:T(8,128)(2,1)} collective-permute-done((bf16[4,512,896]{2,1,0:T(8,128)(2,1)}, bf16[4,512,896]{2,1,0:T(8,128)(2,1)}, u32[]{:S(2)}, u32[]{:S(2)}) %collective-permute-start.7) | collective-permute-done | bytes 3670048 | tf_op jit(solution)/shard_map/ppermute | solution.py:277
  172.3 6.0 %fusion.7 = bf16[4,512,896]{2,1,0:T(8,128)(2,1)} fusion(bf16[4,512,896]{2,1,0:T(8,128)(2,1)} %collective-permute-done.7, bf16[4,2,512,896]{3,2,1,0:T(8,128)(2,1)} %bitcast.208, s32[]{:T(128)S(6)} %select_n.172), kind=kLoop, calls=%fused_computation.16 | loop fusion | flops 7340032 | bytes 11010052 | tf_op jit(solution)/shard_map/convert_element_type | solution.py:278
  178.5 0.4 collective-permute-start.8
  178.9 0.8 collective-permute-done.8
  179.8 1.3 collective-permute-start.9
  181.1 1.4 collective-permute-done.9
  182.5 2.8 %collective-permute-start.10 = (bf16[4,128,16]{1,2,0:T(8,128)(2,1)S(1)}, bf16[4,128,16]{1,2,0:T(8,128)(2,1)S(1)}, u32[]{:S(2)}, u32[]{:S(2)}) collective-permute-start(bf16[4,128,16]{1,2,0:T(8,128)(2,1)S(1)} %add_convert_fusion.5), channel_id=1, source_target_pairs={{0,4},{1,5},{2,6},{3,7},{4,0},{5,1},{6,2},{7,3},{8,12},{9,13},{10,... | collective-permute-start | bytes 49160 | tf_op jit(solution)/shard_map/ppermute | solution.py:60
  185.3 1.3 collective-permute-done.10
  186.6 1.7 convolution_multiply_fusion
  188.4 32.0 %reduce-scatter.2.cloned.1.call-done = bf16[1,512,896]{2,1,0:T(8,128)(2,1)} async-done(((bf16[4,512,896]{2,1,0:T(8,128)(2,1)}), bf16[1,512,896]{2,1,0:T(8,128)(2,1)}) %reduce-scatter.2.cloned.1.call-update) | async-done | bytes 917520 | tf_op jit(solution)/shard_map/reduce_scatter | solution.py:280
  220.3 2.8 %fusion.18 = bf16[512,896]{1,0:T(8,128)(2,1)} fusion(f32[4,128,896]{2,1,0:T(8,128)} %convolution_multiply_fusion, bf16[1,512,896]{2,1,0:T(8,128)(2,1)} %reduce-scatter.2.cloned.1.call-done), kind=kLoop, calls=%fused_computation.31 | loop fusion | flops 1376256 | bytes 3670016 | tf_op jit(solution)/shard_map/convert_element_type | solution.py:286
  (94 shorter events, 4.9 us)
Async XLA Ops:
  6.5 42.6 %copy-start = (bf16[32,128,256]{2,1,0:T(8,128)(2,1)S(1)}, bf16[32,128,256]{2,1,0:T(8,128)(2,1)}, u32[]{:S(2)}) copy-start(bf16[32,128,256]{2,1,0:T(8,128)(2,1)} %param.31) | copy-start | bytes 6291460
  6.5 6.0 %copy-start.3 = (bf16[512,896]{1,0:T(8,128)(2,1)S(1)}, bf16[512,896]{1,0:T(8,128)(2,1)}, u32[]{:S(2)}) copy-start(bf16[512,896]{1,0:T(8,128)(2,1)} %param.16) | copy-start | bytes 2752516
  6.5 109.7 %all-gather.2.cloned.1.call-start = ((), (), s32[]{:S(2)}) async-start(), calls=%async_computation.2 | async-start | bytes 10584064 | tf_op jit(solution)/shard_map/all_gather | solution.py:153
  11.6 36.6 %copy-start.12 = (s32[1,32]{1,0:T(1,128)S(1)}, s32[1,32]{1,0:T(1,128)}, u32[]{:S(2)}) copy-start(s32[1,32]{1,0:T(1,128)} %param.30) | copy-start | bytes 388
  12.6 3.7 %collective-permute-start = (bf16[512,896]{1,0:T(8,128)(2,1)S(1)}, bf16[512,896]{1,0:T(8,128)(2,1)}, u32[]{:S(2)}, u32[]{:S(2)}) collective-permute-start(bf16[512,896]{1,0:T(8,128)(2,1)S(1)} %copy-done.3), channel_id=1, source_target_pairs={{0,1},{1,0},{2,3},{3,2},{4,5},{5,4},{6,7},{7,6},{8,9},{9,8},{10,11... | collective-permute-start | bytes 2752520 | tf_op jit(solution)/shard_map/ppermute | solution.py:106
  19.4 23.1 %collective-permute-start.1 = (bf16[512,1792]{1,0:T(8,128)(2,1)}, bf16[512,1792]{1,0:T(8,128)(2,1)}, u32[]{:S(2)}, u32[]{:S(2)}) collective-permute-start(bf16[512,1792]{1,0:T(8,128)(2,1)} %maximum_select_fusion.1), channel_id=1, source_target_pairs={{6,0},{3,1},{0,2},{5,3},{2,4},{7,5},{4,6},{1,7},{14,8},{11,9},{8,1... | collective-permute-start | bytes 5505032 | tf_op jit(solution)/shard_map/ppermute | solution.py:112
  44.6 17.8 %collective-permute-start.2 = (bf16[512,896]{1,0:T(8,128)(2,1)}, bf16[512,896]{1,0:T(8,128)(2,1)}, u32[]{:S(2)}, u32[]{:S(2)}) collective-permute-start(bf16[512,896]{1,0:T(8,128)(2,1)} %constant_dynamic-slice_fusion), channel_id=1, source_target_pairs={{6,0},{3,1},{0,2},{5,3},{2,4},{7,5},{4,6},{1,7},{14,8},{11,9},{8,1... | collective-permute-start | bytes 2752520 | tf_op jit(solution)/shard_map/ppermute | solution.py:113
  51.2 11.0 %copy-start.13 = (s32[32]{0:T(128)S(1)}, s32[32]{0:T(128)}, u32[]{:S(2)}) copy-start(s32[32]{0:T(128)} %param.29) | copy-start | bytes 388
  51.2 11.1 %copy-start.14 = (s32[32]{0:T(128)S(1)}, s32[32]{0:T(128)}, u32[]{:S(2)}) copy-start(s32[32]{0:T(128)} %param.28) | copy-start | bytes 388
  54.6 60.5 %all-to-all-start = ((bf16[2,16,128,256]{3,2,0,1:T(8,128)(2,1)}), bf16[2,16,128,256]{3,2,0,1:T(8,128)(2,1)S(1)}, u32[]{:S(2)}, u32[]{:S(2)}) async-start(bf16[2,16,128,256]{3,2,0,1:T(8,128)(2,1)} %copy.71), calls=%async_computation | async-start | bytes 4194304 | tf_op jit(solution)/shard_map/all_to_all | solution.py:160
  62.2 4.1 %copy-start.10 = (f32[7168]{0:T(1024)S(1)}, f32[7168]{0:T(1024)}, u32[]{:S(2)}) copy-start(f32[7168]{0:T(1024)} %param.17) | copy-start | bytes 86020
  62.2 158.2 %reduce-scatter.2.cloned.1.call-start = ((), (), s32[]{:S(2)}) async-start(), calls=%async_computation.3 | async-start | bytes 4587520 | tf_op jit(solution)/shard_map/reduce_scatter | solution.py:280
  65.9 10.7 %collective-permute-start.3 = (bf16[512,2688]{1,0:T(8,128)(2,1)}, bf16[512,2688]{1,0:T(8,128)(2,1)}, u32[]{:S(2)}, u32[]{:S(2)}) collective-permute-start(bf16[512,2688]{1,0:T(8,128)(2,1)} %pad_maximum_fusion.1), channel_id=1, source_target_pairs={{0,1},{1,0},{2,3},{3,2},{4,5},{5,4},{6,7},{7,6},{8,9},{9,8},{10,11... | collective-permute-start | bytes 8257544 | tf_op jit(solution)/shard_map/ppermute | solution.py:117
  66.3 6.0 %copy-start.11 = (s32[4]{0:T(128)S(1)}, s32[4]{0:T(128)}, u32[]{:S(2)}) copy-start(s32[4]{0:T(128)} %param.26) | copy-start | bytes 52
  66.3 6.0 %copy-start.15 = (s32[4]{0:T(128)S(1)}, s32[4]{0:T(128)}, u32[]{:S(2)}) copy-start(s32[4]{0:T(128)} %param.27) | copy-start | bytes 52
  92.8 6.5 %copy-start.2 = (bf16[4,512,1792]{2,1,0:T(8,128)(2,1)S(1)}, bf16[4,512,1792]{2,1,0:T(8,128)(2,1)}, u32[]{:S(2)}) copy-start(bf16[4,512,1792]{2,1,0:T(8,128)(2,1)} %gather_fusion) | copy-start | bytes 22020100
  122.9 7.9 %collective-permute-start.4 = (bf16[4,128,48]{1,2,0:T(8,128)(2,1)S(1)}, bf16[4,128,48]{1,2,0:T(8,128)(2,1)S(1)}, u32[]{:S(2)}, u32[]{:S(2)}) collective-permute-start(bf16[4,128,48]{1,2,0:T(8,128)(2,1)S(1)} %convolution_convert_fusion), channel_id=1, source_target_pairs={{0,1},{1,0},{2,3},{3,2},{4,5},{5,4},{6,7},{7,6},{8,9},{9,8},{10,11... | collective-permute-start | bytes 147464 | tf_op jit(solution)/shard_map/ppermute | solution.py:60
  130.8 8.2 %copy-start.8 = (f32[4,128,512]{2,1,0:T(8,128)S(1)}, f32[4,128,512]{2,1,0:T(8,128)}, u32[]{:S(2)}) copy-start(f32[4,128,512]{2,1,0:T(8,128)} %convolution_bitcast_fusion) | copy-start | bytes 3145732
  130.8 3.4 %collective-permute-start.5 = (bf16[4,128,48]{1,2,0:T(8,128)(2,1)S(1)}, bf16[4,128,48]{1,2,0:T(8,128)(2,1)S(1)}, u32[]{:S(2)}, u32[]{:S(2)}) collective-permute-start(bf16[4,128,48]{1,2,0:T(8,128)(2,1)S(1)} %add_convert_fusion.3), channel_id=1, source_target_pairs={{0,2},{1,3},{2,0},{3,1},{4,6},{5,7},{6,4},{7,5},{8,10},{9,11},{10,... | collective-permute-start | bytes 147464 | tf_op jit(solution)/shard_map/ppermute | solution.py:60
  134.2 4.7 %collective-permute-start.6 = (bf16[4,128,48]{1,2,0:T(8,128)(2,1)S(1)}, bf16[4,128,48]{1,2,0:T(8,128)(2,1)S(1)}, u32[]{:S(2)}, u32[]{:S(2)}) collective-permute-start(bf16[4,128,48]{1,2,0:T(8,128)(2,1)S(1)} %add_convert_fusion.2), channel_id=1, source_target_pairs={{0,4},{1,5},{2,6},{3,7},{4,0},{5,1},{6,2},{7,3},{8,12},{9,13},{10,... | collective-permute-start | bytes 147464 | tf_op jit(solution)/shard_map/ppermute | solution.py:60
  139.4 1.0 copy-start.6
  139.4 1.0 copy-start.7
  140.3 1.6 copy-start.5
  145.7 2.2 copy-start.9
  159.7 4.2 %copy-start.4 = (bf16[512,8,896]{2,0,1:T(8,128)(2,1)}, bf16[512,8,896]{2,0,1:T(8,128)(2,1)S(1)}, u32[]{:S(2)}) copy-start(bf16[512,8,896]{2,0,1:T(8,128)(2,1)S(1)} %fusion.8) | copy-start | bytes 22020100
  163.9 8.4 %collective-permute-start.7 = (bf16[4,512,896]{2,1,0:T(8,128)(2,1)}, bf16[4,512,896]{2,1,0:T(8,128)(2,1)}, u32[]{:S(2)}, u32[]{:S(2)}) collective-permute-start(bf16[4,512,896]{2,1,0:T(8,128)(2,1)} %dynamic-slice_bitcast_fusion), channel_id=1, source_target_pairs={{0,1},{1,0},{2,3},{3,2},{4,5},{5,4},{6,7},{7,6},{8,9},{9,8},{10,11... | collective-permute-start | bytes 11010056 | tf_op jit(solution)/shard_map/ppermute | solution.py:277
  178.3 44.9 %copy-start.1 = (bf16[32,128,256]{2,1,0:T(8,128)(2,1)S(1)}, bf16[32,128,256]{2,1,0:T(8,128)(2,1)}, u32[]{:S(2)}) copy-start(bf16[32,128,256]{2,1,0:T(8,128)(2,1)} %param.31) | copy-start | bytes 6291460
  178.5 1.3 collective-permute-start.8
  179.8 2.7 %collective-permute-start.9 = (bf16[4,128,16]{1,2,0:T(8,128)(2,1)S(1)}, bf16[4,128,16]{1,2,0:T(8,128)(2,1)S(1)}, u32[]{:S(2)}, u32[]{:S(2)}) collective-permute-start(bf16[4,128,16]{1,2,0:T(8,128)(2,1)S(1)} %add_convert_fusion.6), channel_id=1, source_target_pairs={{0,2},{1,3},{2,0},{3,1},{4,6},{5,7},{6,4},{7,5},{8,10},{9,11},{10,... | collective-permute-start | bytes 49160 | tf_op jit(solution)/shard_map/ppermute | solution.py:60
  182.5 4.2 %collective-permute-start.10 = (bf16[4,128,16]{1,2,0:T(8,128)(2,1)S(1)}, bf16[4,128,16]{1,2,0:T(8,128)(2,1)S(1)}, u32[]{:S(2)}, u32[]{:S(2)}) collective-permute-start(bf16[4,128,16]{1,2,0:T(8,128)(2,1)S(1)} %add_convert_fusion.5), channel_id=1, source_target_pairs={{0,4},{1,5},{2,6},{3,7},{4,0},{5,1},{6,2},{7,3},{8,12},{9,13},{10,... | collective-permute-start | bytes 49160 | tf_op jit(solution)/shard_map/ppermute | solution.py:60
Sparse Core Ops, SparseCore 0:
  12.7 103.5 all-gather.1
  178.4 41.8 reduce-scatter.1

commit v11 on v8

--- a/solution.py
+++ b/solution.py
@@ -159,9 +159,12 @@
     )
     arrived = lax.all_to_all(outgoing, "req", split_axis=1, concat_axis=1, tiled=True)
     every_adapter, arrived = lax.optimization_barrier((every_adapter, arrived))
-    picked = jnp.take(every_adapter, request_adapter, axis=0, mode="clip").reshape(
-        request_number, -1
-    )
+    picked = jnp.stack(
+        [
+            lax.dynamic_index_in_dim(every_adapter, request_adapter[slot], 0, keepdims=False)
+            for slot in range(request_number)
+        ]
+    ).reshape(request_number, -1)
     picked_parts = []
     start = 0
     for part, flat in zip(adapter_parts, flat_parts):

time: 220 us -> 228 us (1.036)
  between operations: 13.9 us -> 21.8 us
  starting transfers between devices: 26.4 us -> 22.6 us
  other arithmetic: 36.9 us -> 40.5 us
    gather x1 -> x0, local copies, waits for them, and re-layouts: 4.49 us -> none  [local(): jnp.take(every_adapter, request_adapter, axis=0, mode='clip')]
    ppermute x6, starting transfers between devices: 11.3 us -> 7.63 us  [sum_over_tensor(): lax.ppermute(sent, 'tensor', pairs).astype(jnp.float32)]
    all_gather x1, waiting for transfers between devices: 2.55 us -> 0.01 us  [local(): lax.all_gather(joined.reshape(local_adapters, lane_rows, 128), 'req', axi...]
    unnamed x45 -> x65, local copies, waits for them, and re-layouts: 7.98 us -> 9.69 us
  transfers between devices with their start and end apart: 13 -> 13, of which waited for: 11 -> 8; matrix products, arithmetic and copies ran while one was open for 33% -> 35% of each run, Pallas kernels for 0% -> 0%
where the time goes in v11:
time: 228 us; the launch traced here: 227 us
  waiting for transfers between devices  67.6 us (30%)
  other arithmetic  40.5 us (18%)
  local copies, waits for them, and re-layouts  39.4 us (17%)
  matrix products  35.2 us (15%)
  starting transfers between devices  22.6 us (10%)
  between operations  21.8 us (10%)
    reduce_scatter x1, waiting for transfers between devices, local(): lax.psum_scatter(head_terms.astype(jnp.bfloat16), 'tensor', scatter_dimen...  36.8 us
    ppermute x1, waiting for transfers between devices, local(): beside = lax.ppermute(pair, 'tensor', along)  20.5 us
    dot_general x1, matrix products, local(): jnp.einsum('csf,cfn->sn', normed_parts, query_weight.reshape(chip_count,...  10.1 us
    unnamed x65, local copies, waits for them, and re-layouts  9.69 us
    dot_general x1, matrix products, local(): jnp.einsum('sc,ctf->tsf', attended, output_weight.reshape(output_weight.s...  9.15 us
    ppermute x6, waiting for transfers between devices, sum_over_tensor(): lax.ppermute(sent, 'tensor', pairs).astype(jnp.float32)  8.05 us
    all_to_all x1, starting transfers between devices, local(): lax.all_to_all(outgoing, 'req', split_axis=1, concat_axis=1, tiled=True)  7.77 us
    ppermute x6, starting transfers between devices, sum_over_tensor(): lax.ppermute(sent, 'tensor', pairs).astype(jnp.float32)  7.63 us
  transfers between devices with their start and end apart: 13, of which 8 were waited for; matrix products, arithmetic and copies ran while one was open for 35% of the time, Pallas kernels for 0%

profile of v11, /device:TPU:1, one launch (start us, length us, event | category | flops | bytes accessed | tf_op | source)
XLA Modules:
  0.0 227.1 jit_solution(2305876858563209109)
XLA Ops:
  6.5 1.0 copy.107
  7.6 0.9 copy.109
  8.5 0.9 copy.110
  9.4 1.1 copy.106
  10.7 0.8 bitcast_dynamic-update-slice_fusion
  11.6 0.9 copy.150
  12.5 1.5 collective-permute-start
  14.0 2.2 collective-permute-done
  16.2 3.1 %maximum_select_fusion.1 = bf16[512,1792]{1,0:T(8,128)(2,1)} fusion(bf16[512,896]{1,0:T(8,128)(2,1)} %collective-permute-done, bf16[512,896]{1,0:T(8,128)(2,1)S(1)} %copy-done.3, pred[]{:T(512)S(6)} %eq.6), kind=kLoop, calls=%fused_computation.24 | loop fusion | flops 8257536 | bytes 3670017 | tf_op jit(solution)/shard_map/jit(_where)/select_n | solution.py:107
  19.4 2.6 %collective-permute-start.1 = (bf16[512,1792]{1,0:T(8,128)(2,1)}, bf16[512,1792]{1,0:T(8,128)(2,1)}, u32[]{:S(2)}, u32[]{:S(2)}) collective-permute-start(bf16[512,1792]{1,0:T(8,128)(2,1)} %maximum_select_fusion.1), channel_id=1, source_target_pairs={{6,0},{3,1},{0,2},{5,3},{2,4},{7,5},{4,6},{1,7},{14,8},{11,9},{8,1... | collective-permute-start | bytes 5505032 | tf_op jit(solution)/shard_map/ppermute | solution.py:112
  22.0 20.5 %collective-permute-done.1 = bf16[512,1792]{1,0:T(8,128)(2,1)} collective-permute-done((bf16[512,1792]{1,0:T(8,128)(2,1)}, bf16[512,1792]{1,0:T(8,128)(2,1)}, u32[]{:S(2)}, u32[]{:S(2)}) %collective-permute-start.1) | collective-permute-done | bytes 1835040 | tf_op jit(solution)/shard_map/ppermute | solution.py:112
  42.5 2.2 constant_dynamic-slice_fusion.4
  44.6 3.1 %collective-permute-start.2 = (bf16[512,896]{1,0:T(8,128)(2,1)}, bf16[512,896]{1,0:T(8,128)(2,1)}, u32[]{:S(2)}, u32[]{:S(2)}) collective-permute-start(bf16[512,896]{1,0:T(8,128)(2,1)} %constant_dynamic-slice_fusion.4), channel_id=1, source_target_pairs={{6,0},{3,1},{0,2},{5,3},{2,4},{7,5},{4,6},{1,7},{14,8},{11,9},{8,1... | collective-permute-start | bytes 2752520 | tf_op jit(solution)/shard_map/ppermute | solution.py:113
  48.3 0.6 reduce.11
  49.8 2.0 gather_fusion.1
  51.8 3.2 %copy.68 = bf16[2,16,128,256]{3,2,0,1:T(8,128)(2,1)} copy(bf16[2,16,128,256]{3,2,1,0:T(8,128)(2,1)} %bitcast.200) | data formatting | bytes 4194304 | tf_op jit(solution)/shard_map/reshape | solution.py:157
  55.0 7.8 %all-to-all-start = ((bf16[2,16,128,256]{3,2,0,1:T(8,128)(2,1)}), bf16[2,16,128,256]{3,2,0,1:T(8,128)(2,1)S(1)}, u32[]{:S(2)}, u32[]{:S(2)}) async-start(bf16[2,16,128,256]{3,2,0,1:T(8,128)(2,1)} %copy.68), calls=%async_computation | async-start | bytes 4194304 | tf_op jit(solution)/shard_map/all_to_all | solution.py:160
  62.9 3.5 %pad_maximum_fusion.1 = bf16[512,2688]{1,0:T(8,128)(2,1)} fusion(bf16[512,896]{1,0:T(8,128)(2,1)} %collective-permute-done.2, bf16[512,1792]{1,0:T(8,128)(2,1)} %collective-permute-done.1), kind=kLoop, calls=%fused_computation.22 | loop fusion | flops 5505024 | bytes 5505024 | tf_op jit(solution)/shard_map/concatenate | solution.py:116
  66.4 0.7 fusion.89
  72.4 0.6 dynamic_slice.31
  73.4 0.6 mul.219
  74.1 5.9 %copy.72 = bf16[4,1792,256]{1,2,0:T(8,128)(2,1)} copy(bf16[4,1792,256]{2,1,0:T(8,128)(2,1)} %bitcast.208) | data formatting | bytes 7340032 | tf_op jit(solution)/shard_map/reshape | solution.py:198
  82.6 0.6 compare_and_fusion
  83.9 0.8 broadcast_and_fusion
  84.6 1.0 multiply_cosine_fusion.1
  85.6 0.7 fusion.66
  86.3 1.9 maximum_select_fusion
  88.3 1.3 slice_bitcast_fusion.4
  89.5 1.9 maximum_select_fusion.2
  91.4 2.4 %select_bitcast_fusion.1 = (bf16[1,512,1792]{2,1,0:T(8,128)(2,1)S(1)}, bf16[1,512,1792]{2,1,0:T(8,128)(2,1)S(1)}) fusion(bf16[512,1792]{1,0:T(8,128)(2,1)} %collective-permute-done.1, pred[]{:T(512)S(6)} %eq.6, bf16[512,2688]{1,0:T(8,128)(2,1)} %collective-permute-done.3), kind=kLoop, calls=%fused_computation.30 | loop fusion | flops 1835008 | bytes 7340033 | tf_op jit(solution)/shard_map/stack | solution.py:126
  93.8 3.6 %pad_maximum_fusion = bf16[4,512,1792]{2,1,0:T(8,128)(2,1)} fusion(bf16[1,512,1792]{2,1,0:T(8,128)(2,1)S(1)} %get-tuple-element.17, bf16[1,512,1792]{2,1,0:T(8,128)(2,1)S(1)} %maximum_select_fusion.2, bf16[1,512,1792]{2,1,0:T(8,128)(2,1)S(1)} %get-tuple-element.16, bf16[1,512,1792]{2,1,0:T(8,128)(2,1)S(1)} %maximum_select_fusion), kind=kLoop, calls=%fused_computation.13 | loop fusion | flops 11010048 | bytes 14680064 | tf_op jit(solution)/shard_map/stack | solution.py:126
  97.4 7.2 %gather_fusion = bf16[4,512,1792]{2,1,0:T(8,128)(2,1)} fusion(bf16[4,512,1792]{2,1,0:T(8,128)(2,1)} %pad_maximum_fusion, s32[1024]{0:T(1024)} %get-tuple-element.37), kind=kCustom, calls=%fused_computation | custom fusion | bytes 14680080 | tf_op jit(solution)/shard_map/jit(_take)/gather | solution.py:128
  104.7 5.3 %fusion = f32[512]{0:T(512)S(1)} fusion(bf16[4,512,1792]{2,1,0:T(8,128)(2,1)} %gather_fusion, pred[4]{0:T(512)(128)(4,1)} %compare_and_fusion), kind=kLoop, calls=%fused_computation.4 | loop fusion | flops 14679552 | bytes 7342084 | tf_op jit(solution)/shard_map/reduce_sum | solution.py:131
  110.0 1.2 multiply_convert_fusion
  111.2 5.7 %fusion.2 = bf16[4,512,1792]{2,1,0:T(8,128)(2,1)} fusion(f32[4,1792]{1,0:T(4,128)S(1)} %copy-done.12, f32[512]{0:T(512)S(1)} %add_rsqrt_fusion, bf16[4,512,1792]{2,1,0:T(8,128)(2,1)S(1)} %copy-done.2, pred[4]{0:T(512)(128)(4,1)S(1)} %copy-done.16), kind=kLoop, calls=%fused_computation.6 | loop fusion | flops 18350080 | bytes 14710788 | tf_op jit(solution)/shard_map/convert.11
  116.9 10.1 %convolution_bitcast_fusion = f32[4,128,512]{2,1,0:T(8,128)} fusion(bf16[4,128,4,1792]{3,1,0,2:T(8,128)(2,1)} %bitcast.202, bf16[4,1792,512,1]{2,1,3,0:T(8,128)(2,1)} %bitcast.235), kind=kOutput, calls=%fused_computation.40 | convolution fusion | flops 3758096384 | bytes 15728640 | tf_op jit(solution)/shard_map/csf,cfn->sn/dot_general | solution.py:183
  127.0 1.3 constant_dynamic-slice_fusion.3
  128.9 1.6 convolution_convert_fusion
  130.5 0.9 collective-permute-start.4
  131.5 6.0 %fusion.23 = f32[4,128,1,256]{3,1,0,2:T(8,128)} fusion(bf16[4,128,4,1792]{3,1,0,2:T(8,128)(2,1)} %bitcast.203, bf16[4,1792,256]{1,2,0:T(8,128)(2,1)S(1)} %copy-done.5), kind=kOutput, calls=%fused_computation.42 | convolution fusion | flops 1879048192 | bytes 11534336 | tf_op jit(solution)/shard_map/csf,cfn->sn/dot_general | solution.py:195
  137.9 0.7 fusion.88
  138.6 2.3 collective-permute-done.5
  140.8 1.3 collective-permute-start.6
  142.2 0.6 copy.115
  142.8 1.6 copy.78
  144.3 1.0 collective-permute-done.6
  146.1 0.6 fusion.87
  147.4 1.0 copy-done.4
  148.3 1.5 fusion.3
  149.8 2.3 fusion.26
  152.1 2.2 fusion.9
  154.6 1.2 fusion.59
  156.8 1.5 fusion.22
  158.9 9.1 %convert_bitcast_fusion = bf16[8,512,896]{2,1,0:T(8,128)(2,1)} fusion(bf16[512,512,1]{1,0,2:T(8,128)(2,1)S(1)} %reshape.730, bf16[64,8,8,896]{3,2,1,0:T(8,128)(2,1)} %bitcast.236), kind=kOutput, calls=%fused_computation.14 | convolution fusion | flops 3761766400 | bytes 15204352 | tf_op jit(solution)/shard_map/sc,ctf->tsf/dot_general | solution.py:260
  168.1 0.8 copy-done.8
  169.1 2.1 collective-permute-start.7
  171.2 0.8 collective-permute-done.7
  172.0 0.8 collective-permute-start.8
  172.8 1.8 collective-permute-done.8
  174.7 2.0 collective-permute-start.9
  176.8 2.1 collective-permute-done.9
  178.9 1.7 convolution_multiply_fusion
  180.6 36.8 %reduce-scatter.2.cloned.1.call-done = bf16[1,512,896]{2,1,0:T(8,128)(2,1)} async-done(((bf16[8,512,896]{2,1,0:T(8,128)(2,1)}), bf16[1,512,896]{2,1,0:T(8,128)(2,1)}) %reduce-scatter.2.cloned.1.call-update) | async-done | bytes 917520 | tf_op jit(solution)/shard_map/reduce_scatter | solution.py:273
  217.4 2.8 %fusion.16 = bf16[512,896]{1,0:T(8,128)(2,1)} fusion(f32[4,128,896]{2,1,0:T(8,128)} %convolution_multiply_fusion, bf16[1,512,896]{2,1,0:T(8,128)(2,1)} %reduce-scatter.2.cloned.1.call-done), kind=kLoop, calls=%fused_computation.27 | loop fusion | flops 1376256 | bytes 3670016 | tf_op jit(solution)/shard_map/convert_element_type | solution.py:279
  (109 shorter events, 7.2 us)
Async XLA Ops:
  6.5 43.3 %copy-start = (bf16[32,128,256]{2,1,0:T(8,128)(2,1)S(1)}, bf16[32,128,256]{2,1,0:T(8,128)(2,1)}, u32[]{:S(2)}) copy-start(bf16[32,128,256]{2,1,0:T(8,128)(2,1)} %param.31) | copy-start | bytes 6291460
  6.5 6.0 %copy-start.3 = (bf16[512,896]{1,0:T(8,128)(2,1)S(1)}, bf16[512,896]{1,0:T(8,128)(2,1)}, u32[]{:S(2)}) copy-start(bf16[512,896]{1,0:T(8,128)(2,1)} %param.16) | copy-start | bytes 2752516
  6.5 120.5 %all-gather.2.cloned.1.call-start = ((), (), s32[]{:S(2)}) async-start(), calls=%async_computation.2 | async-start | bytes 10584064 | tf_op jit(solution)/shard_map/all_gather | solution.py:153
  11.6 36.7 %copy-start.21 = (s32[1,32]{1,0:T(1,128)S(1)}, s32[1,32]{1,0:T(1,128)}, u32[]{:S(2)}) copy-start(s32[1,32]{1,0:T(1,128)} %param.30) | copy-start | bytes 388
  12.5 3.7 %collective-permute-start = (bf16[512,896]{1,0:T(8,128)(2,1)S(1)}, bf16[512,896]{1,0:T(8,128)(2,1)}, u32[]{:S(2)}, u32[]{:S(2)}) collective-permute-start(bf16[512,896]{1,0:T(8,128)(2,1)S(1)} %copy-done.3), channel_id=1, source_target_pairs={{0,1},{1,0},{2,3},{3,2},{4,5},{5,4},{6,7},{7,6},{8,9},{9,8},{10,11... | collective-permute-start | bytes 2752520 | tf_op jit(solution)/shard_map/ppermute | solution.py:106
  19.4 23.1 %collective-permute-start.1 = (bf16[512,1792]{1,0:T(8,128)(2,1)}, bf16[512,1792]{1,0:T(8,128)(2,1)}, u32[]{:S(2)}, u32[]{:S(2)}) collective-permute-start(bf16[512,1792]{1,0:T(8,128)(2,1)} %maximum_select_fusion.1), channel_id=1, source_target_pairs={{6,0},{3,1},{0,2},{5,3},{2,4},{7,5},{4,6},{1,7},{14,8},{11,9},{8,1... | collective-permute-start | bytes 5505032 | tf_op jit(solution)/shard_map/ppermute | solution.py:112
  44.6 18.2 %collective-permute-start.2 = (bf16[512,896]{1,0:T(8,128)(2,1)}, bf16[512,896]{1,0:T(8,128)(2,1)}, u32[]{:S(2)}, u32[]{:S(2)}) collective-permute-start(bf16[512,896]{1,0:T(8,128)(2,1)} %constant_dynamic-slice_fusion.4), channel_id=1, source_target_pairs={{6,0},{3,1},{0,2},{5,3},{2,4},{7,5},{4,6},{1,7},{14,8},{11,9},{8,1... | collective-permute-start | bytes 2752520 | tf_op jit(solution)/shard_map/ppermute | solution.py:113
  55.0 72.0 %all-to-all-start = ((bf16[2,16,128,256]{3,2,0,1:T(8,128)(2,1)}), bf16[2,16,128,256]{3,2,0,1:T(8,128)(2,1)S(1)}, u32[]{:S(2)}, u32[]{:S(2)}) async-start(bf16[2,16,128,256]{3,2,0,1:T(8,128)(2,1)} %copy.68), calls=%async_computation | async-start | bytes 4194304 | tf_op jit(solution)/shard_map/all_to_all | solution.py:160
  62.8 3.6 %copy-start.15 = (s32[4]{0:T(128)S(1)}, s32[4]{0:T(128)}, u32[]{:S(2)}) copy-start(s32[4]{0:T(128)} %param.26) | copy-start | bytes 52
  62.8 9.5 %copy-start.22 = (s32[32]{0:T(128)S(1)}, s32[32]{0:T(128)}, u32[]{:S(2)}) copy-start(s32[32]{0:T(128)} %param.29) | copy-start | bytes 388
  62.8 9.6 %copy-start.23 = (s32[32]{0:T(128)S(1)}, s32[32]{0:T(128)}, u32[]{:S(2)}) copy-start(s32[32]{0:T(128)} %param.28) | copy-start | bytes 388
  62.8 10.6 %copy-start.14 = (f32[7168]{0:T(1024)S(1)}, f32[7168]{0:T(1024)}, u32[]{:S(2)}) copy-start(f32[7168]{0:T(1024)} %param.17) | copy-start | bytes 86020
  62.8 154.6 %reduce-scatter.2.cloned.1.call-start = ((), (), s32[]{:S(2)}) async-start(), calls=%async_computation.3 | async-start | bytes 8257536 | tf_op jit(solution)/shard_map/reduce_scatter | solution.py:273
  66.4 21.9 %collective-permute-start.3 = (bf16[512,2688]{1,0:T(8,128)(2,1)}, bf16[512,2688]{1,0:T(8,128)(2,1)}, u32[]{:S(2)}, u32[]{:S(2)}) collective-permute-start(bf16[512,2688]{1,0:T(8,128)(2,1)} %pad_maximum_fusion.1), channel_id=1, source_target_pairs={{0,1},{1,0},{2,3},{3,2},{4,5},{5,4},{6,7},{7,6},{8,9},{9,8},{10,11... | collective-permute-start | bytes 8257544 | tf_op jit(solution)/shard_map/ppermute | solution.py:117
  74.1 9.2 %copy-start.24 = (s32[4]{0:T(128)S(1)}, s32[4]{0:T(128)}, u32[]{:S(2)}) copy-start(s32[4]{0:T(128)} %param.27) | copy-start | bytes 52
  83.2 1.4 copy-start.17
  83.4 0.5 copy-start.19
  104.7 6.5 %copy-start.2 = (bf16[4,512,1792]{2,1,0:T(8,128)(2,1)S(1)}, bf16[4,512,1792]{2,1,0:T(8,128)(2,1)}, u32[]{:S(2)}) copy-start(bf16[4,512,1792]{2,1,0:T(8,128)(2,1)} %gather_fusion) | copy-start | bytes 22020100
  104.7 6.5 %copy-start.12 = (f32[4,1792]{1,0:T(4,128)S(1)}, f32[4,1792]{1,0:T(4,128)}, u32[]{:S(2)}) copy-start(f32[4,1792]{1,0:T(4,128)} %mul.219) | copy-start | bytes 86020
  104.7 6.5 %copy-start.16 = (pred[4]{0:T(512)(128)(4,1)S(1)}, pred[4]{0:T(512)(128)(4,1)}, u32[]{:S(2)}) copy-start(pred[4]{0:T(512)(128)(4,1)} %compare_and_fusion) | copy-start | bytes 16
  127.0 4.5 %copy-start.5 = (bf16[4,1792,256]{1,2,0:T(8,128)(2,1)S(1)}, bf16[4,1792,256]{1,2,0:T(8,128)(2,1)}, u32[]{:S(2)}) copy-start(bf16[4,1792,256]{1,2,0:T(8,128)(2,1)} %copy.72) | copy-start | bytes 11010052
  130.5 6.9 %collective-permute-start.4 = (bf16[4,128,48]{1,2,0:T(8,128)(2,1)S(1)}, bf16[4,128,48]{1,2,0:T(8,128)(2,1)S(1)}, u32[]{:S(2)}, u32[]{:S(2)}) collective-permute-start(bf16[4,128,48]{1,2,0:T(8,128)(2,1)S(1)} %convolution_convert_fusion), channel_id=1, source_target_pairs={{0,1},{1,0},{2,3},{3,2},{4,5},{5,4},{6,7},{7,6},{8,9},{9,8},{10,11... | collective-permute-start | bytes 147464 | tf_op jit(solution)/shard_map/ppermute | solution.py:60
  137.4 8.0 %copy-start.6 = (f32[4,128,512]{2,1,0:T(8,128)S(1)}, f32[4,128,512]{2,1,0:T(8,128)}, u32[]{:S(2)}) copy-start(f32[4,128,512]{2,1,0:T(8,128)} %convolution_bitcast_fusion) | copy-start | bytes 3145732
  137.5 3.4 %collective-permute-start.5 = (bf16[4,128,48]{1,2,0:T(8,128)(2,1)S(1)}, bf16[4,128,48]{1,2,0:T(8,128)(2,1)S(1)}, u32[]{:S(2)}, u32[]{:S(2)}) collective-permute-start(bf16[4,128,48]{1,2,0:T(8,128)(2,1)S(1)} %add_convert_fusion.3), channel_id=1, source_target_pairs={{0,2},{1,3},{2,0},{3,1},{4,6},{5,7},{6,4},{7,5},{8,10},{9,11},{10,... | collective-permute-start | bytes 147464 | tf_op jit(solution)/shard_map/ppermute | solution.py:60
  140.8 4.5 %collective-permute-start.6 = (bf16[4,128,48]{1,2,0:T(8,128)(2,1)S(1)}, bf16[4,128,48]{1,2,0:T(8,128)(2,1)S(1)}, u32[]{:S(2)}, u32[]{:S(2)}) collective-permute-start(bf16[4,128,48]{1,2,0:T(8,128)(2,1)S(1)} %add_convert_fusion.2), channel_id=1, source_target_pairs={{0,4},{1,5},{2,6},{3,7},{4,0},{5,1},{6,2},{7,3},{8,12},{9,13},{10,... | collective-permute-start | bytes 147464 | tf_op jit(solution)/shard_map/ppermute | solution.py:60
  145.4 1.4 copy-start.9
  146.7 1.6 copy-start.4
  152.1 2.3 copy-start.10
  152.1 2.3 copy-start.11
  152.1 2.2 copy-start.13
  152.1 2.5 %copy-start.18 = (f32[64]{0:T(128)S(1)}, f32[64]{0:T(128)}, u32[]{:S(2)}) copy-start(f32[64]{0:T(128)} %copy-done.17) | copy-start | bytes 772
  152.1 3.8 %copy-start.7 = (pred[4,128,128]{1,2,0:T(8,128)(4,1)S(1)}, pred[4,128,128]{1,2,0:T(8,128)(4,1)}, u32[]{:S(2)}) copy-start(pred[4,128,128]{1,2,0:T(8,128)(4,1)} %broadcast_and_fusion) | copy-start | bytes 196612
  155.8 1.0 copy-start.20
  168.0 0.8 copy-start.8
  168.1 52.2 %copy-start.1 = (bf16[32,128,256]{2,1,0:T(8,128)(2,1)S(1)}, bf16[32,128,256]{2,1,0:T(8,128)(2,1)}, u32[]{:S(2)}) copy-start(bf16[32,128,256]{2,1,0:T(8,128)(2,1)} %param.31) | copy-start | bytes 6291460
  169.1 2.9 %collective-permute-start.7 = (bf16[4,128,16]{1,2,0:T(8,128)(2,1)S(1)}, bf16[4,128,16]{1,2,0:T(8,128)(2,1)S(1)}, u32[]{:S(2)}, u32[]{:S(2)}) collective-permute-start(bf16[4,128,16]{1,2,0:T(8,128)(2,1)S(1)} %convolution_convert_fusion.1), channel_id=1, source_target_pairs={{0,1},{1,0},{2,3},{3,2},{4,5},{5,4},{6,7},{7,6},{8,9},{9,8},{10,11... | collective-permute-start | bytes 49160 | tf_op jit(solution)/shard_map/ppermute | solution.py:60
  172.0 2.7 %collective-permute-start.8 = (bf16[4,128,16]{1,2,0:T(8,128)(2,1)S(1)}, bf16[4,128,16]{1,2,0:T(8,128)(2,1)S(1)}, u32[]{:S(2)}, u32[]{:S(2)}) collective-permute-start(bf16[4,128,16]{1,2,0:T(8,128)(2,1)S(1)} %add_convert_fusion.6), channel_id=1, source_target_pairs={{0,2},{1,3},{2,0},{3,1},{4,6},{5,7},{6,4},{7,5},{8,10},{9,11},{10,... | collective-permute-start | bytes 49160 | tf_op jit(solution)/shard_map/ppermute | solution.py:60
  174.7 4.2 %collective-permute-start.9 = (bf16[4,128,16]{1,2,0:T(8,128)(2,1)S(1)}, bf16[4,128,16]{1,2,0:T(8,128)(2,1)S(1)}, u32[]{:S(2)}, u32[]{:S(2)}) collective-permute-start(bf16[4,128,16]{1,2,0:T(8,128)(2,1)S(1)} %add_convert_fusion.5), channel_id=1, source_target_pairs={{0,4},{1,5},{2,6},{3,7},{4,0},{5,1},{6,2},{7,3},{8,12},{9,13},{10,... | collective-permute-start | bytes 49160 | tf_op jit(solution)/shard_map/ppermute | solution.py:60
Sparse Core Ops, SparseCore 0:
  12.7 103.5 all-gather.1
  168.2 49.2 reduce-scatter.1

commit v12 on v8

--- a/solution.py
+++ b/solution.py
@@ -139,38 +139,44 @@
         * inverse[0]
         * lax.dynamic_slice_in_dim(input_norm_gain, tensor_index * piece_width, piece_width, 0)
     ).astype(jnp.bfloat16)
-    adapter_parts = (
-        adapter_down_maps,
-        adapter_query_up,
-        adapter_key_value_up,
-        adapter_output_down,
-        adapter_output_up,
-    )
     local_adapters = adapter_down_maps.shape[0]
-    flat_parts = [part.reshape(local_adapters, -1) for part in adapter_parts]
-    joined = jnp.concatenate(flat_parts, axis=1)
-    lane_rows = joined.shape[1] // 128
-    every_adapter = lax.all_gather(
-        joined.reshape(local_adapters, lane_rows, 128), "req", axis=0, tiled=True
-    )
+
+    def gather_adapters(parts):
+        flat_parts = [part.reshape(local_adapters, -1) for part in parts]
+        joined = jnp.concatenate(flat_parts, axis=1)
+        every = lax.all_gather(
+            joined.reshape(local_adapters, joined.shape[1] // 128, 128), "req", axis=0, tiled=True
+        )
+        return every, flat_parts
+
+    def pick_adapters(parts, every, flat_parts):
+        picked = jnp.take(every, request_adapter, axis=0, mode="clip").reshape(
+            request_number, -1
+        )
+        picked_parts = []
+        start = 0
+        for part, flat in zip(parts, flat_parts):
+            width = flat.shape[1]
+            picked_parts.append(
+                picked[:, start : start + width].reshape((request_number,) + part.shape[1:])
+            )
+            start += width
+        return picked_parts
+
+    up_parts = (adapter_query_up, adapter_key_value_up, adapter_output_down, adapter_output_up)
+    every_down, down_flat = gather_adapters((adapter_down_maps,))
+    every_down, up_input = lax.optimization_barrier((every_down, up_parts))
+    every_up, up_flat = gather_adapters(up_input)
     slot_order = page_slot_table[0].reshape(holders, cached_count).T.reshape(-1)
     outgoing = cache_page_pool[slot_order].reshape(
         cached_count, holders, page_rows, cache_page_pool.shape[2]
     )
     arrived = lax.all_to_all(outgoing, "req", split_axis=1, concat_axis=1, tiled=True)
-    every_adapter, arrived = lax.optimization_barrier((every_adapter, arrived))
-    picked = jnp.take(every_adapter, request_adapter, axis=0, mode="clip").reshape(
-        request_number, -1
-    )
-    picked_parts = []
-    start = 0
-    for part, flat in zip(adapter_parts, flat_parts):
-        width = flat.shape[1]
-        picked_parts.append(
-            picked[:, start : start + width].reshape((request_number,) + part.shape[1:])
-        )
-        start += width
-    down_picked, query_picked, key_value_picked, output_down_picked, oup_sel = picked_parts
+    every_up, arrived = lax.optimization_barrier((every_up, arrived))
+    (down_picked,) = pick_adapters((adapter_down_maps,), every_down, down_flat)
+    query_picked, key_value_picked, output_down_picked, oup_sel = pick_adapters(
+        up_parts, every_up, up_flat
+    )
     adapter_rank_size = query_picked.shape[1]
     own_columns = own_normed.reshape(request_number, request_slot_rows, piece_width)
     partial_low = jnp.einsum(

time: 220 us -> 235 us (1.068)
  waiting for transfers between devices: 68.7 us -> 84.8 us
  matrix products: 36.1 us -> 31.5 us
  other arithmetic: 36.9 us -> 39.9 us
    all_gather x1 -> x2, waiting for transfers between devices: 2.55 us -> 21.6 us  [gather_adapters(): lax.all_gather(joined.reshape(local_adapters, joined.shape[1] // 128, 128...]
    unnamed x45 -> x71, local copies, waits for them, and re-layouts: 7.98 us -> 3.46 us
    dot_general x1, matrix products: 7.01 us -> 2.88 us  [local(): jnp.einsum('csf,cfn->sn', normed_parts, key_value_weight.reshape(chip_cou...]
    dot_general x1, matrix products: 10.1 us -> 7.38 us  [local(): jnp.einsum('csf,cfn->sn', normed_parts, query_weight.reshape(chip_count,...]
    another operation x0 -> x2, local copies, waits for them, and re-layouts: none -> 2.56 us  [the longest x1 2.2 us: gather_adapters(): joined.reshape(local_adapters, joined.shape[1] // 128, 128)]
    gather x1 -> x2, local copies, waits for them, and re-layouts: 4.49 us -> 6.03 us  [pick_adapters(): jnp.take(every, request_adapter, axis=0, mode='clip')]
  transfers between devices with their start and end apart: 13 -> 14, of which waited for: 11 -> 8; matrix products, arithmetic and copies ran while one was open for 33% -> 32% of each run, Pallas kernels for 0% -> 0%
where the time goes in v12:
time: 235 us; the launch traced here: 234 us
  waiting for transfers between devices  84.8 us (36%)
  other arithmetic  39.9 us (17%)
  local copies, waits for them, and re-layouts  37.5 us (16%)
  matrix products  31.5 us (13%)
  starting transfers between devices  26.2 us (11%)
  between operations  13.8 us (6%)
    reduce_scatter x1, waiting for transfers between devices, local(): lax.psum_scatter(head_terms.astype(jnp.bfloat16), 'tensor', scatter_dimen...  36.8 us
    all_gather x2, waiting for transfers between devices, gather_adapters(): lax.all_gather(joined.reshape(local_adapters, joined.shape[1] // 128, 128...  21.6 us
    ppermute x1, waiting for transfers between devices, local(): beside = lax.ppermute(pair, 'tensor', along)  20.5 us
    ppermute x6, starting transfers between devices, sum_over_tensor(): lax.ppermute(sent, 'tensor', pairs).astype(jnp.float32)  11.1 us
    dot_general x1, matrix products, local(): jnp.einsum('sc,ctf->tsf', attended, output_weight.reshape(output_weight.s...  9.12 us
    all_to_all x1, starting transfers between devices, local(): lax.all_to_all(outgoing, 'req', split_axis=1, concat_axis=1, tiled=True)  7.8 us
    dot_general x1, matrix products, local(): jnp.einsum('csf,cfn->sn', normed_parts, query_weight.reshape(chip_count,...  7.38 us
    gather x1, local copies, waits for them, and re-layouts, local(): gathered = jnp.take(relative, chip_order, axis=0)  7.08 us
  transfers between devices with their start and end apart: 14, of which 8 were waited for; matrix products, arithmetic and copies ran while one was open for 32% of the time, Pallas kernels for 0%

profile of v12, /device:TPU:1, one launch (start us, length us, event | category | flops | bytes accessed | tf_op | source)
XLA Modules:
  0.0 233.7 jit_solution(16895861276220197481)
XLA Ops:
  6.5 2.2 reshape_reshape.6
  8.8 1.5 collective-permute-start
  10.2 2.3 collective-permute-done
  12.5 3.5 %maximum_select_fusion.1 = bf16[512,1792]{1,0:T(8,128)(2,1)} fusion(bf16[512,896]{1,0:T(8,128)(2,1)S(1)} %collective-permute-done, bf16[512,896]{1,0:T(8,128)(2,1)} %param.16, pred[]{:T(512)S(6)} %eq.6), kind=kLoop, calls=%fused_computation.26 | loop fusion | flops 8257536 | bytes 3670017 | tf_op jit(solution)/shard_map/jit(_where)/select_n | solution.py:107
  16.0 2.6 %collective-permute-start.1 = (bf16[512,1792]{1,0:T(8,128)(2,1)}, bf16[512,1792]{1,0:T(8,128)(2,1)}, u32[]{:S(2)}, u32[]{:S(2)}) collective-permute-start(bf16[512,1792]{1,0:T(8,128)(2,1)} %maximum_select_fusion.1), channel_id=1, source_target_pairs={{6,0},{3,1},{0,2},{5,3},{2,4},{7,5},{4,6},{1,7},{14,8},{11,9},{8,1... | collective-permute-start | bytes 5505032 | tf_op jit(solution)/shard_map/ppermute | solution.py:112
  18.6 20.5 %collective-permute-done.1 = bf16[512,1792]{1,0:T(8,128)(2,1)} collective-permute-done((bf16[512,1792]{1,0:T(8,128)(2,1)}, bf16[512,1792]{1,0:T(8,128)(2,1)}, u32[]{:S(2)}, u32[]{:S(2)}) %collective-permute-start.1) | collective-permute-done | bytes 1835040 | tf_op jit(solution)/shard_map/ppermute | solution.py:112
  39.1 2.2 constant_dynamic-slice_fusion
  41.2 3.1 %collective-permute-start.2 = (bf16[512,896]{1,0:T(8,128)(2,1)}, bf16[512,896]{1,0:T(8,128)(2,1)}, u32[]{:S(2)}, u32[]{:S(2)}) collective-permute-start(bf16[512,896]{1,0:T(8,128)(2,1)} %constant_dynamic-slice_fusion), channel_id=1, source_target_pairs={{6,0},{3,1},{0,2},{5,3},{2,4},{7,5},{4,6},{1,7},{14,8},{11,9},{8,1... | collective-permute-start | bytes 2752520 | tf_op jit(solution)/shard_map/ppermute | solution.py:113
  44.4 0.5 broadcast.418
  44.9 0.6 reduce.11
  45.8 2.0 gather_fusion.2
  47.8 3.2 %copy.68 = bf16[2,16,128,256]{3,2,0,1:T(8,128)(2,1)} copy(bf16[2,16,128,256]{3,2,1,0:T(8,128)(2,1)} %bitcast.192) | data formatting | bytes 4194304 | tf_op jit(solution)/shard_map/reshape | solution.py:171
  51.0 7.8 %all-to-all-start = ((bf16[2,16,128,256]{3,2,0,1:T(8,128)(2,1)}), bf16[2,16,128,256]{3,2,0,1:T(8,128)(2,1)S(1)}, u32[]{:S(2)}, u32[]{:S(2)}) async-start(bf16[2,16,128,256]{3,2,0,1:T(8,128)(2,1)} %copy.68), calls=%async_computation | async-start | bytes 4194304 | tf_op jit(solution)/shard_map/all_to_all | solution.py:174
  58.9 6.0 %copy.72 = bf16[4,1792,256]{1,2,0:T(8,128)(2,1)} copy(bf16[4,1792,256]{2,1,0:T(8,128)(2,1)} %bitcast.200) | data formatting | bytes 7340032 | tf_op jit(solution)/shard_map/reshape | solution.py:201
  65.6 3.6 %pad_maximum_fusion.1 = bf16[512,2688]{1,0:T(8,128)(2,1)} fusion(bf16[512,896]{1,0:T(8,128)(2,1)} %collective-permute-done.2, bf16[512,1792]{1,0:T(8,128)(2,1)} %collective-permute-done.1), kind=kLoop, calls=%fused_computation.24 | loop fusion | flops 5505024 | bytes 5505024 | tf_op jit(solution)/shard_map/concatenate | solution.py:116
  69.5 20.3 %all-gather.3.cloned.1.call-done = bf16[64,336,128]{2,1,0:T(8,128)(2,1)} async-done(((bf16[4,336,128]{2,1,0:T(8,128)(2,1)}), bf16[64,336,128]{2,1,0:T(8,128)(2,1)}) %all-gather.3.cloned.1.call-update) | async-done | bytes 5505040 | tf_op jit(solution)/shard_map/all_gather | solution.py:147
  90.1 0.7 copy.144
  91.2 1.8 multiply_cosine_fusion.1
  93.0 0.7 fusion.64
  93.7 2.0 maximum_select_fusion
  95.7 1.3 slice_bitcast_fusion.4
  97.0 2.0 maximum_select_fusion.2
  99.0 2.3 select_bitcast_fusion.1
  101.3 3.6 %pad_maximum_fusion = bf16[4,512,1792]{2,1,0:T(8,128)(2,1)} fusion(bf16[1,512,1792]{2,1,0:T(8,128)(2,1)S(1)} %get-tuple-element.23, bf16[1,512,1792]{2,1,0:T(8,128)(2,1)S(1)} %maximum_select_fusion.2, bf16[1,512,1792]{2,1,0:T(8,128)(2,1)S(1)} %get-tuple-element.22, bf16[1,512,1792]{2,1,0:T(8,128)(2,1)S(1)} %maximum_select_fusion), kind=kLoop, calls=%fused_computation.15 | loop fusion | flops 11010048 | bytes 14680064 | tf_op jit(solution)/shard_map/stack | solution.py:126
  104.9 7.1 %gather_fusion = bf16[4,512,1792]{2,1,0:T(8,128)(2,1)} fusion(bf16[4,512,1792]{2,1,0:T(8,128)(2,1)} %pad_maximum_fusion, s32[1024]{0:T(1024)S(1)} %pad_clamp_fusion.2), kind=kCustom, calls=%fused_computation | custom fusion | bytes 14680080 | tf_op jit(solution)/shard_map/jit(_take)/gather | solution.py:128
  112.0 5.2 %fusion = f32[512]{0:T(512)S(1)} fusion(bf16[4,512,1792]{2,1,0:T(8,128)(2,1)} %gather_fusion, pred[4]{0:T(512)(128)(4,1)S(1)} %compare_and_fusion), kind=kLoop, calls=%fused_computation.6 | loop fusion | flops 14679552 | bytes 7342084 | tf_op jit(solution)/shard_map/reduce_sum | solution.py:131
  117.2 1.2 multiply_convert_fusion
  118.4 3.2 %gather_fusion.1 = bf16[4,336,128]{2,1,0:T(8,128)(2,1)S(1)} fusion(bf16[64,336,128]{2,1,0:T(8,128)(2,1)} %all-gather.3.cloned.1.call-done, s32[1024]{0:T(1024)S(1)} %pad_clamp_fusion.1), kind=kCustom, calls=%fused_computation.1 | custom fusion | bytes 688144 | tf_op jit(solution)/shard_map/jit(_take)/gather | solution.py:153
  121.6 0.4 reshape_reshape.7
  122.0 1.6 convolution_convert_fusion
  123.7 2.4 %collective-permute-start.4 = (bf16[4,128,48]{1,2,0:T(8,128)(2,1)S(1)}, bf16[4,128,48]{1,2,0:T(8,128)(2,1)S(1)}, u32[]{:S(2)}, u32[]{:S(2)}) collective-permute-start(bf16[4,128,48]{1,2,0:T(8,128)(2,1)S(1)} %convolution_convert_fusion), channel_id=1, source_target_pairs={{0,1},{1,0},{2,3},{3,2},{4,5},{5,4},{6,7},{7,6},{8,9},{9,8},{10,11... | collective-permute-start | bytes 147464 | tf_op jit(solution)/shard_map/ppermute | solution.py:60
  126.1 5.5 %fusion.2 = bf16[4,512,1792]{2,1,0:T(8,128)(2,1)S(1)} fusion(f32[4,1792]{1,0:T(4,128)S(1)} %mul.219, f32[512]{0:T(512)S(1)} %add_rsqrt_fusion, bf16[4,512,1792]{2,1,0:T(8,128)(2,1)} %gather_fusion, pred[4]{0:T(512)(128)(4,1)S(1)} %compare_and_fusion), kind=kLoop, calls=%fused_computation.8 | loop fusion | flops 18350080 | bytes 14710788 | tf_op jit(solution)/shard_map/convert.11
  131.6 1.3 collective-permute-start.5
  132.9 7.4 %convolution_bitcast_fusion = f32[4,128,512]{2,1,0:T(8,128)} fusion(bf16[4,128,4,1792]{3,1,0,2:T(8,128)(2,1)S(1)} %bitcast.194, bf16[4,1792,512,1]{2,1,3,0:T(8,128)(2,1)} %bitcast.225), kind=kOutput, calls=%fused_computation.42 | convolution fusion | flops 3758096384 | bytes 15728640 | tf_op jit(solution)/shard_map/csf,cfn->sn/dot_general | solution.py:186
  140.3 2.4 %collective-permute-start.6 = (bf16[4,128,48]{1,2,0:T(8,128)(2,1)S(1)}, bf16[4,128,48]{1,2,0:T(8,128)(2,1)S(1)}, u32[]{:S(2)}, u32[]{:S(2)}) collective-permute-start(bf16[4,128,48]{1,2,0:T(8,128)(2,1)S(1)} %add_convert_fusion.2), channel_id=1, source_target_pairs={{0,4},{1,5},{2,6},{3,7},{4,0},{5,1},{6,2},{7,3},{8,12},{9,13},{10,... | collective-permute-start | bytes 147464 | tf_op jit(solution)/shard_map/ppermute | solution.py:60
  142.8 2.9 %fusion.23 = f32[4,128,1,256]{3,1,0,2:T(8,128)} fusion(bf16[4,128,4,1792]{3,1,0,2:T(8,128)(2,1)S(1)} %bitcast.195, bf16[4,1792,256]{1,2,0:T(8,128)(2,1)S(1)} %copy-done.5), kind=kOutput, calls=%fused_computation.44 | convolution fusion | flops 1879048192 | bytes 11534336 | tf_op jit(solution)/shard_map/csf,cfn->sn/dot_general | solution.py:198
  145.7 1.3 all-gather.5.cloned.1.call-done
  147.0 2.9 %gather_fusion.3 = bf16[4,272,128]{2,1,0:T(8,128)(2,1)S(1)} fusion(bf16[64,272,128]{2,1,0:T(8,128)(2,1)} %all-gather.5.cloned.1.call-done, s32[1024]{0:T(1024)S(1)} %pad_clamp_fusion.1), kind=kCustom, calls=%fused_computation.3 | custom fusion | bytes 557072 | tf_op jit(solution)/shard_map/jit(_take)/gather | solution.py:153
  150.0 0.6 slice_bitcast_fusion.5
  150.7 2.5 %fusion.21 = f32[4,128,512]{2,1,0:T(8,128)} fusion(f32[4,128,512]{2,1,0:T(8,128)} %convolution_bitcast_fusion, bf16[1,4,16,512]{3,1,2,0:T(4,128)(2,1)S(1)} %bitcast.214, bf16[4,128,48]{1,2,0:T(8,128)(2,1)S(1)} %add_convert_fusion.1), kind=kOutput, calls=%fused_computation.41 | convolution fusion | flops 8912896 | bytes 2179072 | tf_op jit(solution)/shard_map/ibm,imf->ibf/dot_general | solution.py:192
  153.3 1.6 reshape.681
  154.9 0.6 fusion.85
  155.5 1.0 copy-done.3
  156.7 0.3 subtract_convert_fusion
  157.0 0.3 pad_maximum_fusion.2
  157.3 1.5 fusion.3
  158.8 2.2 fusion.9
  161.1 2.3 fusion.26
  163.4 0.2 fusion.29
  163.6 1.2 fusion.57
  164.9 0.5 fusion.87
  165.5 0.2 fusion.34
  165.9 1.5 fusion.22
  167.4 0.3 copy.82
  167.9 9.1 %convert_bitcast_fusion = bf16[8,512,896]{2,1,0:T(8,128)(2,1)} fusion(bf16[512,512,1]{1,0,2:T(8,128)(2,1)S(1)} %reshape.740, bf16[64,8,8,896]{3,2,1,0:T(8,128)(2,1)} %bitcast.226), kind=kOutput, calls=%fused_computation.16 | convolution fusion | flops 3761766400 | bytes 15204352 | tf_op jit(solution)/shard_map/sc,ctf->tsf/dot_general | solution.py:263
  177.3 0.9 collective-permute-start.7
  178.2 0.8 collective-permute-done.7
  179.0 1.3 collective-permute-start.8
  180.3 1.4 collective-permute-done.8
  181.7 2.8 %collective-permute-start.9 = (bf16[4,128,16]{1,2,0:T(8,128)(2,1)S(1)}, bf16[4,128,16]{1,2,0:T(8,128)(2,1)S(1)}, u32[]{:S(2)}, u32[]{:S(2)}) collective-permute-start(bf16[4,128,16]{1,2,0:T(8,128)(2,1)S(1)} %add_convert_fusion.5), channel_id=1, source_target_pairs={{0,4},{1,5},{2,6},{3,7},{4,0},{5,1},{6,2},{7,3},{8,12},{9,13},{10,... | collective-permute-start | bytes 49160 | tf_op jit(solution)/shard_map/ppermute | solution.py:60
  184.5 1.4 collective-permute-done.9
  185.9 1.8 convolution_multiply_fusion
  187.6 36.8 %reduce-scatter.2.cloned.1.call-done = bf16[1,512,896]{2,1,0:T(8,128)(2,1)} async-done(((bf16[8,512,896]{2,1,0:T(8,128)(2,1)}), bf16[1,512,896]{2,1,0:T(8,128)(2,1)}) %reduce-scatter.2.cloned.1.call-update) | async-done | bytes 917520 | tf_op jit(solution)/shard_map/reduce_scatter | solution.py:276
  224.4 2.8 %fusion.16 = bf16[512,896]{1,0:T(8,128)(2,1)} fusion(f32[4,128,896]{2,1,0:T(8,128)} %convolution_multiply_fusion, bf16[1,512,896]{2,1,0:T(8,128)(2,1)} %reduce-scatter.2.cloned.1.call-done), kind=kLoop, calls=%fused_computation.29 | loop fusion | flops 1376256 | bytes 3670016 | tf_op jit(solution)/shard_map/convert_element_type | solution.py:282
  (120 shorter events, 3.0 us)
Async XLA Ops:
  6.5 39.3 %copy-start = (bf16[32,128,256]{2,1,0:T(8,128)(2,1)S(1)}, bf16[32,128,256]{2,1,0:T(8,128)(2,1)}, u32[]{:S(2)}) copy-start(bf16[32,128,256]{2,1,0:T(8,128)(2,1)} %param.31) | copy-start | bytes 6291460
  6.5 38.3 %copy-start.26 = (s32[1,32]{1,0:T(1,128)S(1)}, s32[1,32]{1,0:T(1,128)}, u32[]{:S(2)}) copy-start(s32[1,32]{1,0:T(1,128)} %param.30) | copy-start | bytes 388
  6.5 83.2 %all-gather.3.cloned.1.call-start = ((), (), s32[]{:S(2)}) async-start(), calls=%async_computation.2 | async-start | bytes 5849088 | tf_op jit(solution)/shard_map/all_gather | solution.py:147
  8.8 3.8 %collective-permute-start = (bf16[512,896]{1,0:T(8,128)(2,1)}, bf16[512,896]{1,0:T(8,128)(2,1)S(1)}, u32[]{:S(2)}, u32[]{:S(2)}) collective-permute-start(bf16[512,896]{1,0:T(8,128)(2,1)} %param.16), channel_id=1, source_target_pairs={{0,1},{1,0},{2,3},{3,2},{4,5},{5,4},{6,7},{7,6},{8,9},{9,8},{10,11... | collective-permute-start | bytes 2752520 | tf_op jit(solution)/shard_map/ppermute | solution.py:106
  12.5 35.3 %copy-start.6 = (bf16[512,896]{1,0:T(8,128)(2,1)}, bf16[512,896]{1,0:T(8,128)(2,1)S(1)}, u32[]{:S(2)}) copy-start(bf16[512,896]{1,0:T(8,128)(2,1)S(1)} %collective-permute-done) | copy-start | bytes 2752516
  16.0 23.1 %collective-permute-start.1 = (bf16[512,1792]{1,0:T(8,128)(2,1)}, bf16[512,1792]{1,0:T(8,128)(2,1)}, u32[]{:S(2)}, u32[]{:S(2)}) collective-permute-start(bf16[512,1792]{1,0:T(8,128)(2,1)} %maximum_select_fusion.1), channel_id=1, source_target_pairs={{6,0},{3,1},{0,2},{5,3},{2,4},{7,5},{4,6},{1,7},{14,8},{11,9},{8,1... | collective-permute-start | bytes 5505032 | tf_op jit(solution)/shard_map/ppermute | solution.py:112
  41.2 24.3 %collective-permute-start.2 = (bf16[512,896]{1,0:T(8,128)(2,1)}, bf16[512,896]{1,0:T(8,128)(2,1)}, u32[]{:S(2)}, u32[]{:S(2)}) collective-permute-start(bf16[512,896]{1,0:T(8,128)(2,1)} %constant_dynamic-slice_fusion), channel_id=1, source_target_pairs={{6,0},{3,1},{0,2},{5,3},{2,4},{7,5},{4,6},{1,7},{14,8},{11,9},{8,1... | collective-permute-start | bytes 2752520 | tf_op jit(solution)/shard_map/ppermute | solution.py:113
  47.8 11.1 %copy-start.17 = (f32[7168]{0:T(1024)S(1)}, f32[7168]{0:T(1024)}, u32[]{:S(2)}) copy-start(f32[7168]{0:T(1024)} %param.17) | copy-start | bytes 86020
  51.0 94.7 %all-to-all-start = ((bf16[2,16,128,256]{3,2,0,1:T(8,128)(2,1)}), bf16[2,16,128,256]{3,2,0,1:T(8,128)(2,1)S(1)}, u32[]{:S(2)}, u32[]{:S(2)}) async-start(bf16[2,16,128,256]{3,2,0,1:T(8,128)(2,1)} %copy.68), calls=%async_computation | async-start | bytes 4194304 | tf_op jit(solution)/shard_map/all_to_all | solution.py:174
  58.8 88.2 %all-gather.5.cloned.1.call-start = ((), (), s32[]{:S(2)}) async-start(), calls=%async_computation.3 | async-start | bytes 4734976 | tf_op jit(solution)/shard_map/all_gather | solution.py:147
  58.9 6.1 %copy-start.27 = (s32[32]{0:T(128)S(1)}, s32[32]{0:T(128)}, u32[]{:S(2)}) copy-start(s32[32]{0:T(128)} %param.28) | copy-start | bytes 388
  58.9 6.5 %copy-start.28 = (s32[32]{0:T(128)S(1)}, s32[32]{0:T(128)}, u32[]{:S(2)}) copy-start(s32[32]{0:T(128)} %param.29) | copy-start | bytes 388
  64.9 4.3 %copy-start.25 = (s32[4]{0:T(128)S(1)}, s32[4]{0:T(128)}, u32[]{:S(2)}) copy-start(s32[4]{0:T(128)} %param.26) | copy-start | bytes 52
  64.9 24.9 %copy-start.14 = (bf16[4,16,896]{2,1,0:T(8,128)(2,1)S(1)}, bf16[4,16,896]{2,1,0:T(8,128)(2,1)}, u32[]{:S(2)}) copy-start(bf16[4,16,896]{2,1,0:T(8,128)(2,1)} %param.25) | copy-start | bytes 344068
  64.9 24.9 %copy-start.15 = (bf16[4,16,512]{2,1,0:T(8,128)(2,1)S(1)}, bf16[4,16,512]{2,1,0:T(8,128)(2,1)}, u32[]{:S(2)}) copy-start(bf16[4,16,512]{2,1,0:T(8,128)(2,1)} %param.22) | copy-start | bytes 196612
  64.9 25.0 %copy-start.16 = (bf16[4,16,512]{2,1,0:T(8,128)(2,1)S(1)}, bf16[4,16,512]{2,1,0:T(8,128)(2,1)}, u32[]{:S(2)}) copy-start(bf16[4,16,512]{2,1,0:T(8,128)(2,1)} %param.24) | copy-start | bytes 196612
  64.9 25.0 %copy-start.18 = (bf16[4,2,16,128]{3,2,1,0:T(8,128)(2,1)S(1)}, bf16[4,2,16,128]{3,2,1,0:T(8,128)(2,1)}, u32[]{:S(2)}) copy-start(bf16[4,2,16,128]{3,2,1,0:T(8,128)(2,1)} %param.23) | copy-start | bytes 98308
  65.6 25.4 %copy-start.29 = (s32[4]{0:T(128)S(1)}, s32[4]{0:T(128)}, u32[]{:S(2)}) copy-start(s32[4]{0:T(128)} %param.27) | copy-start | bytes 52
  65.6 28.1 %copy-start.4 = (bf16[512,896]{1,0:T(8,128)(2,1)S(1)}, bf16[512,896]{1,0:T(8,128)(2,1)}, u32[]{:S(2)}) copy-start(bf16[512,896]{1,0:T(8,128)(2,1)} %param.16) | copy-start | bytes 2752516
  69.2 26.5 %collective-permute-start.3 = (bf16[512,2688]{1,0:T(8,128)(2,1)}, bf16[512,2688]{1,0:T(8,128)(2,1)}, u32[]{:S(2)}, u32[]{:S(2)}) collective-permute-start(bf16[512,2688]{1,0:T(8,128)(2,1)} %pad_maximum_fusion.1), channel_id=1, source_target_pairs={{0,1},{1,0},{2,3},{3,2},{4,5},{5,4},{6,7},{7,6},{8,9},{9,8},{10,11... | collective-permute-start | bytes 8257544 | tf_op jit(solution)/shard_map/ppermute | solution.py:117
  69.2 27.8 %copy-start.21 = (f32[64]{0:T(128)}, f32[64]{0:T(128)S(1)}, u32[]{:S(2)}) copy-start(f32[64]{0:T(128)S(1)} %multiply_power_fusion) | copy-start | bytes 772
  69.4 27.6 %copy-start.19 = (f32[4,128]{1,0:T(4,128)}, f32[4,128]{1,0:T(4,128)S(1)}, u32[]{:S(2)}) copy-start(f32[4,128]{1,0:T(4,128)S(1)} %add_convert_fusion.8) | copy-start | bytes 6148
  90.9 133.5 %reduce-scatter.2.cloned.1.call-start = ((), (), s32[]{:S(2)}) async-start(), calls=%async_computation.4 | async-start | bytes 8257536 | tf_op jit(solution)/shard_map/reduce_scatter | solution.py:276
  91.0 7.9 %copy-start.23 = (pred[4,128]{1,0:T(4,128)(4,1)}, pred[4,128]{1,0:T(4,128)(4,1)S(1)}, u32[]{:S(2)}) copy-start(pred[4,128]{1,0:T(4,128)(4,1)S(1)} %iota_compare_fusion.1) | copy-start | bytes 1540
  123.7 8.0 %collective-permute-start.4 = (bf16[4,128,48]{1,2,0:T(8,128)(2,1)S(1)}, bf16[4,128,48]{1,2,0:T(8,128)(2,1)S(1)}, u32[]{:S(2)}, u32[]{:S(2)}) collective-permute-start(bf16[4,128,48]{1,2,0:T(8,128)(2,1)S(1)} %convolution_convert_fusion), channel_id=1, source_target_pairs={{0,1},{1,0},{2,3},{3,2},{4,5},{5,4},{6,7},{7,6},{8,9},{9,8},{10,11... | collective-permute-start | bytes 147464 | tf_op jit(solution)/shard_map/ppermute | solution.py:60
  131.6 8.7 %collective-permute-start.5 = (bf16[4,128,48]{1,2,0:T(8,128)(2,1)S(1)}, bf16[4,128,48]{1,2,0:T(8,128)(2,1)S(1)}, u32[]{:S(2)}, u32[]{:S(2)}) collective-permute-start(bf16[4,128,48]{1,2,0:T(8,128)(2,1)S(1)} %add_convert_fusion.3), channel_id=1, source_target_pairs={{0,2},{1,3},{2,0},{3,1},{4,6},{5,7},{6,4},{7,5},{8,10},{9,11},{10,... | collective-permute-start | bytes 147464 | tf_op jit(solution)/shard_map/ppermute | solution.py:60
  132.9 9.9 %copy-start.5 = (bf16[4,1792,256]{1,2,0:T(8,128)(2,1)S(1)}, bf16[4,1792,256]{1,2,0:T(8,128)(2,1)}, u32[]{:S(2)}) copy-start(bf16[4,1792,256]{1,2,0:T(8,128)(2,1)} %copy.72) | copy-start | bytes 11010052
  140.3 5.3 %collective-permute-start.6 = (bf16[4,128,48]{1,2,0:T(8,128)(2,1)S(1)}, bf16[4,128,48]{1,2,0:T(8,128)(2,1)S(1)}, u32[]{:S(2)}, u32[]{:S(2)}) collective-permute-start(bf16[4,128,48]{1,2,0:T(8,128)(2,1)S(1)} %add_convert_fusion.2), channel_id=1, source_target_pairs={{0,4},{1,5},{2,6},{3,7},{4,0},{5,1},{6,2},{7,3},{8,12},{9,13},{10,... | collective-permute-start | bytes 147464 | tf_op jit(solution)/shard_map/ppermute | solution.py:60
  145.7 5.0 %copy-start.9 = (bf16[4,128,48]{1,2,0:T(8,128)(2,1)}, bf16[4,128,48]{1,2,0:T(8,128)(2,1)S(1)}, u32[]{:S(2)}) copy-start(bf16[4,128,48]{1,2,0:T(8,128)(2,1)S(1)} %add_convert_fusion.1) | copy-start | bytes 147460
  145.7 5.0 %copy-start.2 = (bf16[2,16,128,256]{3,2,0,1:T(8,128)(2,1)}, bf16[2,16,128,256]{3,2,0,1:T(8,128)(2,1)S(1)}, u32[]{:S(2)}) copy-start(bf16[2,16,128,256]{3,2,0,1:T(8,128)(2,1)S(1)} %all-to-all-done) | copy-start | bytes 6291460
  154.8 1.6 copy-start.3
  154.8 1.8 copy-start.7
  154.9 1.8 copy-start.8
  156.6 0.7 copy-start.13
  161.0 2.3 copy-start.12
  161.0 2.3 copy-start.10
  161.0 2.3 copy-start.11
  161.0 2.6 %copy-start.20 = (f32[4,128]{1,0:T(4,128)S(1)}, f32[4,128]{1,0:T(4,128)}, u32[]{:S(2)}) copy-start(f32[4,128]{1,0:T(4,128)} %copy-done.19) | copy-start | bytes 6148
  161.1 2.6 %copy-start.22 = (f32[64]{0:T(128)S(1)}, f32[64]{0:T(128)}, u32[]{:S(2)}) copy-start(f32[64]{0:T(128)} %copy-done.21) | copy-start | bytes 772
  164.8 1.0 copy-start.24
  177.1 50.1 %copy-start.1 = (bf16[32,128,256]{2,1,0:T(8,128)(2,1)S(1)}, bf16[32,128,256]{2,1,0:T(8,128)(2,1)}, u32[]{:S(2)}) copy-start(bf16[32,128,256]{2,1,0:T(8,128)(2,1)} %param.31) | copy-start | bytes 6291460
  177.3 1.8 collective-permute-start.7
  179.0 2.7 %collective-permute-start.8 = (bf16[4,128,16]{1,2,0:T(8,128)(2,1)S(1)}, bf16[4,128,16]{1,2,0:T(8,128)(2,1)S(1)}, u32[]{:S(2)}, u32[]{:S(2)}) collective-permute-start(bf16[4,128,16]{1,2,0:T(8,128)(2,1)S(1)} %add_convert_fusion.6), channel_id=1, source_target_pairs={{0,2},{1,3},{2,0},{3,1},{4,6},{5,7},{6,4},{7,5},{8,10},{9,11},{10,... | collective-permute-start | bytes 49160 | tf_op jit(solution)/shard_map/ppermute | solution.py:60
  181.7 4.2 %collective-permute-start.9 = (bf16[4,128,16]{1,2,0:T(8,128)(2,1)S(1)}, bf16[4,128,16]{1,2,0:T(8,128)(2,1)S(1)}, u32[]{:S(2)}, u32[]{:S(2)}) collective-permute-start(bf16[4,128,16]{1,2,0:T(8,128)(2,1)S(1)} %add_convert_fusion.5), channel_id=1, source_target_pairs={{0,4},{1,5},{2,6},{3,7},{4,0},{5,1},{6,2},{7,3},{8,12},{9,13},{10,... | collective-permute-start | bytes 49160 | tf_op jit(solution)/shard_map/ppermute | solution.py:60
Sparse Core Ops, SparseCore 0:
  9.5 80.2 all-gather.2
  91.9 55.0 all-gather.4
  177.2 47.1 reduce-scatter.1
